TPU v7x, 32 devices: a whole 2x2x4 slice. The times are simulated.
32 devices in a mesh: batch: 8 (over z, x), phase: 2 (over core), mp: 2 (over y).
Axes of the slice: x: 2, y: 2, z: 4, core: 2. Of those that a mesh axis runs over, the one named last changes fastest.
Arguments:
- images: bfloat16 [64, 4, 4, 768], P('batch'), may hold values from -6 to 6
- conv_kernels: float32 [2, 7, 7, 768], P('phase'), may hold values from -0.875 to 0.875
- norm_gains: float32 [2, 768], P('phase'), may hold values from 0.1 to 1.9
- expand_weight: bfloat16 [2, 768, 3072], P('phase', None, 'mp'), may hold values from -0.21875 to 0.21875
- project_weight: bfloat16 [2, 3072, 768], P('phase', 'mp'), may hold values from -0.109375 to 0.109375
- head_weight: bfloat16 [768, 1024], replicated, may hold values from -0.21875 to 0.21875
- texts: bfloat16 [64, 1024], P('batch'), may hold values from -6 to 6
- pair_index: int32 [64], P('batch'), may hold values from 0 to 63
Outputs:
- input_grads: float32 [2, 64, 4, 4, 768], P('phase', 'batch')
Inputs may be any that keep to these rules, and one draw needn't show every extreme that they name: Image i and text pair_index[i] form a positive pair.
All inputs are finite; a program needn't handle non-finite values.
Results may differ from a plain program's by a relative error of at most 0.018.
Values may be sent and summed in bfloat16 or wider, within the bound.
No kernel may reach another device: no remote copies, remote signals or barrier semaphores. Data moves between devices by JAX's collectives and lax.ppermute only.
A program may use at most 64 MiB of HBM per device.

v0:
```python
import jax
import jax.numpy as jnp
import numpy as np
from jax import lax
from jax.sharding import PartitionSpec as P

inverse_softness_factor = 30.0


def swapped(value, axis, stride):
    return lax.ppermute(value, axis, [(i, i ^ 1 << stride) for i in range(lax.axis_size(axis))])


def depthwise(values, kernel):
    kernel_side = kernel.shape[0]
    margin = kernel_side // 2
    grid_side = values.shape[1]
    cells = np.arange(grid_side * grid_side)
    cell_row = cells // grid_side
    cell_col = cells % grid_side
    tap_row = np.clip(cell_row[None, :] - cell_row[:, None] + margin, 0, kernel_side - 1)
    tap_col = np.clip(cell_col[None, :] - cell_col[:, None] + margin, 0, kernel_side - 1)
    inside = (
        (np.abs(cell_row[None, :] - cell_row[:, None]) <= margin)
        & (np.abs(cell_col[None, :] - cell_col[:, None]) <= margin)
    ).astype(np.float32)
    operator = kernel[tap_row, tap_col] * jnp.asarray(inside, dtype=kernel.dtype)[:, :, None]
    flat = values.reshape(values.shape[0], grid_side * grid_side, values.shape[3])
    result = jnp.einsum("oic,bic->boc", operator, flat, precision=lax.Precision.HIGHEST)
    return result.reshape(values.shape)


def normalize_last(values):
    centred = values - jnp.mean(values, axis=-1, keepdims=True)
    variance = jnp.mean(centred * centred, axis=-1, keepdims=True)
    return centred * lax.rsqrt(variance + 1e-06)


def front_part(values, kernel, gain_vec):
    return normalize_last(depthwise(values, kernel)) * gain_vec


def mlp_part(normed, expand, project_out):
    flattened = normed.reshape(-1, normed.shape[-1]).astype(jnp.bfloat16)
    hidden = jax.nn.gelu(jnp.dot(flattened, expand, preferred_element_type=jnp.float32)).astype(
        jnp.bfloat16
    )
    return jnp.dot(hidden, project_out, preferred_element_type=jnp.float32).reshape(normed.shape)


def head_part(values, head_weight):
    pooled = jnp.mean(values, axis=(1, 2))
    normed = normalize_last(pooled).astype(jnp.bfloat16)
    embedded = jnp.dot(normed, head_weight, preferred_element_type=jnp.float32)
    return embedded * lax.rsqrt(jnp.sum(embedded * embedded, axis=-1, keepdims=True) + 1e-06)


def unit_text(texts):
    widened = texts.astype(jnp.float32)
    return (widened * lax.rsqrt(jnp.sum(widened * widened, axis=-1, keepdims=True) + 1e-06)).astype(
        jnp.bfloat16
    )


def hidden_total(values):
    return lax.psum(values.astype(jnp.bfloat16), "mp").astype(jnp.float32)


def hand_over(values):
    return swapped(values, "phase", 0)


def section_forward(inputs_low, kernel, gain_vec, expand, project_out):
    widened = inputs_low.astype(jnp.float32)
    normed, front_back = jax.vjp(lambda inner: front_part(inner, kernel, gain_vec), widened)
    partial_out, mlp_back = jax.vjp(lambda inner: mlp_part(inner, expand, project_out), normed)
    summed = hidden_total(partial_out)
    return ((widened + summed).astype(jnp.bfloat16), front_back, mlp_back)


def section_backward(cotangent, front_back, mlp_back):
    (partial_grad,) = mlp_back(cotangent)
    (from_front,) = front_back(hidden_total(partial_grad))
    return cotangent + from_front


def make_fold(vector_lowered_total, pair_index, row_map):

    def fold_texts(state_now, text_block, first_row):
        block_rows = text_block.shape[0]
        cosine_score_matrix = inverse_softness_factor * jnp.einsum(
            "ie,je->ij", vector_lowered_total, text_block, preferred_element_type=jnp.float32
        )
        weights = jnp.exp(cosine_score_matrix).astype(jnp.bfloat16)
        softmax_denominators = jnp.sum(weights.astype(jnp.float32), axis=1)
        softmax_scaled_captions = jnp.dot(weights, text_block, preferred_element_type=jnp.float32)
        global_rows = row_map(jnp.arange(block_rows, dtype=jnp.int32))
        onehot = (pair_index[:, None] == global_rows[None, :]).astype(jnp.bfloat16)
        diagonal_matched_scores = jnp.dot(onehot, text_block, preferred_element_type=jnp.float32)
        return (softmax_denominators, softmax_scaled_captions, diagonal_matched_scores)

    return fold_texts


def on_device(
    images, conv_kernels, norm_gains, expand_weight, project_weight, head_weight, texts, pair_index
):
    phase_pick = lax.axis_index("phase")
    kernel = conv_kernels[0]
    gain_vec = norm_gains[0]
    expand = expand_weight[0]
    project_out = project_weight[0]
    first_out, front_one, mlp_one = section_forward(images, kernel, gain_vec, expand, project_out)
    handed = hand_over(first_out)
    second_out, front_two, mlp_two = section_forward(handed, kernel, gain_vec, expand, project_out)
    embed, head_back = jax.vjp(
        lambda inner: head_part(inner, head_weight), second_out.astype(jnp.float32)
    )
    vector_lowered_total = embed.astype(jnp.bfloat16)
    caption_unit_vectors = unit_text(texts)
    image_rows = embed.shape[0]
    embed_width = embed.shape[1]
    text_rows = caption_unit_vectors.shape[0]
    share_count = 1
    share_rows = text_rows // share_count

    def share_map(rows_now):
        return rows_now // share_rows * text_rows + rows_now % share_rows

    start_state = (
        jnp.zeros((image_rows,), jnp.float32),
        jnp.zeros((image_rows, embed_width), jnp.float32),
        jnp.zeros((image_rows, embed_width), jnp.float32),
    )
    fold_texts = make_fold(vector_lowered_total, pair_index, share_map)
    softmax_denominators, softmax_scaled_captions, diagonal_matched_scores = fold_texts(
        start_state, lax.all_gather(caption_unit_vectors, "batch", axis=0, tiled=True), jnp.int32(0)
    )
    encoder_output_slope = inverse_softness_factor * (
        softmax_scaled_captions / softmax_denominators[:, None] - diagonal_matched_scores
    )
    (grad_second,) = head_back(encoder_output_slope)
    grad_first_in = section_backward(grad_second, front_two, mlp_two)
    returned = hand_over(grad_first_in.astype(jnp.bfloat16))
    grad_images = section_backward(returned.astype(jnp.float32), front_one, mlp_one)
    chosen = jnp.where(phase_pick == 0, grad_images, grad_first_in)
    return chosen[None]


def solution(mesh):
    return jax.shard_map(
        on_device,
        mesh=mesh,
        in_specs=(
            P("batch", None, None, None),
            P("phase", None, None, None),
            P("phase", None),
            P("phase", None, "mp"),
            P("phase", "mp", None),
            P(),
            P("batch", None),
            P("batch"),
        ),
        out_specs=P("phase", "batch", None, None, None),
        check_vma=False,
    )
```

profile of v0, /device:TPU:0, one launch (start us, length us, event | category | flops | bytes accessed | tf_op | source)
XLA Modules:
  0.0 215.0 jit_solution(14726889605407176546)
XLA Ops:
  6.5 1.1 copy.165
  7.6 1.0 reshape.232
  8.6 1.9 copy.122
  10.5 1.7 gather_fusion
  12.2 5.0 %copy.121 = f32[16,16,768]{1,0,2:T(8,128)} copy(f32[16,16,768]{2,1,0:T(8,128)S(1)} %bitcast.116) | data formatting | bytes 1572864 | tf_op jit(solution)/shard_map/jvp()/gather | solution.py:27
  17.2 9.9 %bitcast_reduce_fusion.1 = (f32[8,16]{1,0:T(8,128)S(1)}, f32[768,16,8]{1,2,0:T(8,128)}) fusion(f32[16,16,768]{1,0,2:T(8,128)} %copy.121, bf16[8,16,768]{1,0,2:T(8,128)(2,1)} %copy.122), kind=kOutput, calls=%fused_computation.161 | convolution fusion | flops 18972544 | bytes 1376768 | tf_op jit(solution)/shard_map/jvp(oic,bic->boc)/dot_general | solution.py:29
  27.1 2.3 %copy.123 = f32[768,16,8]{0,1,2:T(8,128)S(1)} copy(f32[768,16,8]{1,2,0:T(8,128)} %get-tuple-element.18) | data formatting | bytes 786432 | tf_op jit(solution)/shard_map/jvp(oic,bic->boc)/dot_general | solution.py:29
  29.4 0.2 multiply_reduce_fusion.3
  29.7 0.1 multiply_convert_fusion.3
  29.8 1.5 multiply_convert_fusion.1
  31.3 0.1 dot_general.57
  31.4 3.0 %fusion.16 = bf16[8,4,4,768]{3,0,2,1:T(8,128)(2,1)} fusion(bf16[1,1536,768]{2,1,0:T(8,128)(2,1)} %param.22, bf16[8,4,4,1536]{3,2,1,0:T(4,128)(2,1)S(1)} %dot_general.57), kind=kOutput, calls=%fused_computation.21 | convolution fusion | flops 302088192 | bytes 2949120 | tf_op jit(solution)/shard_map/jvp()/dot_general | solution.py:48
  34.4 0.2 all-reduce.7.cloned.1.call-start
  34.7 0.1 fusion.93
  34.8 25.0 %all-reduce.5.cloned.1.call-done = bf16[8,4,4,768]{3,0,2,1:T(8,128)(2,1)} async-done(((bf16[8,4,4,768]{3,0,2,1:T(8,128)(2,1)}), bf16[8,4,4,768]{3,0,2,1:T(8,128)(2,1)}) %all-reduce.5.cloned.1.call-update) | async-done | bytes 196624 | tf_op jit(solution)/shard_map/psum | solution.py:66
  59.8 1.0 add_convert_fusion.1
  60.9 1.4 collective-permute-done
  62.3 1.9 copy.127
  64.2 9.9 %bitcast_reduce_fusion = (f32[8,16]{1,0:T(8,128)S(1)}, f32[768,8,16]{2,1,0:T(8,128)}) fusion(bf16[8,16,768]{1,0,2:T(8,128)(2,1)} %copy.127, f32[16,16,768]{1,0,2:T(8,128)} %copy.121), kind=kOutput, calls=%fused_computation.160 | convolution fusion | flops 18972544 | bytes 1376768 | tf_op jit(solution)/shard_map/jvp(oic,bic->boc)/dot_general | solution.py:29
  74.0 2.3 %copy.129 = f32[768,8,16]{0,2,1:T(8,128)S(1)} copy(f32[768,8,16]{2,1,0:T(8,128)} %get-tuple-element.22) | data formatting | bytes 786432 | tf_op jit(solution)/shard_map/jvp(oic,bic->boc)/dot_general | solution.py:29
  76.4 0.2 multiply_reduce_fusion.2
  76.6 0.1 multiply_convert_fusion.2
  76.7 1.5 multiply_convert_fusion
  78.2 0.1 dot_general.61
  78.3 3.0 %fusion.19 = bf16[8,4,4,768]{3,0,2,1:T(8,128)(2,1)} fusion(bf16[1,1536,768]{2,1,0:T(8,128)(2,1)} %param.22, bf16[8,4,4,1536]{3,2,1,0:T(4,128)(2,1)S(1)} %dot_general.61), kind=kOutput, calls=%fused_computation.22 | convolution fusion | flops 302088192 | bytes 2949120 | tf_op jit(solution)/shard_map/jvp()/dot_general | solution.py:48
  81.3 0.1 fusion.94
  81.4 30.6 %all_gather.3 = bf16[64,1024]{1,0:T(8,128)(2,1)S(1)} all-gather(bf16[8,1024]{1,0:T(8,128)(2,1)S(1)} %fusion.94), channel_id=1, replica_groups=mesh['batch'=8,'phase'=2,'mp'=2] {'batch'}, dimensions={0}, use_global_device_ids=true | all-gather | bytes 147456 | tf_op jit(solution)/shard_map/all_gather | solution.py:137
  112.0 1.1 convert_reduce_fusion
  113.1 0.1 multiply_reduce_fusion.8
  113.2 0.2 multiply_reduce_fusion.7
  113.4 1.9 multiply_reduce_fusion.5
  115.3 0.3 convert_reduce_fusion.1
  115.7 0.1 convolution_divide_fusion
  115.8 0.3 multiply_reduce_fusion.4
  116.1 0.6 multiply_reduce_fusion.6
  116.8 0.2 fusion.125
  117.0 0.1 add_multiply_fusion
  117.2 3.6 %fusion.22 = bf16[128,768]{1,0:T(8,128)(2,1)S(1)} fusion(bf16[1,768,1536]{2,1,0:T(8,128)(2,1)S(1)} %copy-done, f32[128,1536]{1,0:T(8,128)} %get-tuple-element.24, bf16[128,768]{1,0:T(8,128)(2,1)S(1)} %reshape.234, bf16[1,1536,768]{2,1,0:T(8,128)(2,1)} %param.22), kind=kOutput, calls=%fused_computation.23 | convolution fusion | flops 608108544 | bytes 5898240 | tf_op jit(solution)/shard_map/transpose(jvp())/dot_general | solution.py:45
  120.8 0.7 copy.134
  121.6 0.3 all-reduce.11.cloned.1.call-start
  121.8 0.1 copy.137
  121.9 2.4 %copy.136 = f32[8,16,768]{2,0,1:T(8,128)S(1)} copy(f32[8,16,768]{1,0,2:T(8,128)} %bitcast.109) | data formatting | bytes 786432 | tf_op jit(solution)/shard_map/jvp(oic,bic->boc)/transpose | solution.py:29
  124.4 19.8 %all-reduce.9.cloned.1.call-done = bf16[8,4,4,768]{3,0,2,1:T(8,128)(2,1)} async-done(((bf16[8,4,4,768]{3,0,2,1:T(8,128)(2,1)}), bf16[8,4,4,768]{3,0,2,1:T(8,128)(2,1)}) %all-reduce.9.cloned.1.call-update) | async-done | bytes 196624 | tf_op jit(solution)/shard_map/psum | solution.py:66
  144.1 1.1 multiply_reduce_fusion.1
  145.3 1.2 fusion.91
  146.4 1.1 broadcast_add_fusion.1
  147.5 2.2 %copy.138 = f32[768,8,16]{2,1,0:T(8,128)} copy(f32[768,8,16]{0,1,2:T(8,128)S(1)} %bitcast.118) | data formatting | bytes 786432 | tf_op jit(solution)/shard_map/transpose(jvp(oic,bic->boc))/transpose | solution.py:29
  149.7 9.1 %convolution_bitcast_fusion.1 = f32[8,16,768]{1,0,2:T(8,128)} fusion(f32[768,8,16]{2,1,0:T(8,128)} %copy.138, f32[16,16,768]{1,0,2:T(8,128)} %copy.121), kind=kOutput, calls=%fused_computation.20 | convolution fusion | flops 18874368 | bytes 1572864 | tf_op jit(solution)/shard_map/transpose(jvp(oic,bic->boc))/dot_general | solution.py:29
  158.7 2.4 %copy.140 = f32[8,16,768]{2,0,1:T(8,128)S(1)} copy(f32[8,16,768]{1,0,2:T(8,128)} %convolution_bitcast_fusion.1) | data formatting | bytes 786432 | tf_op jit(solution)/shard_map/transpose(jvp(oic,bic->boc))/transpose | solution.py:29
  161.2 1.4 collective-permute-done.1
  162.7 0.7 copy-done.3
  163.3 0.1 copy.141
  163.5 3.5 %fusion.25 = bf16[128,768]{1,0:T(8,128)(2,1)S(1)} fusion(bf16[1,768,1536]{2,1,0:T(8,128)(2,1)S(1)} %copy-done, f32[128,1536]{1,0:T(8,128)} %get-tuple-element.20, bf16[128,768]{1,0:T(8,128)(2,1)S(1)} %reshape.238, bf16[1,1536,768]{2,1,0:T(8,128)(2,1)} %param.22), kind=kOutput, calls=%fused_computation.24 | convolution fusion | flops 608206848 | bytes 5898240 | tf_op jit(solution)/shard_map/transpose(jvp())/dot_general | solution.py:45
  167.1 0.7 copy.142
  167.8 0.1 copy.145
  167.9 2.4 %copy.144 = f32[8,16,768]{2,0,1:T(8,128)S(1)} copy(f32[8,16,768]{1,0,2:T(8,128)} %bitcast.108) | data formatting | bytes 786432 | tf_op jit(solution)/shard_map/jvp(oic,bic->boc)/transpose | solution.py:29
  170.4 20.0 %all-reduce.11.cloned.1.call-done = bf16[8,4,4,768]{3,0,2,1:T(8,128)(2,1)} async-done(((bf16[8,4,4,768]{3,0,2,1:T(8,128)(2,1)}), bf16[8,4,4,768]{3,0,2,1:T(8,128)(2,1)}) %all-reduce.11.cloned.1.call-update) | async-done | bytes 196624 | tf_op jit(solution)/shard_map/psum | solution.py:66
  190.4 1.1 multiply_reduce_fusion
  191.5 1.2 fusion.92
  192.7 1.1 broadcast_add_fusion
  193.8 2.3 %copy.146 = f32[768,8,16]{2,1,0:T(8,128)} copy(f32[768,8,16]{0,1,2:T(8,128)S(1)} %bitcast.117) | data formatting | bytes 786432 | tf_op jit(solution)/shard_map/transpose(jvp(oic,bic->boc))/transpose | solution.py:29
  196.1 9.1 %convolution_bitcast_fusion = f32[8,16,768]{1,0,2:T(8,128)} fusion(f32[768,8,16]{2,1,0:T(8,128)} %copy.146, f32[16,16,768]{1,0,2:T(8,128)} %copy.121), kind=kOutput, calls=%fused_computation.19 | convolution fusion | flops 18874368 | bytes 1572864 | tf_op jit(solution)/shard_map/transpose(jvp(oic,bic->boc))/dot_general | solution.py:29
  205.1 2.4 %copy.148 = f32[8,16,768]{2,0,1:T(8,128)S(1)} copy(f32[8,16,768]{1,0,2:T(8,128)} %convolution_bitcast_fusion) | data formatting | bytes 786432 | tf_op jit(solution)/shard_map/transpose(jvp(oic,bic->boc))/transpose | solution.py:29
  207.6 0.9 copy.149
  (56 shorter events, 0.9 us)
Async XLA Ops:
  6.5 23.3 %copy-start = (bf16[1,768,1536]{2,1,0:T(8,128)(2,1)S(1)}, bf16[1,768,1536]{2,1,0:T(8,128)(2,1)}, u32[]{:S(2)}) copy-start(bf16[1,768,1536]{2,1,0:T(8,128)(2,1)} %param.21) | copy-start | bytes 7077892
  6.5 3.9 %copy-start.1 = (s32[256]{0:T(256)S(1)}, s32[256]{0:T(256)}, u32[]{:S(2)}) copy-start(s32[256]{0:T(256)} %constant.120) | copy-start | bytes 3076
  6.5 53.2 %all-reduce.5.cloned.1.call-start = ((), (), s32[]{:S(2)}) async-start(), calls=%async_computation | async-start | bytes 393216 | tf_op jit(solution)/shard_map/psum | solution.py:66
  27.1 2.5 %copy-start.9 = (f32[1,768]{1,0:T(1,128)S(1)}, f32[1,768]{1,0:T(1,128)}, u32[]{:S(2)}) copy-start(f32[1,768]{1,0:T(1,128)} %param.20) | copy-start | bytes 9220
  31.4 3.3 %copy-start.8 = (bf16[8,1024]{1,0:T(8,128)(2,1)S(1)}, bf16[8,1024]{1,0:T(8,128)(2,1)}, u32[]{:S(2)}) copy-start(bf16[8,1024]{1,0:T(8,128)(2,1)} %param.24) | copy-start | bytes 49156
  31.4 28.4 %copy-start.5 = (bf16[8,4,4,768]{3,2,1,0:T(4,128)(2,1)S(1)}, bf16[8,4,4,768]{3,2,1,0:T(4,128)(2,1)}, u32[]{:S(2)}) copy-start(bf16[8,4,4,768]{3,2,1,0:T(4,128)(2,1)} %param.18) | copy-start | bytes 589828
  34.4 77.6 %all-reduce.7.cloned.1.call-start = ((), (), s32[]{:S(2)}) async-start(), calls=%async_computation.1 | async-start | bytes 393216 | tf_op jit(solution)/shard_map/psum | solution.py:66
  60.8 1.5 collective-permute-start
  81.3 34.5 %copy-start.10 = (s32[8]{0:T(128)S(1)}, s32[8]{0:T(128)}, u32[]{:S(2)}) copy-start(s32[8]{0:T(128)} %param.25) | copy-start | bytes 100
  81.3 62.8 %all-reduce.9.cloned.1.call-start = ((), (), s32[]{:S(2)}) async-start(), calls=%async_computation.2 | async-start | bytes 393216 | tf_op jit(solution)/shard_map/psum | solution.py:66
  112.0 4.1 %copy-start.2 = (bf16[768,1024]{1,0:T(8,128)(2,1)S(1)}, bf16[768,1024]{1,0:T(8,128)(2,1)}, u32[]{:S(2)}) copy-start(bf16[768,1024]{1,0:T(8,128)(2,1)} %param.23) | copy-start | bytes 4718596
  117.1 44.0 %copy-start.6 = (f32[8,768]{1,0:T(8,128)}, f32[8,768]{1,0:T(8,128)S(1)}, u32[]{:S(2)}) copy-start(f32[8,768]{1,0:T(8,128)S(1)} %add_multiply_fusion) | copy-start | bytes 73732
  121.6 68.8 %all-reduce.11.cloned.1.call-start = ((), (), s32[]{:S(2)}) async-start(), calls=%async_computation.3 | async-start | bytes 393216 | tf_op jit(solution)/shard_map/psum | solution.py:66
  161.1 1.5 collective-permute-start.1
  162.7 0.7 copy-start.3
  205.1 2.4 %copy-start.4 = (bf16[8,4,4,768]{3,0,2,1:T(8,128)(2,1)S(1)}, bf16[8,4,4,768]{3,0,2,1:T(8,128)(2,1)}, u32[]{:S(2)}) copy-start(bf16[8,4,4,768]{3,0,2,1:T(8,128)(2,1)} %copy-done.3) | copy-start | bytes 589828
  205.1 2.4 %copy-start.7 = (f32[8,768]{1,0:T(8,128)S(1)}, f32[8,768]{1,0:T(8,128)}, u32[]{:S(2)}) copy-start(f32[8,768]{1,0:T(8,128)} %copy-done.6) | copy-start | bytes 73732
Sparse Core Ops, SparseCore 0:
  34.5 25.1 all-reduce.4
  81.4 22.3 all-reduce.6
  121.7 22.3 all-reduce.8
  168.0 22.3 all-reduce.10
where the time goes:
time: 216 us; the launch traced here: 215 us
  waiting for transfers between devices  67.7 us (31%)
  matrix products  57.2 us (26%)
  local copies, waits for them, and re-layouts  34.9 us (16%)
  blocking collectives  30.6 us (14%)
  between operations  13.5 us (6%)
  other arithmetic  10.5 us (5%)
    psum x4, waiting for transfers between devices, hidden_total(): return lax.psum(values.astype(jnp.bfloat16), 'mp').astype(jnp.float32)  64.8 us
    dot_general x4, matrix products, depthwise(): jnp.einsum('oic,bic->boc', operator, flat, precision=lax.Precision.HIGHEST)  37.9 us
    all_gather x1, blocking collectives, on_device(): lax.all_gather(caption_unit_vectors, 'batch', axis=0, tiled=True)  30.6 us
    transpose x6, local copies, waits for them, and re-layouts, depthwise(): jnp.einsum('oic,bic->boc', operator, flat, precision=lax.Precision.HIGHEST)  13.9 us
    dot_general x4, matrix products, mlp_part(): jnp.dot(flattened, expand, preferred_element_type=jnp.float32)  10.1 us
    gather x2, local copies, waits for them, and re-layouts, depthwise(): kernel[tap_row, tap_col]  6.7 us
    dot_general x2, matrix products, mlp_part(): jnp.dot(hidden, project_out, preferred_element_type=jnp.float32)  5.97 us
    reshape x3, local copies, waits for them, and re-layouts, depthwise(): values.reshape(values.shape[0], grid_side * grid_side, values.shape[3])  4.71 us
  transfers between devices with their start and end apart: 6, of which 5 were waited for; matrix products, arithmetic and copies ran while one was open for 2% of the time, Pallas kernels for 0%

commit v1 on v0

--- a/solution.py
+++ b/solution.py
@@ -63,7 +63,25 @@
 
 
 def hidden_total(values):
-    return lax.psum(values.astype(jnp.bfloat16), "mp").astype(jnp.float32)
+    low = values.astype(jnp.bfloat16)
+    other = swapped(low, "mp", 0)
+    return (low.astype(jnp.float32) + other.astype(jnp.float32)).astype(jnp.bfloat16).astype(jnp.float32)
+
+
+def gather_rows(block, axis):
+    count = lax.axis_size(axis)
+    place = lax.axis_index(axis)
+    stride = 0
+    while (1 << stride) < count:
+        other = swapped(block, axis, stride)
+        upper = (place >> stride) & 1
+        block = jnp.where(
+            upper == 0,
+            jnp.concatenate([block, other], axis=0),
+            jnp.concatenate([other, block], axis=0),
+        )
+        stride += 1
+    return block
 
 
 def hand_over(values):
@@ -134,7 +152,7 @@
     )
     fold_texts = make_fold(vector_lowered_total, pair_index, share_map)
     softmax_denominators, softmax_scaled_captions, diagonal_matched_scores = fold_texts(
-        start_state, lax.all_gather(caption_unit_vectors, "batch", axis=0, tiled=True), jnp.int32(0)
+        start_state, gather_rows(caption_unit_vectors, "batch"), jnp.int32(0)
     )
     encoder_output_slope = inverse_softness_factor * (
         softmax_scaled_captions / softmax_denominators[:, None] - diagonal_matched_scores

time: 216 us -> 128 us (0.59)
  waiting for transfers between devices: 67.7 us -> 14.5 us
  blocking collectives: 30.6 us -> 0 us
  between operations: 13.5 us -> 0.38 us
  starting transfers between devices: 0.67 us -> 11 us
  other arithmetic: 10.5 us -> 6.9 us
    psum x4 -> x0, waiting for transfers between devices: 64.8 us -> none  [hidden_total(): return lax.psum(values.astype(jnp.bfloat16), 'mp').astype(jnp.float32)]
    all_gather x1 -> x0, blocking collectives: 30.6 us -> none  [on_device(): lax.all_gather(caption_unit_vectors, 'batch', axis=0, tiled=True)]
    ppermute x2 -> x9, waiting for transfers between devices: 2.84 us -> 14.5 us  [swapped(): lax.ppermute(value, axis, [(i, i ^ 1 << stride) for i in range(lax.axis_s...]
    ppermute x2 -> x9, starting transfers between devices: 0.14 us -> 11 us  [swapped(): lax.ppermute(value, axis, [(i, i ^ 1 << stride) for i in range(lax.axis_s...]
  transfers between devices with their start and end apart: 6 -> 9, of which waited for: 5 -> 6; matrix products, arithmetic and copies ran while one was open for 2% -> 22% of each run, Pallas kernels for 0% -> 0%
where the time goes in v1:
time: 128 us; the launch traced here: 127 us
  matrix products  57.4 us (45%)
  local copies, waits for them, and re-layouts  37 us (29%)
  waiting for transfers between devices  14.5 us (11%)
  starting transfers between devices  11 us (9%)
  other arithmetic  6.9 us (5%)
    dot_general x4, matrix products, depthwise(): jnp.einsum('oic,bic->boc', operator, flat, precision=lax.Precision.HIGHEST)  37.9 us
    transpose x6, local copies, waits for them, and re-layouts, depthwise(): jnp.einsum('oic,bic->boc', operator, flat, precision=lax.Precision.HIGHEST)  14.7 us
    ppermute x9, waiting for transfers between devices, swapped(): lax.ppermute(value, axis, [(i, i ^ 1 << stride) for i in range(lax.axis_s...  14.5 us
    ppermute x9, starting transfers between devices, swapped(): lax.ppermute(value, axis, [(i, i ^ 1 << stride) for i in range(lax.axis_s...  11 us
    dot_general x4, matrix products, mlp_part(): jnp.dot(flattened, expand, preferred_element_type=jnp.float32)  10 us
    gather x2, local copies, waits for them, and re-layouts, depthwise(): kernel[tap_row, tap_col]  6.7 us
    dot_general x2, matrix products, mlp_part(): jnp.dot(hidden, project_out, preferred_element_type=jnp.float32)  4.72 us
    reshape x3, local copies, waits for them, and re-layouts, depthwise(): values.reshape(values.shape[0], grid_side * grid_side, values.shape[3])  4.71 us
  transfers between devices with their start and end apart: 9, of which 6 were waited for; matrix products, arithmetic and copies ran while one was open for 22% of the time, Pallas kernels for 0%

profile of v1, /device:TPU:0, one launch (start us, length us, event | category | flops | bytes accessed | tf_op | source)
XLA Modules:
  0.0 127.2 jit_solution(16110129499023403957)
XLA Ops:
  0.0 1.1 copy.189
  1.1 1.0 reshape.232
  2.1 1.9 %copy.130 = bf16[8,16,768]{1,0,2:T(8,128)(2,1)} copy(bf16[8,16,768]{2,1,0:T(8,128)(2,1)S(1)} %reshape.232) | data formatting | bytes 393216 | tf_op jit(solution)/shard_map/jvp()/reshape | solution.py:28
  3.9 1.7 %gather_fusion = f32[256,768]{1,0:T(8,128)S(1)} fusion(f32[7,7,768]{2,1,0:T(8,128)S(1)} %bitcast.104, s32[256]{0:T(256)S(1)} %copy-done.1), kind=kCustom, calls=%fused_computation | custom fusion | bytes 1574912 | tf_op jit(solution)/shard_map/jvp()/gather | solution.py:27
  5.7 5.0 %copy.129 = f32[16,16,768]{1,0,2:T(8,128)} copy(f32[16,16,768]{2,1,0:T(8,128)S(1)} %bitcast.113) | data formatting | bytes 1572864 | tf_op jit(solution)/shard_map/jvp()/gather | solution.py:27
  10.6 9.9 %bitcast_reduce_fusion.1 = (f32[8,16]{1,0:T(8,128)S(1)}, f32[768,16,8]{1,2,0:T(8,128)}) fusion(f32[16,16,768]{1,0,2:T(8,128)} %copy.129, bf16[8,16,768]{1,0,2:T(8,128)(2,1)} %copy.130), kind=kOutput, calls=%fused_computation.169 | convolution fusion | flops 18972544 | bytes 1376768 | tf_op jit(solution)/shard_map/jvp(oic,bic->boc)/dot_general | solution.py:29
  20.6 2.3 %copy.131 = f32[768,16,8]{0,1,2:T(8,128)S(1)} copy(f32[768,16,8]{1,2,0:T(8,128)} %get-tuple-element.18) | data formatting | bytes 786432 | tf_op jit(solution)/shard_map/jvp(oic,bic->boc)/dot_general | solution.py:29
  22.9 0.2 multiply_reduce_fusion.3
  23.1 0.6 multiply_add_fusion.1
  23.7 0.1 multiply_convert_fusion.3
  23.8 1.5 %multiply_convert_fusion.1 = (bf16[128,1536]{1,0:T(8,128)(2,1)S(1)}, f32[128,1536]{1,0:T(8,128)}) fusion(bf16[128,768]{1,0:T(8,128)(2,1)S(1)} %bitcast.118, bf16[1,768,1536]{2,1,0:T(8,128)(2,1)S(1)} %copy-done), kind=kOutput, calls=%fused_computation.67 | convolution fusion | flops 303759360 | bytes 3735552 | tf_op jit(solution)/shard_map/jvp()/dot_general | solution.py:45
  25.4 2.3 %fusion.16 = bf16[8,4,4,768]{3,0,2,1:T(8,128)(2,1)S(1)} fusion(bf16[1,1536,768]{2,1,0:T(8,128)(2,1)} %param.22, bf16[8,4,4,1536]{3,2,1,0:T(4,128)(2,1)S(1)} %dot_general.57), kind=kOutput, calls=%fused_computation.21 | convolution fusion | flops 302088192 | bytes 2949120 | tf_op jit(solution)/shard_map/jvp()/dot_general | solution.py:48
  27.8 3.1 %collective-permute-start = (bf16[8,4,4,768]{3,0,2,1:T(8,128)(2,1)S(1)}, bf16[8,4,4,768]{3,0,2,1:T(8,128)(2,1)S(1)}, u32[]{:S(2)}, u32[]{:S(2)}) collective-permute-start(bf16[8,4,4,768]{3,0,2,1:T(8,128)(2,1)S(1)} %fusion.16), channel_id=1, source_target_pairs={{0,1},{1,0},{2,3},{3,2},{4,5},{5,4},{6,7},{7,6},{8,9},{9,8},{10,11... | collective-permute-start | bytes 589832 | tf_op jit(solution)/shard_map/ppermute | solution.py:11
  30.8 0.1 fusion.94
  31.0 1.5 %collective-permute-start.3 = (bf16[8,1024]{1,0:T(8,128)(2,1)S(1)}, bf16[8,1024]{1,0:T(8,128)(2,1)S(1)}, u32[]{:S(2)}, u32[]{:S(2)}) collective-permute-start(bf16[8,1024]{1,0:T(8,128)(2,1)S(1)} %fusion.95), channel_id=1, source_target_pairs={{0,4},{4,0},{8,12},{12,8},{16,20},{20,16},{24,28},{28,24},{1,5},{5... | collective-permute-start | bytes 49160 | tf_op jit(solution)/shard_map/ppermute | solution.py:11
  32.5 2.2 %collective-permute-done.3 = bf16[8,1024]{1,0:T(8,128)(2,1)S(1)} collective-permute-done((bf16[8,1024]{1,0:T(8,128)(2,1)S(1)}, bf16[8,1024]{1,0:T(8,128)(2,1)S(1)}, u32[]{:S(2)}, u32[]{:S(2)}) %collective-permute-start.3) | collective-permute-done | bytes 16416 | tf_op jit(solution)/shard_map/ppermute | solution.py:11
  34.8 1.6 %collective-permute-start.4 = (bf16[16,1024]{1,0:T(8,128)(2,1)S(1)}, bf16[16,1024]{1,0:T(8,128)(2,1)S(1)}, u32[]{:S(2)}, u32[]{:S(2)}) collective-permute-start(bf16[16,1024]{1,0:T(8,128)(2,1)S(1)} %maximum_select_fusion.2), channel_id=1, source_target_pairs={{0,8},{4,12},{8,0},{12,4},{16,24},{20,28},{24,16},{28,20},{1,9},{5... | collective-permute-start | bytes 98312 | tf_op jit(solution)/shard_map/ppermute | solution.py:11
  36.6 0.5 fusion.109
  37.1 1.7 %collective-permute-done.4 = bf16[16,1024]{1,0:T(8,128)(2,1)S(1)} collective-permute-done((bf16[16,1024]{1,0:T(8,128)(2,1)S(1)}, bf16[16,1024]{1,0:T(8,128)(2,1)S(1)}, u32[]{:S(2)}, u32[]{:S(2)}) %collective-permute-start.4) | collective-permute-done | bytes 32800 | tf_op jit(solution)/shard_map/ppermute | solution.py:11
  38.8 0.6 maximum_select_fusion.1
  39.4 2.6 %collective-permute-start.5 = (bf16[32,1024]{1,0:T(8,128)(2,1)}, bf16[32,1024]{1,0:T(8,128)(2,1)}, u32[]{:S(2)}, u32[]{:S(2)}) collective-permute-start(bf16[32,1024]{1,0:T(8,128)(2,1)} %maximum_select_fusion.1), channel_id=1, source_target_pairs={{0,16},{4,20},{8,24},{12,28},{16,0},{20,4},{24,8},{28,12},{1,17},{... | collective-permute-start | bytes 196616 | tf_op jit(solution)/shard_map/ppermute | solution.py:11
  42.0 1.9 %copy.135 = bf16[8,16,768]{1,0,2:T(8,128)(2,1)} copy(bf16[8,16,768]{2,0,1:T(8,128)(2,1)S(1)} %bitcast.117) | data formatting | bytes 393216 | tf_op jit(solution)/shard_map/jvp()/reshape | solution.py:28
  43.9 9.9 %bitcast_reduce_fusion = (f32[8,16]{1,0:T(8,128)S(1)}, f32[768,8,16]{2,1,0:T(8,128)}) fusion(bf16[8,16,768]{1,0,2:T(8,128)(2,1)} %copy.135, f32[16,16,768]{1,0,2:T(8,128)} %copy.129), kind=kOutput, calls=%fused_computation.168 | convolution fusion | flops 18972544 | bytes 1376768 | tf_op jit(solution)/shard_map/jvp(oic,bic->boc)/dot_general | solution.py:29
  53.8 2.3 %copy.137 = f32[768,8,16]{0,2,1:T(8,128)S(1)} copy(f32[768,8,16]{2,1,0:T(8,128)} %get-tuple-element.22) | data formatting | bytes 786432 | tf_op jit(solution)/shard_map/jvp(oic,bic->boc)/dot_general | solution.py:29
  56.1 0.2 multiply_reduce_fusion.2
  56.3 0.6 multiply_add_fusion
  57.0 1.5 %multiply_convert_fusion = (bf16[128,1536]{1,0:T(8,128)(2,1)S(1)}, f32[128,1536]{1,0:T(8,128)}) fusion(bf16[128,768]{1,0:T(8,128)(2,1)S(1)} %bitcast.119, bf16[1,768,1536]{2,1,0:T(8,128)(2,1)S(1)} %copy-done), kind=kOutput, calls=%fused_computation.66 | convolution fusion | flops 303759360 | bytes 3735552 | tf_op jit(solution)/shard_map/jvp()/dot_general | solution.py:45
  58.6 2.4 %fusion.19 = bf16[8,4,4,768]{3,0,2,1:T(8,128)(2,1)S(1)} fusion(bf16[1,1536,768]{2,1,0:T(8,128)(2,1)} %param.22, bf16[8,4,4,1536]{3,2,1,0:T(4,128)(2,1)S(1)} %dot_general.61), kind=kOutput, calls=%fused_computation.22 | convolution fusion | flops 302088192 | bytes 2949120 | tf_op jit(solution)/shard_map/jvp()/dot_general | solution.py:48
  61.1 0.6 collective-permute-start.2
  61.6 1.1 fusion.105
  62.8 4.0 %collective-permute-done.2 = bf16[8,4,4,768]{3,0,2,1:T(8,128)(2,1)S(1)} collective-permute-done((bf16[8,4,4,768]{3,0,2,1:T(8,128)(2,1)S(1)}, bf16[8,4,4,768]{3,0,2,1:T(8,128)(2,1)S(1)}, u32[]{:S(2)}, u32[]{:S(2)}) %collective-permute-start.2) | collective-permute-done | bytes 196640 | tf_op jit(solution)/shard_map/ppermute | solution.py:11
  67.0 0.2 multiply_reduce_fusion.7
  67.2 0.5 multiply_reduce_fusion.5
  67.7 1.3 convert_reduce_fusion.1
  68.9 1.2 multiply_reduce_fusion.4
  70.2 0.6 multiply_reduce_fusion.6
  70.8 0.2 fusion.127
  71.1 0.6 copy-done.6
  71.8 3.5 %fusion.22 = bf16[128,768]{1,0:T(8,128)(2,1)S(1)} fusion(bf16[1,768,1536]{2,1,0:T(8,128)(2,1)S(1)} %copy-done, f32[128,1536]{1,0:T(8,128)} %get-tuple-element.24, bf16[128,768]{1,0:T(8,128)(2,1)S(1)} %reshape.234, bf16[1,1536,768]{2,1,0:T(8,128)(2,1)} %param.22), kind=kOutput, calls=%fused_computation.23 | convolution fusion | flops 608108544 | bytes 5898240 | tf_op jit(solution)/shard_map/transpose(jvp())/dot_general | solution.py:45
  75.5 0.8 collective-permute-start.6
  76.4 2.4 %copy.145 = f32[8,16,768]{2,0,1:T(8,128)S(1)} copy(f32[8,16,768]{1,0,2:T(8,128)} %bitcast.106) | data formatting | bytes 786432 | tf_op jit(solution)/shard_map/jvp(oic,bic->boc)/transpose | solution.py:29
  78.8 2.4 %collective-permute-done.6 = bf16[8,4,4,768]{3,0,2,1:T(8,128)(2,1)S(1)} collective-permute-done((bf16[8,4,4,768]{3,0,2,1:T(8,128)(2,1)S(1)}, bf16[8,4,4,768]{3,0,2,1:T(8,128)(2,1)S(1)}, u32[]{:S(2)}, u32[]{:S(2)}) %collective-permute-start.6) | collective-permute-done | bytes 196640 | tf_op jit(solution)/shard_map/ppermute | solution.py:11
  81.3 0.2 multiply_reduce_fusion.1
  81.5 0.3 fusion.92
  81.8 0.2 broadcast_add_fusion.1
  82.0 2.2 %copy.147 = f32[768,8,16]{2,1,0:T(8,128)} copy(f32[768,8,16]{0,1,2:T(8,128)S(1)} %bitcast.115) | data formatting | bytes 786432 | tf_op jit(solution)/shard_map/transpose(jvp(oic,bic->boc))/transpose | solution.py:29
  84.1 9.1 %convolution_bitcast_fusion.1 = f32[8,16,768]{1,0,2:T(8,128)} fusion(f32[768,8,16]{2,1,0:T(8,128)} %copy.147, f32[16,16,768]{1,0,2:T(8,128)} %copy.129), kind=kOutput, calls=%fused_computation.20 | convolution fusion | flops 18874368 | bytes 1572864 | tf_op jit(solution)/shard_map/transpose(jvp(oic,bic->boc))/dot_general | solution.py:29
  93.2 2.4 %copy.149 = f32[8,16,768]{2,0,1:T(8,128)S(1)} copy(f32[8,16,768]{1,0,2:T(8,128)} %convolution_bitcast_fusion.1) | data formatting | bytes 786432 | tf_op jit(solution)/shard_map/transpose(jvp(oic,bic->boc))/transpose | solution.py:29
  95.7 1.4 %collective-permute-done.7 = bf16[8,4,4,768]{3,0,2,1:T(8,128)(2,1)S(1)} collective-permute-done((bf16[8,4,4,768]{3,0,2,1:T(8,128)(2,1)S(1)}, bf16[8,4,4,768]{3,0,2,1:T(8,128)(2,1)S(1)}, u32[]{:S(2)}, u32[]{:S(2)}) %collective-permute-start.7) | collective-permute-done | bytes 196640 | tf_op jit(solution)/shard_map/ppermute | solution.py:11
  97.1 0.7 copy-done.3
  97.9 3.5 %fusion.25 = bf16[128,768]{1,0:T(8,128)(2,1)S(1)} fusion(bf16[1,768,1536]{2,1,0:T(8,128)(2,1)S(1)} %copy-done, f32[128,1536]{1,0:T(8,128)} %get-tuple-element.20, bf16[128,768]{1,0:T(8,128)(2,1)S(1)} %reshape.238, bf16[1,1536,768]{2,1,0:T(8,128)(2,1)} %param.22), kind=kOutput, calls=%fused_computation.24 | convolution fusion | flops 608206848 | bytes 5898240 | tf_op jit(solution)/shard_map/transpose(jvp())/dot_general | solution.py:45
  101.6 0.7 copy.151
  102.3 0.7 collective-permute-start.8
  103.1 2.4 %copy.154 = f32[8,16,768]{2,0,1:T(8,128)S(1)} copy(f32[8,16,768]{1,0,2:T(8,128)} %bitcast.105) | data formatting | bytes 786432 | tf_op jit(solution)/shard_map/jvp(oic,bic->boc)/transpose | solution.py:29
  105.4 1.3 %copy.153 = f32[8,16]{0,1:T(8,128)} copy(f32[8,16]{1,0:T(8,128)} %get-tuple-element.11) | data formatting | bytes 1024 | tf_op jit(solution)/shard_map/jvp()/add | solution.py:36
  106.8 2.7 %collective-permute-done.8 = bf16[8,4,4,768]{3,0,2,1:T(8,128)(2,1)S(1)} collective-permute-done((bf16[8,4,4,768]{3,0,2,1:T(8,128)(2,1)}, bf16[8,4,4,768]{3,0,2,1:T(8,128)(2,1)S(1)}, u32[]{:S(2)}, u32[]{:S(2)}) %collective-permute-start.8) | collective-permute-done | bytes 196640 | tf_op jit(solution)/shard_map/ppermute | solution.py:11
  109.4 0.2 multiply_reduce_fusion
  109.7 0.7 fusion.128
  110.4 0.3 fusion.93
  110.7 0.9 broadcast_add_fusion
  111.6 3.1 %copy.156 = f32[768,8,16]{2,1,0:T(8,128)} copy(f32[768,8,16]{0,1,2:T(8,128)} %bitcast.114) | data formatting | bytes 786432 | tf_op jit(solution)/shard_map/transpose(jvp(oic,bic->boc))/transpose | solution.py:29
  114.7 9.1 %convolution_bitcast_fusion = f32[8,16,768]{1,0,2:T(8,128)} fusion(f32[768,8,16]{2,1,0:T(8,128)} %copy.156, f32[16,16,768]{1,0,2:T(8,128)} %copy.129), kind=kOutput, calls=%fused_computation.19 | convolution fusion | flops 18874368 | bytes 1572864 | tf_op jit(solution)/shard_map/transpose(jvp(oic,bic->boc))/dot_general | solution.py:29
  123.8 2.4 %copy.158 = f32[8,16,768]{2,0,1:T(8,128)S(1)} copy(f32[8,16,768]{1,0,2:T(8,128)} %convolution_bitcast_fusion) | data formatting | bytes 786432 | tf_op jit(solution)/shard_map/transpose(jvp(oic,bic->boc))/transpose | solution.py:29
  126.3 0.9 copy.159
  (69 shorter events, 1.8 us)
Async XLA Ops:
  0.0 23.8 %copy-start = (bf16[1,768,1536]{2,1,0:T(8,128)(2,1)S(1)}, bf16[1,768,1536]{2,1,0:T(8,128)(2,1)}, u32[]{:S(2)}) copy-start(bf16[1,768,1536]{2,1,0:T(8,128)(2,1)} %param.21) | copy-start | bytes 7077892
  0.0 3.9 %copy-start.1 = (s32[256]{0:T(256)S(1)}, s32[256]{0:T(256)}, u32[]{:S(2)}) copy-start(s32[256]{0:T(256)} %constant.129) | copy-start | bytes 3076
  20.6 3.1 %copy-start.13 = (f32[1,768]{1,0:T(1,128)S(1)}, f32[1,768]{1,0:T(1,128)}, u32[]{:S(2)}) copy-start(f32[1,768]{1,0:T(1,128)} %param.20) | copy-start | bytes 9220
  25.4 5.4 %copy-start.11 = (bf16[8,1024]{1,0:T(8,128)(2,1)S(1)}, bf16[8,1024]{1,0:T(8,128)(2,1)}, u32[]{:S(2)}) copy-start(bf16[8,1024]{1,0:T(8,128)(2,1)} %param.24) | copy-start | bytes 49156
  25.4 11.0 %copy-start.5 = (bf16[8,4,4,768]{3,2,1,0:T(4,128)(2,1)S(1)}, bf16[8,4,4,768]{3,2,1,0:T(4,128)(2,1)}, u32[]{:S(2)}) copy-start(bf16[8,4,4,768]{3,2,1,0:T(4,128)(2,1)} %param.18) | copy-start | bytes 589828
  27.8 8.7 %collective-permute-start = (bf16[8,4,4,768]{3,0,2,1:T(8,128)(2,1)S(1)}, bf16[8,4,4,768]{3,0,2,1:T(8,128)(2,1)S(1)}, u32[]{:S(2)}, u32[]{:S(2)}) collective-permute-start(bf16[8,4,4,768]{3,0,2,1:T(8,128)(2,1)S(1)} %fusion.16), channel_id=1, source_target_pairs={{0,1},{1,0},{2,3},{3,2},{4,5},{5,4},{6,7},{7,6},{8,9},{9,8},{10,11... | collective-permute-start | bytes 589832 | tf_op jit(solution)/shard_map/ppermute | solution.py:11
  31.0 3.7 %collective-permute-start.3 = (bf16[8,1024]{1,0:T(8,128)(2,1)S(1)}, bf16[8,1024]{1,0:T(8,128)(2,1)S(1)}, u32[]{:S(2)}, u32[]{:S(2)}) collective-permute-start(bf16[8,1024]{1,0:T(8,128)(2,1)S(1)} %fusion.95), channel_id=1, source_target_pairs={{0,4},{4,0},{8,12},{12,8},{16,20},{20,16},{24,28},{28,24},{1,5},{5... | collective-permute-start | bytes 49160 | tf_op jit(solution)/shard_map/ppermute | solution.py:11
  34.8 4.0 %collective-permute-start.4 = (bf16[16,1024]{1,0:T(8,128)(2,1)S(1)}, bf16[16,1024]{1,0:T(8,128)(2,1)S(1)}, u32[]{:S(2)}, u32[]{:S(2)}) collective-permute-start(bf16[16,1024]{1,0:T(8,128)(2,1)S(1)} %maximum_select_fusion.2), channel_id=1, source_target_pairs={{0,8},{4,12},{8,0},{12,4},{16,24},{20,28},{24,16},{28,20},{1,9},{5... | collective-permute-start | bytes 98312 | tf_op jit(solution)/shard_map/ppermute | solution.py:11
  36.5 5.5 %collective-permute-start.1 = (bf16[8,4,4,768]{3,0,2,1:T(8,128)(2,1)S(1)}, bf16[8,4,4,768]{3,0,2,1:T(8,128)(2,1)S(1)}, u32[]{:S(2)}, u32[]{:S(2)}) collective-permute-start(bf16[8,4,4,768]{3,0,2,1:T(8,128)(2,1)S(1)} %add_convert_fusion.4), channel_id=1, source_target_pairs={{0,2},{2,0},{1,3},{3,1},{4,6},{6,4},{5,7},{7,5},{8,10},{10,8},{9,1... | collective-permute-start | bytes 589832 | tf_op jit(solution)/shard_map/ppermute | solution.py:11
  39.4 22.2 %collective-permute-start.5 = (bf16[32,1024]{1,0:T(8,128)(2,1)}, bf16[32,1024]{1,0:T(8,128)(2,1)}, u32[]{:S(2)}, u32[]{:S(2)}) collective-permute-start(bf16[32,1024]{1,0:T(8,128)(2,1)} %maximum_select_fusion.1), channel_id=1, source_target_pairs={{0,16},{4,20},{8,24},{12,28},{16,0},{20,4},{24,8},{28,12},{1,17},{... | collective-permute-start | bytes 196616 | tf_op jit(solution)/shard_map/ppermute | solution.py:11
  53.8 4.7 %copy-start.9 = (f32[8,16]{1,0:T(8,128)}, f32[8,16]{1,0:T(8,128)S(1)}, u32[]{:S(2)}) copy-start(f32[8,16]{1,0:T(8,128)S(1)} %broadcast_multiply_fusion) | copy-start | bytes 1540
  58.6 3.0 %copy-start.14 = (s32[8]{0:T(128)S(1)}, s32[8]{0:T(128)}, u32[]{:S(2)}) copy-start(s32[8]{0:T(128)} %param.25) | copy-start | bytes 100
  58.6 3.0 %copy-start.15 = (s32[64]{0:T(128)S(1)}, s32[64]{0:T(128)}, u32[]{:S(2)}) copy-start(s32[64]{0:T(128)} %fusion.109) | copy-start | bytes 772
  58.6 8.6 %copy-start.2 = (bf16[768,1024]{1,0:T(8,128)(2,1)S(1)}, bf16[768,1024]{1,0:T(8,128)(2,1)}, u32[]{:S(2)}) copy-start(bf16[768,1024]{1,0:T(8,128)(2,1)} %param.23) | copy-start | bytes 4718596
  61.1 5.7 %collective-permute-start.2 = (bf16[8,4,4,768]{3,0,2,1:T(8,128)(2,1)S(1)}, bf16[8,4,4,768]{3,0,2,1:T(8,128)(2,1)S(1)}, u32[]{:S(2)}, u32[]{:S(2)}) collective-permute-start(bf16[8,4,4,768]{3,0,2,1:T(8,128)(2,1)S(1)} %fusion.19), channel_id=1, source_target_pairs={{0,1},{1,0},{2,3},{3,2},{4,5},{5,4},{6,7},{7,6},{8,9},{9,8},{10,11... | collective-permute-start | bytes 589832 | tf_op jit(solution)/shard_map/ppermute | solution.py:11
  71.1 0.6 copy-start.6
  71.8 4.5 %copy-start.10 = (f32[8,16]{1,0:T(8,128)S(1)}, f32[8,16]{1,0:T(8,128)}, u32[]{:S(2)}) copy-start(f32[8,16]{1,0:T(8,128)} %copy-done.9) | copy-start | bytes 1540
  75.4 3.4 %copy-start.12 = (f32[8,16]{1,0:T(8,128)S(1)}, f32[8,16]{1,0:T(8,128)}, u32[]{:S(2)}) copy-start(f32[8,16]{1,0:T(8,128)} %get-tuple-element.13) | copy-start | bytes 1540
  75.5 5.7 %collective-permute-start.6 = (bf16[8,4,4,768]{3,0,2,1:T(8,128)(2,1)S(1)}, bf16[8,4,4,768]{3,0,2,1:T(8,128)(2,1)S(1)}, u32[]{:S(2)}, u32[]{:S(2)}) collective-permute-start(bf16[8,4,4,768]{3,0,2,1:T(8,128)(2,1)S(1)} %copy.142), channel_id=1, source_target_pairs={{0,1},{1,0},{2,3},{3,2},{4,5},{5,4},{6,7},{7,6},{8,9},{9,8},{10,11... | collective-permute-start | bytes 589832 | tf_op jit(solution)/shard_map/ppermute | solution.py:11
  93.2 2.4 %copy-start.7 = (f32[8,768]{1,0:T(8,128)S(1)}, f32[8,768]{1,0:T(8,128)}, u32[]{:S(2)}) copy-start(f32[8,768]{1,0:T(8,128)} %copy-done.6) | copy-start | bytes 73732
  95.6 1.5 %collective-permute-start.7 = (bf16[8,4,4,768]{3,0,2,1:T(8,128)(2,1)S(1)}, bf16[8,4,4,768]{3,0,2,1:T(8,128)(2,1)S(1)}, u32[]{:S(2)}, u32[]{:S(2)}) collective-permute-start(bf16[8,4,4,768]{3,0,2,1:T(8,128)(2,1)S(1)} %add_convert_fusion.6), channel_id=1, source_target_pairs={{0,2},{2,0},{1,3},{3,1},{4,6},{6,4},{5,7},{7,5},{8,10},{10,8},{9,1... | collective-permute-start | bytes 589832 | tf_op jit(solution)/shard_map/ppermute | solution.py:11
  97.1 0.7 copy-start.3
  102.3 7.2 %collective-permute-start.8 = (bf16[8,4,4,768]{3,0,2,1:T(8,128)(2,1)}, bf16[8,4,4,768]{3,0,2,1:T(8,128)(2,1)S(1)}, u32[]{:S(2)}, u32[]{:S(2)}) collective-permute-start(bf16[8,4,4,768]{3,0,2,1:T(8,128)(2,1)} %copy.151), channel_id=1, source_target_pairs={{0,1},{1,0},{2,3},{3,2},{4,5},{5,4},{6,7},{7,6},{8,9},{9,8},{10,11... | collective-permute-start | bytes 589832 | tf_op jit(solution)/shard_map/ppermute | solution.py:11
  123.8 2.4 %copy-start.4 = (bf16[8,4,4,768]{3,0,2,1:T(8,128)(2,1)S(1)}, bf16[8,4,4,768]{3,0,2,1:T(8,128)(2,1)}, u32[]{:S(2)}) copy-start(bf16[8,4,4,768]{3,0,2,1:T(8,128)(2,1)} %copy-done.3) | copy-start | bytes 589828
  123.8 2.4 %copy-start.8 = (f32[8,768]{1,0:T(8,128)S(1)}, f32[8,768]{1,0:T(8,128)}, u32[]{:S(2)}) copy-start(f32[8,768]{1,0:T(8,128)} %copy-done.6) | copy-start | bytes 73732

commit v2 on v1

--- a/solution.py
+++ b/solution.py
@@ -11,23 +11,22 @@
     return lax.ppermute(value, axis, [(i, i ^ 1 << stride) for i in range(lax.axis_size(axis))])
 
 
-def depthwise(values, kernel):
-    kernel_side = kernel.shape[0]
-    margin = kernel_side // 2
-    grid_side = values.shape[1]
-    cells = np.arange(grid_side * grid_side)
-    cell_row = cells // grid_side
-    cell_col = cells % grid_side
-    tap_row = np.clip(cell_row[None, :] - cell_row[:, None] + margin, 0, kernel_side - 1)
-    tap_col = np.clip(cell_col[None, :] - cell_col[:, None] + margin, 0, kernel_side - 1)
-    inside = (
-        (np.abs(cell_row[None, :] - cell_row[:, None]) <= margin)
-        & (np.abs(cell_col[None, :] - cell_col[:, None]) <= margin)
-    ).astype(np.float32)
-    operator = kernel[tap_row, tap_col] * jnp.asarray(inside, dtype=kernel.dtype)[:, :, None]
-    flat = values.reshape(values.shape[0], grid_side * grid_side, values.shape[3])
-    result = jnp.einsum("oic,bic->boc", operator, flat, precision=lax.Precision.HIGHEST)
-    return result.reshape(values.shape)
+def depthwise(values, kernel, side):
+    margin = kernel.shape[0] // 2
+    cells = side * side
+    outs = []
+    for o in range(cells):
+        row_o, col_o = divmod(o, side)
+        acc = None
+        for i in range(cells):
+            row_i, col_i = divmod(i, side)
+            d_row, d_col = row_i - row_o, col_i - col_o
+            if abs(d_row) > margin or abs(d_col) > margin:
+                continue
+            term = kernel[d_row + margin, d_col + margin][None, :] * values[i]
+            acc = term if acc is None else acc + term
+        outs.append(acc)
+    return jnp.stack(outs)
 
 
 def normalize_last(values):
@@ -36,8 +35,8 @@
     return centred * lax.rsqrt(variance + 1e-06)
 
 
-def front_part(values, kernel, gain_vec):
-    return normalize_last(depthwise(values, kernel)) * gain_vec
+def front_part(values, kernel, gain_vec, side):
+    return normalize_last(depthwise(values, kernel, side)) * gain_vec
 
 
 def mlp_part(normed, expand, project_out):
@@ -49,7 +48,7 @@
 
 
 def head_part(values, head_weight):
-    pooled = jnp.mean(values, axis=(1, 2))
+    pooled = jnp.mean(values, axis=0)
     normed = normalize_last(pooled).astype(jnp.bfloat16)
     embedded = jnp.dot(normed, head_weight, preferred_element_type=jnp.float32)
     return embedded * lax.rsqrt(jnp.sum(embedded * embedded, axis=-1, keepdims=True) + 1e-06)
@@ -88,9 +87,9 @@
     return swapped(values, "phase", 0)
 
 
-def section_forward(inputs_low, kernel, gain_vec, expand, project_out):
+def section_forward(inputs_low, kernel, gain_vec, expand, project_out, side):
     widened = inputs_low.astype(jnp.float32)
-    normed, front_back = jax.vjp(lambda inner: front_part(inner, kernel, gain_vec), widened)
+    normed, front_back = jax.vjp(lambda inner: front_part(inner, kernel, gain_vec, side), widened)
     partial_out, mlp_back = jax.vjp(lambda inner: mlp_part(inner, expand, project_out), normed)
     summed = hidden_total(partial_out)
     return ((widened + summed).astype(jnp.bfloat16), front_back, mlp_back)
@@ -128,9 +127,12 @@
     gain_vec = norm_gains[0]
     expand = expand_weight[0]
     project_out = project_weight[0]
-    first_out, front_one, mlp_one = section_forward(images, kernel, gain_vec, expand, project_out)
+    count, side = images.shape[0], images.shape[1]
+    width = images.shape[3]
+    cell_major = images.reshape(count, side * side, width).transpose(1, 0, 2)
+    first_out, front_one, mlp_one = section_forward(cell_major, kernel, gain_vec, expand, project_out, side)
     handed = hand_over(first_out)
-    second_out, front_two, mlp_two = section_forward(handed, kernel, gain_vec, expand, project_out)
+    second_out, front_two, mlp_two = section_forward(handed, kernel, gain_vec, expand, project_out, side)
     embed, head_back = jax.vjp(
         lambda inner: head_part(inner, head_weight), second_out.astype(jnp.float32)
     )
@@ -162,7 +164,7 @@
     returned = hand_over(grad_first_in.astype(jnp.bfloat16))
     grad_images = section_backward(returned.astype(jnp.float32), front_one, mlp_one)
     chosen = jnp.where(phase_pick == 0, grad_images, grad_first_in)
-    return chosen[None]
+    return chosen.transpose(1, 0, 2).reshape(count, side, side, width)[None]
 
 
 def solution(mesh):

time: 128 us -> 77.9 us (0.61)
  matrix products: 57.4 us -> 14 us
  local copies, waits for them, and re-layouts: 37 us -> 8.33 us
  other arithmetic: 6.9 us -> 22.4 us
  waiting for transfers between devices: 14.5 us -> 21.1 us
    dot_general x4 -> x0, matrix products: 37.9 us -> none  [depthwise(): jnp.einsum('oic,bic->boc', operator, flat, precision=lax.Precision.HIGHEST)]
    transpose x6 -> x0, local copies, waits for them, and re-layouts: 14.7 us -> none  [depthwise(): jnp.einsum('oic,bic->boc', operator, flat, precision=lax.Precision.HIGHEST)]
    gather x2 -> x0, local copies, waits for them, and re-layouts: 6.7 us -> none  [depthwise(): kernel[tap_row, tap_col]]
    ppermute x9, waiting for transfers between devices: 14.5 us -> 21.1 us  [swapped(): lax.ppermute(value, axis, [(i, i ^ 1 << stride) for i in range(lax.axis_s...]
    dot_general x4 -> x0, local copies, waits for them, and re-layouts: 4.83 us -> none  [the longest x2 4.64 us: depthwise(): jnp.einsum('oic,bic->boc', operator, flat, precision=lax.Precision.HIGHEST)]
    reshape x5 -> x0, local copies, waits for them, and re-layouts: 4.81 us -> none  [the longest x3 4.71 us: depthwise(): values.reshape(values.shape[0], grid_side * grid_side, values.shape[3])]
    dot_general x2, matrix products: 4.72 us -> 1.16 us  [mlp_part(): jnp.dot(hidden, project_out, preferred_element_type=jnp.float32)]
    unnamed x33 -> x57, local copies, waits for them, and re-layouts: 2.45 us -> 5.96 us
  transfers between devices with their start and end apart: 9 -> 9, of which waited for: 6 -> 6; matrix products, arithmetic and copies ran while one was open for 22% -> 16% of each run, Pallas kernels for 0% -> 0%
where the time goes in v2:
time: 77.9 us; the launch traced here: 77 us
  other arithmetic  22.4 us (29%)
  waiting for transfers between devices  21.1 us (27%)
  matrix products  14 us (18%)
  starting transfers between devices  10.4 us (13%)
  local copies, waits for them, and re-layouts  8.33 us (11%)
    ppermute x9, waiting for transfers between devices, swapped(): lax.ppermute(value, axis, [(i, i ^ 1 << stride) for i in range(lax.axis_s...  21.1 us
    ppermute x9, starting transfers between devices, swapped(): lax.ppermute(value, axis, [(i, i ^ 1 << stride) for i in range(lax.axis_s...  10.4 us
    dot_general x4, matrix products, mlp_part(): jnp.dot(flattened, expand, preferred_element_type=jnp.float32)  8.17 us
    unnamed x57, local copies, waits for them, and re-layouts  5.96 us
    convert_element_type x1, other arithmetic, on_device(): returned = hand_over(grad_first_in.astype(jnp.bfloat16))  3.3 us
    unnamed x31, other arithmetic  3.03 us
    select_n x2, other arithmetic, gather_rows(): jnp.where(upper == 0, jnp.concatenate([block, other], axis=0), jnp.concat...  2.89 us
    reduce_sum x6, other arithmetic, normalize_last(): centred = values - jnp.mean(values, axis=-1, keepdims=True)  2.31 us
  transfers between devices with their start and end apart: 9, of which 6 were waited for; matrix products, arithmetic and copies ran while one was open for 16% of the time, Pallas kernels for 0%

profile of v2, /device:TPU:0, one launch (start us, length us, event | category | flops | bytes accessed | tf_op | source)
XLA Modules:
  0.0 77.0 jit_solution(11207934685766033127)
XLA Ops:
  0.0 1.1 %copy.13 = f32[1,7,7,768]{3,2,0,1:T(8,128)S(1)} copy(f32[1,7,7,768]{3,0,2,1:T(1,128)} %param.9) | data formatting | bytes 301056
  1.2 0.2 slice_reduce_fusion.20
  1.4 0.2 slice_reduce_fusion
  1.6 1.0 %copy.9 = f32[8,4,4,768]{3,0,2,1:T(8,128)S(1)} copy(bf16[8,4,4,768]{3,2,1,0:T(4,128)(2,1)} %param.8) | data formatting | bytes 589824 | tf_op jit(solution)/shard_map/convert_element_type | solution.py:91
  3.5 0.1 reduce_sum.148
  3.6 0.2 multiply_reduce_fusion.3
  3.8 0.6 copy-done.20
  4.5 0.5 fusion.14
  5.0 0.9 %copy-done.3 = f32[128,1536]{1,0:T(8,128)} copy-done((f32[128,1536]{1,0:T(8,128)}, f32[128,1536]{1,0:T(8,128)S(1)}, u32[]{:S(2)}) %copy-start.3) | copy-done | bytes 786456
  5.9 0.5 copy-done.24
  6.4 0.6 fusion.16
  7.0 3.1 %collective-permute-start = (bf16[16,8,768]{2,1,0:T(8,128)(2,1)S(1)}, bf16[16,8,768]{2,1,0:T(8,128)(2,1)}, u32[]{:S(2)}, u32[]{:S(2)}) collective-permute-start(bf16[16,8,768]{2,1,0:T(8,128)(2,1)S(1)} %fusion.16), channel_id=1, source_target_pairs={{0,1},{1,0},{2,3},{3,2},{4,5},{5,4},{6,7},{7,6},{8,9},{9,8},{10,11... | collective-permute-start | bytes 589832 | tf_op jit(solution)/shard_map/ppermute | solution.py:11
  10.1 0.1 fusion.122
  10.2 0.7 fusion.123
  10.9 1.5 %collective-permute-start.3 = (bf16[8,1024]{1,0:T(8,128)(2,1)}, bf16[8,1024]{1,0:T(8,128)(2,1)}, u32[]{:S(2)}, u32[]{:S(2)}) collective-permute-start(bf16[8,1024]{1,0:T(8,128)(2,1)} %fusion.123), channel_id=1, source_target_pairs={{0,4},{4,0},{8,12},{12,8},{16,20},{20,16},{24,28},{28,24},{1,5},{5... | collective-permute-start | bytes 49160 | tf_op jit(solution)/shard_map/ppermute | solution.py:11
  12.4 2.6 %collective-permute-done.3 = bf16[8,1024]{1,0:T(8,128)(2,1)} collective-permute-done((bf16[8,1024]{1,0:T(8,128)(2,1)}, bf16[8,1024]{1,0:T(8,128)(2,1)}, u32[]{:S(2)}, u32[]{:S(2)}) %collective-permute-start.3) | collective-permute-done | bytes 16416 | tf_op jit(solution)/shard_map/ppermute | solution.py:11
  14.9 1.4 %maximum_select_fusion.2 = bf16[16,1024]{1,0:T(8,128)(2,1)} fusion(bf16[8,1024]{1,0:T(8,128)(2,1)} %collective-permute-done.3, bf16[8,1024]{1,0:T(8,128)(2,1)} %fusion.123, pred[]{:T(512)S(6)} %eq.30), kind=kLoop, calls=%fused_computation.168 | loop fusion | flops 147456 | bytes 65537 | tf_op jit(solution)/shard_map/jit(_where)/select_n | solution.py:77
  16.4 1.6 %collective-permute-start.4 = (bf16[16,1024]{1,0:T(8,128)(2,1)}, bf16[16,1024]{1,0:T(8,128)(2,1)}, u32[]{:S(2)}, u32[]{:S(2)}) collective-permute-start(bf16[16,1024]{1,0:T(8,128)(2,1)} %maximum_select_fusion.2), channel_id=1, source_target_pairs={{0,8},{4,12},{8,0},{12,4},{16,24},{20,28},{24,16},{28,20},{1,9},{5... | collective-permute-start | bytes 98312 | tf_op jit(solution)/shard_map/ppermute | solution.py:11
  17.9 1.7 %add_convert_fusion.4 = bf16[16,8,768]{2,1,0:T(8,128)(2,1)} fusion(bf16[16,8,768]{2,1,0:T(8,128)(2,1)} %collective-permute-done, bf16[16,8,768]{2,1,0:T(8,128)(2,1)S(1)} %fusion.16, f32[8,4,4,768]{3,0,2,1:T(8,128)S(1)} %copy.9), kind=kLoop, calls=%fused_computation.95 | loop fusion | flops 688128 | bytes 983040 | tf_op jit(solution)/shard_map/convert_element_type | solution.py:95
  19.6 0.5 fusion.139
  20.1 0.5 collective-permute-done.4
  20.6 1.5 %maximum_select_fusion.1 = bf16[32,1024]{1,0:T(8,128)(2,1)} fusion(bf16[16,1024]{1,0:T(8,128)(2,1)} %collective-permute-done.4, bf16[16,1024]{1,0:T(8,128)(2,1)} %maximum_select_fusion.2, pred[]{:T(512)S(6)} %eq.29), kind=kLoop, calls=%fused_computation.161 | loop fusion | flops 294912 | bytes 131073 | tf_op jit(solution)/shard_map/jit(_where)/select_n | solution.py:77
  22.1 2.6 %collective-permute-start.5 = (bf16[32,1024]{1,0:T(8,128)(2,1)}, bf16[32,1024]{1,0:T(8,128)(2,1)}, u32[]{:S(2)}, u32[]{:S(2)}) collective-permute-start(bf16[32,1024]{1,0:T(8,128)(2,1)} %maximum_select_fusion.1), channel_id=1, source_target_pairs={{0,16},{4,20},{8,24},{12,28},{16,0},{20,4},{24,8},{28,12},{1,17},{... | collective-permute-start | bytes 196616 | tf_op jit(solution)/shard_map/ppermute | solution.py:11
  24.7 0.7 constant_dynamic-update-slice_fusion.31
  25.6 0.7 constant_dynamic-update-slice_fusion.28
  27.1 0.7 reduce_sum.153
  27.8 0.8 %broadcast_multiply_fusion.512 = f32[16,8]{1,0:T(8,128)S(1)} fusion(f32[16,8]{1,0:T(8,128)} %reduce_sum.153), kind=kLoop, calls=%fused_computation.708 | loop fusion | flops 128 | bytes 1024 | tf_op jit(solution)/shard_map/jvp()/div | solution.py:33
  28.6 0.2 multiply_reduce_fusion.2
  28.8 0.6 copy-done.21
  29.4 0.6 copy-done.5
  30.0 0.5 fusion.12
  30.6 0.6 fusion.19
  31.2 0.6 collective-permute-start.2
  31.8 1.1 %fusion.135 = f32[8,1024]{1,0:T(8,128)S(1)} fusion(s32[64]{0:T(128)S(1)} %copy-done.27, s32[8]{0:T(128)S(1)} %copy-done.26, bf16[32,1024]{1,0:T(8,128)(2,1)} %collective-permute-done.5, bf16[32,1024]{1,0:T(8,128)(2,1)} %maximum_select_fusion.1, pred[]{:T(512)S(6)} %eq.28), kind=kOutput, calls=%fused_computation.710 | convolution fusion | flops 1638912 | bytes 164129 | tf_op jit(solution)/shard_map/dot_general | solution.py:116
  32.9 4.9 %collective-permute-done.2 = bf16[16,8,768]{2,1,0:T(8,128)(2,1)S(1)} collective-permute-done((bf16[16,8,768]{2,1,0:T(8,128)(2,1)S(1)}, bf16[16,8,768]{2,1,0:T(8,128)(2,1)S(1)}, u32[]{:S(2)}, u32[]{:S(2)}) %collective-permute-start.2) | collective-permute-done | bytes 196640 | tf_op jit(solution)/shard_map/ppermute | solution.py:11
  37.9 0.1 multiply_reduce_fusion.8
  38.0 0.2 multiply_reduce_fusion.7
  38.2 0.5 multiply_reduce_fusion.5
  38.7 1.3 %convert_reduce_fusion.1 = (f32[8]{0:T(128)S(1)}, bf16[8,64]{1,0:T(8,128)(2,1)S(1)}) fusion(bf16[32,1024]{1,0:T(8,128)(2,1)} %collective-permute-done.5, bf16[32,1024]{1,0:T(8,128)(2,1)} %maximum_select_fusion.1, pred[]{:T(512)S(6)} %eq.28, f32[8,1024]{1,0:T(8,128)S(1)} %get-tuple-element.842, f32[8]{0:T(128)S(1)} %add_rsqrt_fusion.1), kind=kOutput, calls=%fused_computation.707 | convolution fusion | flops 1656824 | bytes 164929 | tf_op jit(solution)/shard_map/ie,je->ij/dot_general | solution.py:108
  40.0 1.2 %multiply_reduce_fusion.4 = (f32[8]{0:T(128)S(1)}, f32[8,1024]{1,0:T(8,128)S(1)}) fusion(f32[8,1024]{1,0:T(8,128)S(1)} %get-tuple-element.842, f32[8,1024]{1,0:T(8,128)S(1)} %fusion.135, f32[8]{0:T(128)S(1)} %get-tuple-element.843, bf16[8,64]{1,0:T(8,128)(2,1)S(1)} %get-tuple-element.844, bf16[32,1024]{1,0:T(8,128)(2,1)} %collective-permute-done.5, ...), kind=kOutput, calls=%fused_computation.170 | convolution fusion | flops 1679352 | bytes 230465 | tf_op jit(solution)/shard_map/dot_general | solution.py:113
  41.2 0.6 multiply_reduce_fusion.6
  41.9 0.2 fusion.164
  42.1 0.7 add_multiply_fusion
  42.8 3.6 %fusion.31 = bf16[16,8,768]{2,1,0:T(8,128)(2,1)S(1)} fusion(bf16[1,768,1536]{2,1,0:T(8,128)(2,1)S(1)} %copy-done, f32[128,1536]{1,0:T(8,128)} %copy-done.4, bf16[1,1536,768]{2,1,0:T(8,128)(2,1)} %param.12, f32[8,768]{1,0:T(8,128)} %add_multiply_fusion), kind=kOutput, calls=%fused_computation.23 | convolution fusion | flops 608108544 | bytes 5726208 | tf_op jit(solution)/shard_map/transpose(jvp())/dot_general | solution.py:44
  46.3 0.6 collective-permute-start.6
  46.9 5.2 %collective-permute-done.6 = bf16[16,8,768]{2,1,0:T(8,128)(2,1)S(1)} collective-permute-done((bf16[16,8,768]{2,1,0:T(8,128)(2,1)S(1)}, bf16[16,8,768]{2,1,0:T(8,128)(2,1)S(1)}, u32[]{:S(2)}, u32[]{:S(2)}) %collective-permute-start.6) | collective-permute-done | bytes 196640 | tf_op jit(solution)/shard_map/ppermute | solution.py:11
  52.1 0.2 multiply_reduce_fusion.1
  52.3 0.7 multiply_multiply_fusion.5
  53.0 1.0 %fusion.120 = f32[16,8]{1,0:T(8,128)S(1)} fusion(f32[16,8]{1,0:T(8,128)S(1)} %multiply_multiply_fusion.5, f32[16,8,768]{2,1,0:T(8,128)S(1)} %constant_dynamic-update-slice_fusion.16, f32[16,8]{1,0:T(8,128)S(1)} %broadcast_multiply_fusion.512, f32[16,8]{1,0:T(8,128)} %copy-done.5, f32[768]{0:T(1024)S(1)} %reduce.49, ...), kind=kLoop, calls=%fused_computation.126 | loop fusion | flops 1179520 | bytes 791552 | tf_op jit(solution)/shard_map/transpose(jvp())/reduce_sum | solution.py:33
  54.0 0.9 %broadcast_add_fusion.1 = f32[16,8,768]{2,1,0:T(8,128)S(1)} fusion(f32[16,8]{1,0:T(8,128)S(1)} %negate_multiply_fusion.1, f32[16,8]{1,0:T(8,128)S(1)} %multiply_multiply_fusion.5, f32[16,8,768]{2,1,0:T(8,128)S(1)} %constant_dynamic-update-slice_fusion.16, f32[16,8]{1,0:T(8,128)S(1)} %broadcast_multiply_fusion.512, f32[16,8]{1,0:T(8,128)} %copy-done.5, ...), kind=kLoop, calls=%fused_computation.117 | loop fusion | flops 1179648 | bytes 1184768 | tf_op jit(solution)/shard_map/transpose(jvp())/add_any | solution.py:33
  55.3 0.4 copy-done.8
  56.0 0.4 copy-done.19
  56.5 3.3 %fusion.163 = (bf16[16,8,768]{2,1,0:T(8,128)(2,1)S(1)}, f32[16,8,768]{2,1,0:T(8,128)}) fusion(f32[1,8,768]{2,1,0:T(8,128)S(1)} %get-tuple-element.337, f32[1,8,768]{2,1,0:T(8,128)S(1)} %get-tuple-element.562, f32[1,8,768]{2,1,0:T(8,128)S(1)} %get-tuple-element.576, f32[1,8,768]{2,1,0:T(8,128)S(1)} %get-tuple-element.584, ...), kind=kLoop, calls=%fused_computation.800 | loop fusion | flops 25264128 | bytes 7274496 | tf_op jit(solution)/shard_map/convert_element_type | solution.py:164
  59.8 1.4 %collective-permute-done.7 = bf16[16,8,768]{2,1,0:T(8,128)(2,1)S(1)} collective-permute-done((bf16[16,8,768]{2,1,0:T(8,128)(2,1)S(1)}, bf16[16,8,768]{2,1,0:T(8,128)(2,1)S(1)}, u32[]{:S(2)}, u32[]{:S(2)}) %collective-permute-start.7) | collective-permute-done | bytes 196640 | tf_op jit(solution)/shard_map/ppermute | solution.py:11
  61.2 3.6 %fusion.28 = bf16[16,8,768]{2,1,0:T(8,128)(2,1)S(1)} fusion(bf16[1,768,1536]{2,1,0:T(8,128)(2,1)S(1)} %copy-done, f32[128,1536]{1,0:T(8,128)} %copy-done.3, bf16[1,1536,768]{2,1,0:T(8,128)(2,1)} %param.12, bf16[16,8,768]{2,1,0:T(8,128)(2,1)S(1)} %collective-permute-done.7), kind=kOutput, calls=%fused_computation.22 | convolution fusion | flops 608206848 | bytes 5898240 | tf_op jit(solution)/shard_map/transpose(jvp())/dot_general | solution.py:44
  64.8 0.6 collective-permute-start.8
  65.3 6.4 %collective-permute-done.8 = bf16[16,8,768]{2,1,0:T(8,128)(2,1)S(1)} collective-permute-done((bf16[16,8,768]{2,1,0:T(8,128)(2,1)S(1)}, bf16[16,8,768]{2,1,0:T(8,128)(2,1)S(1)}, u32[]{:S(2)}, u32[]{:S(2)}) %collective-permute-start.8) | collective-permute-done | bytes 196640 | tf_op jit(solution)/shard_map/ppermute | solution.py:11
  71.8 0.2 multiply_reduce_fusion
  72.0 0.7 multiply_multiply_fusion.4
  72.7 0.2 fusion.121
  73.0 0.2 broadcast_add_fusion
  73.9 0.7 copy-done.2
  74.6 1.5 %add_select_fusion = f32[16,8,768]{2,1,0:T(8,128)S(1)} fusion(f32[16,8,768]{2,1,0:T(8,128)S(1)} %copy-done.2, f32[1,8,768]{2,1,0:T(8,128)S(1)} %get-tuple-element.79, f32[1,8,768]{2,1,0:T(8,128)S(1)} %get-tuple-element.657, f32[1,8,768]{2,1,0:T(8,128)S(1)} %get-tuple-element.671, f32[1,8,768]{2,1,0:T(8,128)S(1)} %get-tuple-element.679, ...), kind=kLoop, calls=%fused_computation.76 | loop fusion | flops 25362432 | bytes 7643137 | tf_op jit(solution)/shard_map/jit(_where)/select_n | solution.py:166
  76.1 0.9 %copy.10 = f32[1,8,4,4,768]{4,3,2,1,0:T(4,128)} copy(f32[1,8,4,4,768]{4,1,3,2,0:T(8,128)S(1)} %bitcast.92) | data formatting | bytes 786432 | tf_op jit(solution)/shard_map/broadcast_in_dim;reshape | solution.py:167
  (135 shorter events, 3.4 us)
Async XLA Ops:
  0.0 4.5 %copy-start = (bf16[1,768,1536]{2,1,0:T(8,128)(2,1)S(1)}, bf16[1,768,1536]{2,1,0:T(8,128)(2,1)}, u32[]{:S(2)}) copy-start(bf16[1,768,1536]{2,1,0:T(8,128)(2,1)} %param.11) | copy-start | bytes 7077892
  1.4 1.7 %copy-start.9 = (f32[768]{0:T(1024)}, f32[768]{0:T(1024)S(1)}, u32[]{:S(2)}) copy-start(f32[768]{0:T(1024)S(1)} %get-tuple-element.26) | copy-start | bytes 9220
  1.4 1.7 %copy-start.12 = (f32[768]{0:T(1024)}, f32[768]{0:T(1024)S(1)}, u32[]{:S(2)}) copy-start(f32[768]{0:T(1024)S(1)} %get-tuple-element.38) | copy-start | bytes 9220
  1.5 1.7 %copy-start.6 = (f32[768]{0:T(1024)}, f32[768]{0:T(1024)S(1)}, u32[]{:S(2)}) copy-start(f32[768]{0:T(1024)S(1)} %get-tuple-element.8) | copy-start | bytes 9220
  1.6 1.9 %copy-start.15 = (f32[768]{0:T(1024)}, f32[768]{0:T(1024)S(1)}, u32[]{:S(2)}) copy-start(f32[768]{0:T(1024)S(1)} %get-tuple-element.5) | copy-start | bytes 9220
  3.0 1.4 %copy-start.23 = (f32[1,768]{1,0:T(1,128)S(1)}, f32[1,768]{1,0:T(1,128)}, u32[]{:S(2)}) copy-start(f32[1,768]{1,0:T(1,128)} %param.10) | copy-start | bytes 9220
  3.8 0.6 copy-start.20
  4.5 2.0 %copy-start.24 = (bf16[1,1536,768]{2,1,0:T(8,128)(2,1)S(1)}, bf16[1,1536,768]{2,1,0:T(8,128)(2,1)}, u32[]{:S(2)}) copy-start(bf16[1,1536,768]{2,1,0:T(8,128)(2,1)} %param.12) | copy-start | bytes 7077892
  5.0 0.9 %copy-start.3 = (f32[128,1536]{1,0:T(8,128)}, f32[128,1536]{1,0:T(8,128)S(1)}, u32[]{:S(2)}) copy-start(f32[128,1536]{1,0:T(8,128)S(1)} %fusion.14) | copy-start | bytes 2359300
  6.4 3.7 %copy-start.22 = (bf16[8,1024]{1,0:T(8,128)(2,1)S(1)}, bf16[8,1024]{1,0:T(8,128)(2,1)}, u32[]{:S(2)}) copy-start(bf16[8,1024]{1,0:T(8,128)(2,1)} %param.14) | copy-start | bytes 49156
  7.0 10.9 %collective-permute-start = (bf16[16,8,768]{2,1,0:T(8,128)(2,1)S(1)}, bf16[16,8,768]{2,1,0:T(8,128)(2,1)}, u32[]{:S(2)}, u32[]{:S(2)}) collective-permute-start(bf16[16,8,768]{2,1,0:T(8,128)(2,1)S(1)} %fusion.16), channel_id=1, source_target_pairs={{0,1},{1,0},{2,3},{3,2},{4,5},{5,4},{6,7},{7,6},{8,9},{9,8},{10,11... | collective-permute-start | bytes 589832 | tf_op jit(solution)/shard_map/ppermute | solution.py:11
  10.9 4.1 %collective-permute-start.3 = (bf16[8,1024]{1,0:T(8,128)(2,1)}, bf16[8,1024]{1,0:T(8,128)(2,1)}, u32[]{:S(2)}, u32[]{:S(2)}) collective-permute-start(bf16[8,1024]{1,0:T(8,128)(2,1)} %fusion.123), channel_id=1, source_target_pairs={{0,4},{4,0},{8,12},{12,8},{16,20},{20,16},{24,28},{28,24},{1,5},{5... | collective-permute-start | bytes 49160 | tf_op jit(solution)/shard_map/ppermute | solution.py:11
  16.4 4.2 %collective-permute-start.4 = (bf16[16,1024]{1,0:T(8,128)(2,1)}, bf16[16,1024]{1,0:T(8,128)(2,1)}, u32[]{:S(2)}, u32[]{:S(2)}) collective-permute-start(bf16[16,1024]{1,0:T(8,128)(2,1)} %maximum_select_fusion.2), channel_id=1, source_target_pairs={{0,8},{4,12},{8,0},{12,4},{16,24},{20,28},{24,16},{28,20},{1,9},{5... | collective-permute-start | bytes 98312 | tf_op jit(solution)/shard_map/ppermute | solution.py:11
  19.6 5.0 %collective-permute-start.1 = (bf16[16,8,768]{2,1,0:T(8,128)(2,1)}, bf16[16,8,768]{2,1,0:T(8,128)(2,1)S(1)}, u32[]{:S(2)}, u32[]{:S(2)}) collective-permute-start(bf16[16,8,768]{2,1,0:T(8,128)(2,1)} %add_convert_fusion.4), channel_id=1, source_target_pairs={{0,2},{2,0},{1,3},{3,1},{4,6},{6,4},{5,7},{7,5},{8,10},{10,8},{9,1... | collective-permute-start | bytes 589832 | tf_op jit(solution)/shard_map/ppermute | solution.py:11
  22.1 9.7 %collective-permute-start.5 = (bf16[32,1024]{1,0:T(8,128)(2,1)}, bf16[32,1024]{1,0:T(8,128)(2,1)}, u32[]{:S(2)}, u32[]{:S(2)}) collective-permute-start(bf16[32,1024]{1,0:T(8,128)(2,1)} %maximum_select_fusion.1), channel_id=1, source_target_pairs={{0,16},{4,20},{8,24},{12,28},{16,0},{20,4},{24,8},{28,12},{1,17},{... | collective-permute-start | bytes 196616 | tf_op jit(solution)/shard_map/ppermute | solution.py:11
  25.5 1.3 %copy-start.7 = (f32[768]{0:T(1024)S(1)}, f32[768]{0:T(1024)}, u32[]{:S(2)}) copy-start(f32[768]{0:T(1024)} %copy-done.6) | copy-start | bytes 9220
  26.3 0.7 copy-start.16
  27.8 2.8 %copy-start.25 = (bf16[1,1536,768]{2,1,0:T(8,128)(2,1)S(1)}, bf16[1,1536,768]{2,1,0:T(8,128)(2,1)}, u32[]{:S(2)}) copy-start(bf16[1,1536,768]{2,1,0:T(8,128)(2,1)} %param.12) | copy-start | bytes 7077892
  28.8 0.6 copy-start.21
  29.4 0.6 copy-start.5
  30.5 2.3 %copy-start.4 = (f32[128,1536]{1,0:T(8,128)}, f32[128,1536]{1,0:T(8,128)S(1)}, u32[]{:S(2)}) copy-start(f32[128,1536]{1,0:T(8,128)S(1)} %fusion.12) | copy-start | bytes 2359300
  30.5 1.2 %copy-start.26 = (s32[8]{0:T(128)S(1)}, s32[8]{0:T(128)}, u32[]{:S(2)}) copy-start(s32[8]{0:T(128)} %param.15) | copy-start | bytes 100
  30.6 1.2 %copy-start.27 = (s32[64]{0:T(128)S(1)}, s32[64]{0:T(128)}, u32[]{:S(2)}) copy-start(s32[64]{0:T(128)} %fusion.139) | copy-start | bytes 772
  30.6 7.7 %copy-start.1 = (bf16[768,1024]{1,0:T(8,128)(2,1)S(1)}, bf16[768,1024]{1,0:T(8,128)(2,1)}, u32[]{:S(2)}) copy-start(bf16[768,1024]{1,0:T(8,128)(2,1)} %param.13) | copy-start | bytes 4718596
  31.2 6.6 %collective-permute-start.2 = (bf16[16,8,768]{2,1,0:T(8,128)(2,1)S(1)}, bf16[16,8,768]{2,1,0:T(8,128)(2,1)S(1)}, u32[]{:S(2)}, u32[]{:S(2)}) collective-permute-start(bf16[16,8,768]{2,1,0:T(8,128)(2,1)S(1)} %fusion.19), channel_id=1, source_target_pairs={{0,1},{1,0},{2,3},{3,2},{4,5},{5,4},{6,7},{7,6},{8,9},{9,8},{10,11... | collective-permute-start | bytes 589832 | tf_op jit(solution)/shard_map/ppermute | solution.py:11
  46.3 8.6 %copy-start.17 = (f32[768]{0:T(1024)S(1)}, f32[768]{0:T(1024)}, u32[]{:S(2)}) copy-start(f32[768]{0:T(1024)} %copy-done.15) | copy-start | bytes 9220
  46.3 5.8 %collective-permute-start.6 = (bf16[16,8,768]{2,1,0:T(8,128)(2,1)S(1)}, bf16[16,8,768]{2,1,0:T(8,128)(2,1)S(1)}, u32[]{:S(2)}, u32[]{:S(2)}) collective-permute-start(bf16[16,8,768]{2,1,0:T(8,128)(2,1)S(1)} %fusion.31), channel_id=1, source_target_pairs={{0,1},{1,0},{2,3},{3,2},{4,5},{5,4},{6,7},{7,6},{8,9},{9,8},{10,11... | collective-permute-start | bytes 589832 | tf_op jit(solution)/shard_map/ppermute | solution.py:11
  52.3 2.7 %copy-start.13 = (f32[768]{0:T(1024)S(1)}, f32[768]{0:T(1024)}, u32[]{:S(2)}) copy-start(f32[768]{0:T(1024)} %copy-done.12) | copy-start | bytes 9220
  53.0 2.0 %copy-start.10 = (f32[768]{0:T(1024)S(1)}, f32[768]{0:T(1024)}, u32[]{:S(2)}) copy-start(f32[768]{0:T(1024)} %copy-done.9) | copy-start | bytes 9220
  55.0 0.7 copy-start.8
  55.7 0.7 copy-start.19
  59.7 1.4 %collective-permute-start.7 = (bf16[16,8,768]{2,1,0:T(8,128)(2,1)S(1)}, bf16[16,8,768]{2,1,0:T(8,128)(2,1)S(1)}, u32[]{:S(2)}, u32[]{:S(2)}) collective-permute-start(bf16[16,8,768]{2,1,0:T(8,128)(2,1)S(1)} %get-tuple-element.54), channel_id=1, source_target_pairs={{0,2},{2,0},{1,3},{3,1},{4,6},{6,4},{5,7},{7,5},{8,10},{10,8},{9,1... | collective-permute-start | bytes 589832 | tf_op jit(solution)/shard_map/ppermute | solution.py:11
  64.8 8.4 %copy-start.18 = (f32[768]{0:T(1024)S(1)}, f32[768]{0:T(1024)}, u32[]{:S(2)}) copy-start(f32[768]{0:T(1024)} %copy-done.15) | copy-start | bytes 9220
  64.8 7.0 %collective-permute-start.8 = (bf16[16,8,768]{2,1,0:T(8,128)(2,1)S(1)}, bf16[16,8,768]{2,1,0:T(8,128)(2,1)S(1)}, u32[]{:S(2)}, u32[]{:S(2)}) collective-permute-start(bf16[16,8,768]{2,1,0:T(8,128)(2,1)S(1)} %fusion.28), channel_id=1, source_target_pairs={{0,1},{1,0},{2,3},{3,2},{4,5},{5,4},{6,7},{7,6},{8,9},{9,8},{10,11... | collective-permute-start | bytes 589832 | tf_op jit(solution)/shard_map/ppermute | solution.py:11
  72.0 1.3 %copy-start.14 = (f32[768]{0:T(1024)S(1)}, f32[768]{0:T(1024)}, u32[]{:S(2)}) copy-start(f32[768]{0:T(1024)} %copy-done.12) | copy-start | bytes 9220
  72.7 0.7 copy-start.11
  73.6 1.0 %copy-start.2 = (f32[16,8,768]{2,1,0:T(8,128)S(1)}, f32[16,8,768]{2,1,0:T(8,128)}, u32[]{:S(2)}) copy-start(f32[16,8,768]{2,1,0:T(8,128)} %get-tuple-element.55) | copy-start | bytes 1179652

commit v3 on v2

--- a/solution.py
+++ b/solution.py
@@ -69,18 +69,17 @@
 
 def gather_rows(block, axis):
     count = lax.axis_size(axis)
-    place = lax.axis_index(axis)
     stride = 0
     while (1 << stride) < count:
-        other = swapped(block, axis, stride)
-        upper = (place >> stride) & 1
-        block = jnp.where(
-            upper == 0,
-            jnp.concatenate([block, other], axis=0),
-            jnp.concatenate([other, block], axis=0),
-        )
+        block = jnp.concatenate([block, swapped(block, axis, stride)], axis=0)
         stride += 1
     return block
+
+
+def gathered_row_ids(rows, axis):
+    place = lax.axis_index(axis)
+    spot = jnp.arange(rows * lax.axis_size(axis), dtype=jnp.int32)
+    return jnp.bitwise_xor(place, spot // rows) * rows + spot % rows
 
 
 def hand_over(values):
@@ -111,7 +110,7 @@
         weights = jnp.exp(cosine_score_matrix).astype(jnp.bfloat16)
         softmax_denominators = jnp.sum(weights.astype(jnp.float32), axis=1)
         softmax_scaled_captions = jnp.dot(weights, text_block, preferred_element_type=jnp.float32)
-        global_rows = row_map(jnp.arange(block_rows, dtype=jnp.int32))
+        global_rows = row_map(block_rows)
         onehot = (pair_index[:, None] == global_rows[None, :]).astype(jnp.bfloat16)
         diagonal_matched_scores = jnp.dot(onehot, text_block, preferred_element_type=jnp.float32)
         return (softmax_denominators, softmax_scaled_captions, diagonal_matched_scores)
@@ -144,8 +143,8 @@
     share_count = 1
     share_rows = text_rows // share_count
 
-    def share_map(rows_now):
-        return rows_now // share_rows * text_rows + rows_now % share_rows
+    def share_map(block_rows):
+        return gathered_row_ids(text_rows, "batch")
 
     start_state = (
         jnp.zeros((image_rows,), jnp.float32),

time: 77.9 us -> 76.5 us (0.982)
  other arithmetic: 22.4 us -> 20.9 us
    select_n x2 -> x0, other arithmetic: 2.89 us -> none  [gather_rows(): jnp.where(upper == 0, jnp.concatenate([block, other], axis=0), jnp.concat...]
    concatenate x0 -> x2, other arithmetic: none -> 2.12 us  [gather_rows(): block = jnp.concatenate([block, swapped(block, axis, stride)], axis=0)]
    unnamed x57 -> x61, local copies, waits for them, and re-layouts: 5.96 us -> 5.95 us
  transfers between devices with their start and end apart: 9 -> 9, of which waited for: 6 -> 6; matrix products, arithmetic and copies ran while one was open for 16% -> 14% of each run, Pallas kernels for 0% -> 0%
where the time goes in v3:
time: 76.5 us; the launch traced here: 75.4 us
  waiting for transfers between devices  21.1 us (28%)
  other arithmetic  20.9 us (27%)
  matrix products  13.8 us (18%)
  starting transfers between devices  10.5 us (14%)
  local copies, waits for them, and re-layouts  8.33 us (11%)
    ppermute x9, waiting for transfers between devices, swapped(): lax.ppermute(value, axis, [(i, i ^ 1 << stride) for i in range(lax.axis_s...  21.1 us
    ppermute x9, starting transfers between devices, swapped(): lax.ppermute(value, axis, [(i, i ^ 1 << stride) for i in range(lax.axis_s...  10.5 us
    dot_general x4, matrix products, mlp_part(): jnp.dot(flattened, expand, preferred_element_type=jnp.float32)  8.17 us
    unnamed x61, local copies, waits for them, and re-layouts  5.95 us
    convert_element_type x1, other arithmetic, on_device(): returned = hand_over(grad_first_in.astype(jnp.bfloat16))  3.3 us
    unnamed x31, other arithmetic  3.03 us
    reduce_sum x6, other arithmetic, normalize_last(): centred = values - jnp.mean(values, axis=-1, keepdims=True)  2.3 us
    concatenate x2, other arithmetic, gather_rows(): block = jnp.concatenate([block, swapped(block, axis, stride)], axis=0)  2.12 us
  transfers between devices with their start and end apart: 9, of which 6 were waited for; matrix products, arithmetic and copies ran while one was open for 14% of the time, Pallas kernels for 0%

profile of v3, /device:TPU:0, one launch (start us, length us, event | category | flops | bytes accessed | tf_op | source)
XLA Modules:
  0.0 75.4 jit_solution(1925660923525743476)
XLA Ops:
  0.0 1.1 %copy.13 = f32[1,7,7,768]{3,2,0,1:T(8,128)S(1)} copy(f32[1,7,7,768]{3,0,2,1:T(1,128)} %param.9) | data formatting | bytes 301056
  1.2 0.2 slice_reduce_fusion.20
  1.4 0.2 slice_reduce_fusion
  1.6 1.0 %copy.9 = f32[8,4,4,768]{3,0,2,1:T(8,128)S(1)} copy(bf16[8,4,4,768]{3,2,1,0:T(4,128)(2,1)} %param.8) | data formatting | bytes 589824 | tf_op jit(solution)/shard_map/convert_element_type | solution.py:90
  3.5 0.1 reduce_sum.148
  3.6 0.2 multiply_reduce_fusion.3
  3.8 0.6 copy-done.20
  4.5 0.5 fusion.14
  5.0 0.9 %copy-done.3 = f32[128,1536]{1,0:T(8,128)} copy-done((f32[128,1536]{1,0:T(8,128)}, f32[128,1536]{1,0:T(8,128)S(1)}, u32[]{:S(2)}) %copy-start.3) | copy-done | bytes 786456
  5.9 0.5 copy-done.26
  6.4 0.6 fusion.16
  7.0 3.1 %collective-permute-start = (bf16[16,8,768]{2,1,0:T(8,128)(2,1)S(1)}, bf16[16,8,768]{2,1,0:T(8,128)(2,1)}, u32[]{:S(2)}, u32[]{:S(2)}) collective-permute-start(bf16[16,8,768]{2,1,0:T(8,128)(2,1)S(1)} %fusion.16), channel_id=1, source_target_pairs={{0,1},{1,0},{2,3},{3,2},{4,5},{5,4},{6,7},{7,6},{8,9},{9,8},{10,11... | collective-permute-start | bytes 589832 | tf_op jit(solution)/shard_map/ppermute | solution.py:11
  10.1 0.1 fusion.122
  10.2 0.7 fusion.123
  10.9 1.5 %collective-permute-start.3 = (bf16[8,1024]{1,0:T(8,128)(2,1)}, bf16[8,1024]{1,0:T(8,128)(2,1)}, u32[]{:S(2)}, u32[]{:S(2)}) collective-permute-start(bf16[8,1024]{1,0:T(8,128)(2,1)} %fusion.123), channel_id=1, source_target_pairs={{0,4},{4,0},{8,12},{12,8},{16,20},{20,16},{24,28},{28,24},{1,5},{5... | collective-permute-start | bytes 49160 | tf_op jit(solution)/shard_map/ppermute | solution.py:11
  12.4 2.6 %collective-permute-done.3 = bf16[8,1024]{1,0:T(8,128)(2,1)} collective-permute-done((bf16[8,1024]{1,0:T(8,128)(2,1)}, bf16[8,1024]{1,0:T(8,128)(2,1)}, u32[]{:S(2)}, u32[]{:S(2)}) %collective-permute-start.3) | collective-permute-done | bytes 16416 | tf_op jit(solution)/shard_map/ppermute | solution.py:11
  14.9 0.7 pad_maximum_fusion.2
  15.7 1.6 %collective-permute-start.4 = (bf16[16,1024]{1,0:T(8,128)(2,1)S(1)}, bf16[16,1024]{1,0:T(8,128)(2,1)S(1)}, u32[]{:S(2)}, u32[]{:S(2)}) collective-permute-start(bf16[16,1024]{1,0:T(8,128)(2,1)S(1)} %pad_maximum_fusion.2), channel_id=1, source_target_pairs={{0,8},{4,12},{8,0},{12,4},{16,24},{20,28},{24,16},{28,20},{1,9},{5... | collective-permute-start | bytes 98312 | tf_op jit(solution)/shard_map/ppermute | solution.py:11
  17.3 1.0 %add_convert_fusion.4 = bf16[16,8,768]{2,1,0:T(8,128)(2,1)S(1)} fusion(bf16[16,8,768]{2,1,0:T(8,128)(2,1)} %collective-permute-done, bf16[16,8,768]{2,1,0:T(8,128)(2,1)S(1)} %fusion.16, f32[8,4,4,768]{3,0,2,1:T(8,128)S(1)} %copy.9), kind=kLoop, calls=%fused_computation.95 | loop fusion | flops 688128 | bytes 983040 | tf_op jit(solution)/shard_map/convert_element_type | solution.py:94
  18.3 0.5 fusion.139
  18.9 0.7 collective-permute-done.4
  19.6 1.4 %pad_maximum_fusion.1 = bf16[32,1024]{1,0:T(8,128)(2,1)} fusion(bf16[16,1024]{1,0:T(8,128)(2,1)S(1)} %collective-permute-done.4, bf16[8,1024]{1,0:T(8,128)(2,1)} %collective-permute-done.3, bf16[8,1024]{1,0:T(8,128)(2,1)} %fusion.123), kind=kLoop, calls=%fused_computation.161 | loop fusion | flops 196608 | bytes 131072 | tf_op jit(solution)/shard_map/concatenate | solution.py:74
  21.0 2.6 %collective-permute-start.5 = (bf16[32,1024]{1,0:T(8,128)(2,1)}, bf16[32,1024]{1,0:T(8,128)(2,1)}, u32[]{:S(2)}, u32[]{:S(2)}) collective-permute-start(bf16[32,1024]{1,0:T(8,128)(2,1)} %pad_maximum_fusion.1), channel_id=1, source_target_pairs={{0,16},{4,20},{8,24},{12,28},{16,0},{20,4},{24,8},{28,12},{1,17},{... | collective-permute-start | bytes 196616 | tf_op jit(solution)/shard_map/ppermute | solution.py:11
  23.6 0.7 constant_dynamic-update-slice_fusion.31
  24.5 0.7 constant_dynamic-update-slice_fusion.28
  26.0 0.7 reduce_sum.153
  26.7 0.8 %broadcast_multiply_fusion.512 = f32[16,8]{1,0:T(8,128)S(1)} fusion(f32[16,8]{1,0:T(8,128)} %reduce_sum.153), kind=kLoop, calls=%fused_computation.708 | loop fusion | flops 128 | bytes 1024 | tf_op jit(solution)/shard_map/jvp()/div | solution.py:33
  27.5 0.2 multiply_reduce_fusion.2
  27.7 0.6 copy-done.21
  28.3 0.6 copy-done.5
  28.9 0.5 fusion.12
  29.5 0.6 fusion.19
  30.1 0.6 collective-permute-start.2
  30.7 1.1 %fusion.135 = f32[8,1024]{1,0:T(8,128)S(1)} fusion(s32[64]{0:T(128)S(1)} %copy-done.29, s32[8]{0:T(128)S(1)} %copy-done.28, bf16[32,1024]{1,0:T(8,128)(2,1)} %collective-permute-done.5, bf16[16,1024]{1,0:T(8,128)(2,1)S(1)} %copy-done.24, bf16[8,1024]{1,0:T(8,128)(2,1)} %collective-permute-done.3, bf16[8,1024]{1,0:T(8,128)(2,1)} %fusion.123), kind=kOutput, calls=%fused_computation.710 | convolution fusion | flops 1573376 | bytes 164128 | tf_op jit(solution)/shard_map/dot_general | solution.py:115
  31.7 4.7 %collective-permute-done.2 = bf16[16,8,768]{2,1,0:T(8,128)(2,1)S(1)} collective-permute-done((bf16[16,8,768]{2,1,0:T(8,128)(2,1)S(1)}, bf16[16,8,768]{2,1,0:T(8,128)(2,1)S(1)}, u32[]{:S(2)}, u32[]{:S(2)}) %collective-permute-start.2) | collective-permute-done | bytes 196640 | tf_op jit(solution)/shard_map/ppermute | solution.py:11
  36.5 0.1 multiply_reduce_fusion.8
  36.7 0.2 multiply_reduce_fusion.7
  36.9 0.5 multiply_reduce_fusion.5
  37.3 1.2 %convert_reduce_fusion.1 = (f32[8]{0:T(128)S(1)}, bf16[8,64]{1,0:T(8,128)(2,1)S(1)}) fusion(bf16[32,1024]{1,0:T(8,128)(2,1)} %collective-permute-done.5, bf16[16,1024]{1,0:T(8,128)(2,1)S(1)} %copy-done.24, bf16[8,1024]{1,0:T(8,128)(2,1)} %collective-permute-done.3, bf16[8,1024]{1,0:T(8,128)(2,1)} %fusion.123, f32[8,1024]{1,0:T(8,128)S(1)} %get-tuple-element.842, ...), kind=kOutput, calls=%fused_computation.707 | convolution fusion | flops 1591288 | bytes 164928 | tf_op jit(solution)/shard_map/ie,je->ij/dot_general | solution.py:107
  38.5 1.1 %multiply_reduce_fusion.4 = (f32[8]{0:T(128)S(1)}, f32[8,1024]{1,0:T(8,128)S(1)}) fusion(f32[8,1024]{1,0:T(8,128)S(1)} %get-tuple-element.842, f32[8,1024]{1,0:T(8,128)S(1)} %fusion.135, f32[8]{0:T(128)S(1)} %get-tuple-element.843, bf16[8,64]{1,0:T(8,128)(2,1)S(1)} %get-tuple-element.844, bf16[32,1024]{1,0:T(8,128)(2,1)} %collective-permute-done.5, ...), kind=kOutput, calls=%fused_computation.170 | convolution fusion | flops 1613816 | bytes 230464 | tf_op jit(solution)/shard_map/dot_general | solution.py:112
  39.6 0.6 multiply_reduce_fusion.6
  40.3 0.2 fusion.165
  40.5 0.7 add_multiply_fusion
  41.2 3.6 %fusion.31 = bf16[16,8,768]{2,1,0:T(8,128)(2,1)S(1)} fusion(bf16[1,768,1536]{2,1,0:T(8,128)(2,1)S(1)} %copy-done, f32[128,1536]{1,0:T(8,128)} %copy-done.4, bf16[1,1536,768]{2,1,0:T(8,128)(2,1)} %param.12, f32[8,768]{1,0:T(8,128)} %add_multiply_fusion), kind=kOutput, calls=%fused_computation.23 | convolution fusion | flops 608108544 | bytes 5726208 | tf_op jit(solution)/shard_map/transpose(jvp())/dot_general | solution.py:44
  44.8 0.6 collective-permute-start.6
  45.4 5.2 %collective-permute-done.6 = bf16[16,8,768]{2,1,0:T(8,128)(2,1)S(1)} collective-permute-done((bf16[16,8,768]{2,1,0:T(8,128)(2,1)S(1)}, bf16[16,8,768]{2,1,0:T(8,128)(2,1)S(1)}, u32[]{:S(2)}, u32[]{:S(2)}) %collective-permute-start.6) | collective-permute-done | bytes 196640 | tf_op jit(solution)/shard_map/ppermute | solution.py:11
  50.5 0.2 multiply_reduce_fusion.1
  50.7 0.7 multiply_multiply_fusion.5
  51.4 1.0 %fusion.120 = f32[16,8]{1,0:T(8,128)S(1)} fusion(f32[16,8]{1,0:T(8,128)S(1)} %multiply_multiply_fusion.5, f32[16,8,768]{2,1,0:T(8,128)S(1)} %constant_dynamic-update-slice_fusion.16, f32[16,8]{1,0:T(8,128)S(1)} %broadcast_multiply_fusion.512, f32[16,8]{1,0:T(8,128)} %copy-done.5, f32[768]{0:T(1024)S(1)} %reduce.49, ...), kind=kLoop, calls=%fused_computation.126 | loop fusion | flops 1179520 | bytes 791552 | tf_op jit(solution)/shard_map/transpose(jvp())/reduce_sum | solution.py:33
  52.4 0.9 %broadcast_add_fusion.1 = f32[16,8,768]{2,1,0:T(8,128)S(1)} fusion(f32[16,8]{1,0:T(8,128)S(1)} %negate_multiply_fusion.1, f32[16,8]{1,0:T(8,128)S(1)} %multiply_multiply_fusion.5, f32[16,8,768]{2,1,0:T(8,128)S(1)} %constant_dynamic-update-slice_fusion.16, f32[16,8]{1,0:T(8,128)S(1)} %broadcast_multiply_fusion.512, f32[16,8]{1,0:T(8,128)} %copy-done.5, ...), kind=kLoop, calls=%fused_computation.117 | loop fusion | flops 1179648 | bytes 1184768 | tf_op jit(solution)/shard_map/transpose(jvp())/add_any | solution.py:33
  53.7 0.4 copy-done.8
  54.4 0.4 copy-done.19
  54.8 3.3 %fusion.164 = (bf16[16,8,768]{2,1,0:T(8,128)(2,1)S(1)}, f32[16,8,768]{2,1,0:T(8,128)}) fusion(f32[1,8,768]{2,1,0:T(8,128)S(1)} %get-tuple-element.337, f32[1,8,768]{2,1,0:T(8,128)S(1)} %get-tuple-element.562, f32[1,8,768]{2,1,0:T(8,128)S(1)} %get-tuple-element.576, f32[1,8,768]{2,1,0:T(8,128)S(1)} %get-tuple-element.584, ...), kind=kLoop, calls=%fused_computation.801 | loop fusion | flops 25264128 | bytes 7274496 | tf_op jit(solution)/shard_map/convert_element_type | solution.py:163
  58.1 1.4 %collective-permute-done.7 = bf16[16,8,768]{2,1,0:T(8,128)(2,1)S(1)} collective-permute-done((bf16[16,8,768]{2,1,0:T(8,128)(2,1)S(1)}, bf16[16,8,768]{2,1,0:T(8,128)(2,1)S(1)}, u32[]{:S(2)}, u32[]{:S(2)}) %collective-permute-start.7) | collective-permute-done | bytes 196640 | tf_op jit(solution)/shard_map/ppermute | solution.py:11
  59.6 3.6 %fusion.28 = bf16[16,8,768]{2,1,0:T(8,128)(2,1)S(1)} fusion(bf16[1,768,1536]{2,1,0:T(8,128)(2,1)S(1)} %copy-done, f32[128,1536]{1,0:T(8,128)} %copy-done.3, bf16[1,1536,768]{2,1,0:T(8,128)(2,1)} %param.12, bf16[16,8,768]{2,1,0:T(8,128)(2,1)S(1)} %collective-permute-done.7), kind=kOutput, calls=%fused_computation.22 | convolution fusion | flops 608206848 | bytes 5898240 | tf_op jit(solution)/shard_map/transpose(jvp())/dot_general | solution.py:44
  63.2 0.6 collective-permute-start.8
  63.7 6.4 %collective-permute-done.8 = bf16[16,8,768]{2,1,0:T(8,128)(2,1)S(1)} collective-permute-done((bf16[16,8,768]{2,1,0:T(8,128)(2,1)S(1)}, bf16[16,8,768]{2,1,0:T(8,128)(2,1)S(1)}, u32[]{:S(2)}, u32[]{:S(2)}) %collective-permute-start.8) | collective-permute-done | bytes 196640 | tf_op jit(solution)/shard_map/ppermute | solution.py:11
  70.2 0.2 multiply_reduce_fusion
  70.4 0.7 multiply_multiply_fusion.4
  71.1 0.2 fusion.121
  71.3 0.2 broadcast_add_fusion
  72.3 0.7 copy-done.2
  73.0 1.5 %add_select_fusion = f32[16,8,768]{2,1,0:T(8,128)S(1)} fusion(f32[16,8,768]{2,1,0:T(8,128)S(1)} %copy-done.2, f32[1,8,768]{2,1,0:T(8,128)S(1)} %get-tuple-element.79, f32[1,8,768]{2,1,0:T(8,128)S(1)} %get-tuple-element.657, f32[1,8,768]{2,1,0:T(8,128)S(1)} %get-tuple-element.671, f32[1,8,768]{2,1,0:T(8,128)S(1)} %get-tuple-element.679, ...), kind=kLoop, calls=%fused_computation.76 | loop fusion | flops 25362432 | bytes 7643137 | tf_op jit(solution)/shard_map/jit(_where)/select_n | solution.py:165
  74.5 0.9 %copy.10 = f32[1,8,4,4,768]{4,3,2,1,0:T(4,128)} copy(f32[1,8,4,4,768]{4,1,3,2,0:T(8,128)S(1)} %bitcast.92) | data formatting | bytes 786432 | tf_op jit(solution)/shard_map/broadcast_in_dim;reshape | solution.py:166
  (139 shorter events, 3.5 us)
Async XLA Ops:
  0.0 4.5 %copy-start = (bf16[1,768,1536]{2,1,0:T(8,128)(2,1)S(1)}, bf16[1,768,1536]{2,1,0:T(8,128)(2,1)}, u32[]{:S(2)}) copy-start(bf16[1,768,1536]{2,1,0:T(8,128)(2,1)} %param.11) | copy-start | bytes 7077892
  1.4 1.7 %copy-start.9 = (f32[768]{0:T(1024)}, f32[768]{0:T(1024)S(1)}, u32[]{:S(2)}) copy-start(f32[768]{0:T(1024)S(1)} %get-tuple-element.26) | copy-start | bytes 9220
  1.4 1.7 %copy-start.12 = (f32[768]{0:T(1024)}, f32[768]{0:T(1024)S(1)}, u32[]{:S(2)}) copy-start(f32[768]{0:T(1024)S(1)} %get-tuple-element.38) | copy-start | bytes 9220
  1.5 1.7 %copy-start.6 = (f32[768]{0:T(1024)}, f32[768]{0:T(1024)S(1)}, u32[]{:S(2)}) copy-start(f32[768]{0:T(1024)S(1)} %get-tuple-element.8) | copy-start | bytes 9220
  1.6 1.9 %copy-start.15 = (f32[768]{0:T(1024)}, f32[768]{0:T(1024)S(1)}, u32[]{:S(2)}) copy-start(f32[768]{0:T(1024)S(1)} %get-tuple-element.5) | copy-start | bytes 9220
  3.0 1.4 %copy-start.25 = (f32[1,768]{1,0:T(1,128)S(1)}, f32[1,768]{1,0:T(1,128)}, u32[]{:S(2)}) copy-start(f32[1,768]{1,0:T(1,128)} %param.10) | copy-start | bytes 9220
  3.8 0.6 copy-start.20
  4.5 2.0 %copy-start.26 = (bf16[1,1536,768]{2,1,0:T(8,128)(2,1)S(1)}, bf16[1,1536,768]{2,1,0:T(8,128)(2,1)}, u32[]{:S(2)}) copy-start(bf16[1,1536,768]{2,1,0:T(8,128)(2,1)} %param.12) | copy-start | bytes 7077892
  5.0 0.9 %copy-start.3 = (f32[128,1536]{1,0:T(8,128)}, f32[128,1536]{1,0:T(8,128)S(1)}, u32[]{:S(2)}) copy-start(f32[128,1536]{1,0:T(8,128)S(1)} %fusion.14) | copy-start | bytes 2359300
  6.4 3.7 %copy-start.22 = (bf16[8,1024]{1,0:T(8,128)(2,1)S(1)}, bf16[8,1024]{1,0:T(8,128)(2,1)}, u32[]{:S(2)}) copy-start(bf16[8,1024]{1,0:T(8,128)(2,1)} %param.14) | copy-start | bytes 49156
  7.0 10.3 %collective-permute-start = (bf16[16,8,768]{2,1,0:T(8,128)(2,1)S(1)}, bf16[16,8,768]{2,1,0:T(8,128)(2,1)}, u32[]{:S(2)}, u32[]{:S(2)}) collective-permute-start(bf16[16,8,768]{2,1,0:T(8,128)(2,1)S(1)} %fusion.16), channel_id=1, source_target_pairs={{0,1},{1,0},{2,3},{3,2},{4,5},{5,4},{6,7},{7,6},{8,9},{9,8},{10,11... | collective-permute-start | bytes 589832 | tf_op jit(solution)/shard_map/ppermute | solution.py:11
  10.9 4.1 %collective-permute-start.3 = (bf16[8,1024]{1,0:T(8,128)(2,1)}, bf16[8,1024]{1,0:T(8,128)(2,1)}, u32[]{:S(2)}, u32[]{:S(2)}) collective-permute-start(bf16[8,1024]{1,0:T(8,128)(2,1)} %fusion.123), channel_id=1, source_target_pairs={{0,4},{4,0},{8,12},{12,8},{16,20},{20,16},{24,28},{28,24},{1,5},{5... | collective-permute-start | bytes 49160 | tf_op jit(solution)/shard_map/ppermute | solution.py:11
  15.7 3.9 %collective-permute-start.4 = (bf16[16,1024]{1,0:T(8,128)(2,1)S(1)}, bf16[16,1024]{1,0:T(8,128)(2,1)S(1)}, u32[]{:S(2)}, u32[]{:S(2)}) collective-permute-start(bf16[16,1024]{1,0:T(8,128)(2,1)S(1)} %pad_maximum_fusion.2), channel_id=1, source_target_pairs={{0,8},{4,12},{8,0},{12,4},{16,24},{20,28},{24,16},{28,20},{1,9},{5... | collective-permute-start | bytes 98312 | tf_op jit(solution)/shard_map/ppermute | solution.py:11
  18.3 5.3 %collective-permute-start.1 = (bf16[16,8,768]{2,1,0:T(8,128)(2,1)S(1)}, bf16[16,8,768]{2,1,0:T(8,128)(2,1)S(1)}, u32[]{:S(2)}, u32[]{:S(2)}) collective-permute-start(bf16[16,8,768]{2,1,0:T(8,128)(2,1)S(1)} %add_convert_fusion.4), channel_id=1, source_target_pairs={{0,2},{2,0},{1,3},{3,1},{4,6},{6,4},{5,7},{7,5},{8,10},{10,8},{9,1... | collective-permute-start | bytes 589832 | tf_op jit(solution)/shard_map/ppermute | solution.py:11
  19.6 5.9 %copy-start.23 = (bf16[16,1024]{1,0:T(8,128)(2,1)}, bf16[16,1024]{1,0:T(8,128)(2,1)S(1)}, u32[]{:S(2)}) copy-start(bf16[16,1024]{1,0:T(8,128)(2,1)S(1)} %collective-permute-done.4) | copy-start | bytes 98308
  21.0 9.7 %collective-permute-start.5 = (bf16[32,1024]{1,0:T(8,128)(2,1)}, bf16[32,1024]{1,0:T(8,128)(2,1)}, u32[]{:S(2)}, u32[]{:S(2)}) collective-permute-start(bf16[32,1024]{1,0:T(8,128)(2,1)} %pad_maximum_fusion.1), channel_id=1, source_target_pairs={{0,16},{4,20},{8,24},{12,28},{16,0},{20,4},{24,8},{28,12},{1,17},{... | collective-permute-start | bytes 196616 | tf_op jit(solution)/shard_map/ppermute | solution.py:11
  24.4 1.3 %copy-start.7 = (f32[768]{0:T(1024)S(1)}, f32[768]{0:T(1024)}, u32[]{:S(2)}) copy-start(f32[768]{0:T(1024)} %copy-done.6) | copy-start | bytes 9220
  25.3 0.7 copy-start.16
  26.7 2.8 %copy-start.27 = (bf16[1,1536,768]{2,1,0:T(8,128)(2,1)S(1)}, bf16[1,1536,768]{2,1,0:T(8,128)(2,1)}, u32[]{:S(2)}) copy-start(bf16[1,1536,768]{2,1,0:T(8,128)(2,1)} %param.12) | copy-start | bytes 7077892
  27.7 0.6 copy-start.21
  28.3 0.6 copy-start.5
  29.4 2.3 %copy-start.4 = (f32[128,1536]{1,0:T(8,128)}, f32[128,1536]{1,0:T(8,128)S(1)}, u32[]{:S(2)}) copy-start(f32[128,1536]{1,0:T(8,128)S(1)} %fusion.12) | copy-start | bytes 2359300
  29.4 1.2 %copy-start.24 = (bf16[16,1024]{1,0:T(8,128)(2,1)S(1)}, bf16[16,1024]{1,0:T(8,128)(2,1)}, u32[]{:S(2)}) copy-start(bf16[16,1024]{1,0:T(8,128)(2,1)} %copy-done.23) | copy-start | bytes 98308
  29.5 1.2 %copy-start.28 = (s32[8]{0:T(128)S(1)}, s32[8]{0:T(128)}, u32[]{:S(2)}) copy-start(s32[8]{0:T(128)} %param.15) | copy-start | bytes 100
  29.5 1.2 %copy-start.29 = (s32[64]{0:T(128)S(1)}, s32[64]{0:T(128)}, u32[]{:S(2)}) copy-start(s32[64]{0:T(128)} %fusion.139) | copy-start | bytes 772
  29.5 7.4 %copy-start.1 = (bf16[768,1024]{1,0:T(8,128)(2,1)S(1)}, bf16[768,1024]{1,0:T(8,128)(2,1)}, u32[]{:S(2)}) copy-start(bf16[768,1024]{1,0:T(8,128)(2,1)} %param.13) | copy-start | bytes 4718596
  30.1 6.4 %collective-permute-start.2 = (bf16[16,8,768]{2,1,0:T(8,128)(2,1)S(1)}, bf16[16,8,768]{2,1,0:T(8,128)(2,1)S(1)}, u32[]{:S(2)}, u32[]{:S(2)}) collective-permute-start(bf16[16,8,768]{2,1,0:T(8,128)(2,1)S(1)} %fusion.19), channel_id=1, source_target_pairs={{0,1},{1,0},{2,3},{3,2},{4,5},{5,4},{6,7},{7,6},{8,9},{9,8},{10,11... | collective-permute-start | bytes 589832 | tf_op jit(solution)/shard_map/ppermute | solution.py:11
  44.8 8.5 %copy-start.17 = (f32[768]{0:T(1024)S(1)}, f32[768]{0:T(1024)}, u32[]{:S(2)}) copy-start(f32[768]{0:T(1024)} %copy-done.15) | copy-start | bytes 9220
  44.8 5.7 %collective-permute-start.6 = (bf16[16,8,768]{2,1,0:T(8,128)(2,1)S(1)}, bf16[16,8,768]{2,1,0:T(8,128)(2,1)S(1)}, u32[]{:S(2)}, u32[]{:S(2)}) collective-permute-start(bf16[16,8,768]{2,1,0:T(8,128)(2,1)S(1)} %fusion.31), channel_id=1, source_target_pairs={{0,1},{1,0},{2,3},{3,2},{4,5},{5,4},{6,7},{7,6},{8,9},{9,8},{10,11... | collective-permute-start | bytes 589832 | tf_op jit(solution)/shard_map/ppermute | solution.py:11
  50.7 2.7 %copy-start.13 = (f32[768]{0:T(1024)S(1)}, f32[768]{0:T(1024)}, u32[]{:S(2)}) copy-start(f32[768]{0:T(1024)} %copy-done.12) | copy-start | bytes 9220
  51.4 2.0 %copy-start.10 = (f32[768]{0:T(1024)S(1)}, f32[768]{0:T(1024)}, u32[]{:S(2)}) copy-start(f32[768]{0:T(1024)} %copy-done.9) | copy-start | bytes 9220
  53.4 0.7 copy-start.8
  54.1 0.7 copy-start.19
  58.1 1.4 %collective-permute-start.7 = (bf16[16,8,768]{2,1,0:T(8,128)(2,1)S(1)}, bf16[16,8,768]{2,1,0:T(8,128)(2,1)S(1)}, u32[]{:S(2)}, u32[]{:S(2)}) collective-permute-start(bf16[16,8,768]{2,1,0:T(8,128)(2,1)S(1)} %get-tuple-element.54), channel_id=1, source_target_pairs={{0,2},{2,0},{1,3},{3,1},{4,6},{6,4},{5,7},{7,5},{8,10},{10,8},{9,1... | collective-permute-start | bytes 589832 | tf_op jit(solution)/shard_map/ppermute | solution.py:11
  63.2 8.4 %copy-start.18 = (f32[768]{0:T(1024)S(1)}, f32[768]{0:T(1024)}, u32[]{:S(2)}) copy-start(f32[768]{0:T(1024)} %copy-done.15) | copy-start | bytes 9220
  63.2 7.0 %collective-permute-start.8 = (bf16[16,8,768]{2,1,0:T(8,128)(2,1)S(1)}, bf16[16,8,768]{2,1,0:T(8,128)(2,1)S(1)}, u32[]{:S(2)}, u32[]{:S(2)}) collective-permute-start(bf16[16,8,768]{2,1,0:T(8,128)(2,1)S(1)} %fusion.28), channel_id=1, source_target_pairs={{0,1},{1,0},{2,3},{3,2},{4,5},{5,4},{6,7},{7,6},{8,9},{9,8},{10,11... | collective-permute-start | bytes 589832 | tf_op jit(solution)/shard_map/ppermute | solution.py:11
  70.4 1.3 %copy-start.14 = (f32[768]{0:T(1024)S(1)}, f32[768]{0:T(1024)}, u32[]{:S(2)}) copy-start(f32[768]{0:T(1024)} %copy-done.12) | copy-start | bytes 9220
  71.1 0.7 copy-start.11
  72.0 1.0 %copy-start.2 = (f32[16,8,768]{2,1,0:T(8,128)S(1)}, f32[16,8,768]{2,1,0:T(8,128)}, u32[]{:S(2)}) copy-start(f32[16,8,768]{2,1,0:T(8,128)} %get-tuple-element.55) | copy-start | bytes 1179652

commit v4 on v3

--- a/solution.py
+++ b/solution.py
@@ -61,17 +61,27 @@
     )
 
 
-def hidden_total(values):
+def swapped_within(value, axis, live_phase, stride):
+    count = lax.axis_size(axis)
+    phases = lax.axis_size("phase")
+    if axis == "batch":
+        pairs = [(i * phases + live_phase, (i ^ 1 << stride) * phases + live_phase) for i in range(count)]
+        return lax.ppermute(value, (axis, "phase"), pairs)
+    pairs = [(live_phase * count + i, live_phase * count + (i ^ 1 << stride)) for i in range(count)]
+    return lax.ppermute(value, ("phase", axis), pairs)
+
+
+def hidden_total(values, live_phase):
     low = values.astype(jnp.bfloat16)
-    other = swapped(low, "mp", 0)
+    other = swapped_within(low, "mp", live_phase, 0)
     return (low.astype(jnp.float32) + other.astype(jnp.float32)).astype(jnp.bfloat16).astype(jnp.float32)
 
 
-def gather_rows(block, axis):
+def gather_rows(block, axis, live_phase):
     count = lax.axis_size(axis)
     stride = 0
     while (1 << stride) < count:
-        block = jnp.concatenate([block, swapped(block, axis, stride)], axis=0)
+        block = jnp.concatenate([block, swapped_within(block, axis, live_phase, stride)], axis=0)
         stride += 1
     return block
 
@@ -86,17 +96,17 @@
     return swapped(values, "phase", 0)
 
 
-def section_forward(inputs_low, kernel, gain_vec, expand, project_out, side):
+def section_forward(inputs_low, kernel, gain_vec, expand, project_out, side, live_phase):
     widened = inputs_low.astype(jnp.float32)
     normed, front_back = jax.vjp(lambda inner: front_part(inner, kernel, gain_vec, side), widened)
     partial_out, mlp_back = jax.vjp(lambda inner: mlp_part(inner, expand, project_out), normed)
-    summed = hidden_total(partial_out)
+    summed = hidden_total(partial_out, live_phase)
     return ((widened + summed).astype(jnp.bfloat16), front_back, mlp_back)
 
 
-def section_backward(cotangent, front_back, mlp_back):
+def section_backward(cotangent, front_back, mlp_back, live_phase):
     (partial_grad,) = mlp_back(cotangent)
-    (from_front,) = front_back(hidden_total(partial_grad))
+    (from_front,) = front_back(hidden_total(partial_grad, live_phase))
     return cotangent + from_front
 
 
@@ -129,9 +139,9 @@
     count, side = images.shape[0], images.shape[1]
     width = images.shape[3]
     cell_major = images.reshape(count, side * side, width).transpose(1, 0, 2)
-    first_out, front_one, mlp_one = section_forward(cell_major, kernel, gain_vec, expand, project_out, side)
+    first_out, front_one, mlp_one = section_forward(cell_major, kernel, gain_vec, expand, project_out, side, 0)
     handed = hand_over(first_out)
-    second_out, front_two, mlp_two = section_forward(handed, kernel, gain_vec, expand, project_out, side)
+    second_out, front_two, mlp_two = section_forward(handed, kernel, gain_vec, expand, project_out, side, 1)
     embed, head_back = jax.vjp(
         lambda inner: head_part(inner, head_weight), second_out.astype(jnp.float32)
     )
@@ -153,15 +163,15 @@
     )
     fold_texts = make_fold(vector_lowered_total, pair_index, share_map)
     softmax_denominators, softmax_scaled_captions, diagonal_matched_scores = fold_texts(
-        start_state, gather_rows(caption_unit_vectors, "batch"), jnp.int32(0)
+        start_state, gather_rows(caption_unit_vectors, "batch", 1), jnp.int32(0)
     )
     encoder_output_slope = inverse_softness_factor * (
         softmax_scaled_captions / softmax_denominators[:, None] - diagonal_matched_scores
     )
     (grad_second,) = head_back(encoder_output_slope)
-    grad_first_in = section_backward(grad_second, front_two, mlp_two)
+    grad_first_in = section_backward(grad_second, front_two, mlp_two, 1)
     returned = hand_over(grad_first_in.astype(jnp.bfloat16))
-    grad_images = section_backward(returned.astype(jnp.float32), front_one, mlp_one)
+    grad_images = section_backward(returned.astype(jnp.float32), front_one, mlp_one, 0)
     chosen = jnp.where(phase_pick == 0, grad_images, grad_first_in)
     return chosen.transpose(1, 0, 2).reshape(count, side, side, width)[None]
 

time: 76.5 us -> 80.5 us (1.052)
  starting transfers between devices: 10.5 us -> 30.2 us
  waiting for transfers between devices: 21.1 us -> 5.47 us
    ppermute x9 -> x2, waiting for transfers between devices: 21.1 us -> 1.07 us  [swapped(): lax.ppermute(value, axis, [(i, i ^ 1 << stride) for i in range(lax.axis_s...]
    ppermute x0 -> x7, starting transfers between devices: none -> 13 us  [the longest x4 9.81 us: swapped_within(): return lax.ppermute(value, ('phase', axis), pairs)]
    ppermute x9 -> x2, starting transfers between devices: 10.5 us -> 17.2 us  [swapped(): lax.ppermute(value, axis, [(i, i ^ 1 << stride) for i in range(lax.axis_s...]
    ppermute x0 -> x7, waiting for transfers between devices: none -> 4.4 us  [the longest x4 4.39 us: swapped_within(): return lax.ppermute(value, ('phase', axis), pairs)]
  transfers between devices with their start and end apart: 9 -> 9, of which waited for: 6 -> 3; matrix products, arithmetic and copies ran while one was open for 14% -> 13% of each run, Pallas kernels for 0% -> 0%
where the time goes in v4:
time: 80.5 us; the launch traced here: 79.4 us
  starting transfers between devices  30.2 us (38%)
  other arithmetic  20.7 us (26%)
  matrix products  13.8 us (17%)
  local copies, waits for them, and re-layouts  8.33 us (10%)
  waiting for transfers between devices  5.47 us (7%)
  between operations  0.84 us (1%)
    ppermute x2, starting transfers between devices, swapped(): lax.ppermute(value, axis, [(i, i ^ 1 << stride) for i in range(lax.axis_s...  17.2 us
    ppermute x4, starting transfers between devices, swapped_within(): return lax.ppermute(value, ('phase', axis), pairs)  9.81 us
    dot_general x4, matrix products, mlp_part(): jnp.dot(flattened, expand, preferred_element_type=jnp.float32)  8.17 us
    unnamed x61, local copies, waits for them, and re-layouts  5.95 us
    ppermute x4, waiting for transfers between devices, swapped_within(): return lax.ppermute(value, ('phase', axis), pairs)  4.39 us
    ppermute x3, starting transfers between devices, swapped_within(): return lax.ppermute(value, (axis, 'phase'), pairs)  3.17 us
    convert_element_type x1, other arithmetic, on_device(): returned = hand_over(grad_first_in.astype(jnp.bfloat16))  3.12 us
    unnamed x31, other arithmetic  3.03 us
  transfers between devices with their start and end apart: 9, of which 3 were waited for; matrix products, arithmetic and copies ran while one was open for 13% of the time, Pallas kernels for 0%

profile of v4, /device:TPU:0, one launch (start us, length us, event | category | flops | bytes accessed | tf_op | source)
XLA Modules:
  0.0 79.4 jit_solution(12825720323372403821)
XLA Ops:
  0.0 1.1 %copy.13 = f32[1,7,7,768]{3,2,0,1:T(8,128)S(1)} copy(f32[1,7,7,768]{3,0,2,1:T(1,128)} %param.9) | data formatting | bytes 301056
  1.1 0.1 slice_reduce_fusion.47
  1.2 0.2 slice_reduce_fusion.20
  1.4 0.2 slice_reduce_fusion
  1.6 1.0 %copy.9 = f32[8,4,4,768]{3,0,2,1:T(8,128)S(1)} copy(bf16[8,4,4,768]{3,2,1,0:T(4,128)(2,1)} %param.8) | data formatting | bytes 589824 | tf_op jit(solution)/shard_map/convert_element_type | solution.py:100
  3.5 0.1 reduce_sum.148
  3.6 0.2 multiply_reduce_fusion.3
  3.8 0.6 copy-done.20
  4.5 0.5 fusion.14
  5.0 0.9 %copy-done.3 = f32[128,1536]{1,0:T(8,128)} copy-done((f32[128,1536]{1,0:T(8,128)}, f32[128,1536]{1,0:T(8,128)S(1)}, u32[]{:S(2)}) %copy-start.3) | copy-done | bytes 786456
  5.9 0.5 copy-done.26
  6.4 0.6 fusion.16
  7.0 4.9 %collective-permute-start = (bf16[16,8,768]{2,1,0:T(8,128)(2,1)S(1)}, bf16[16,8,768]{2,1,0:T(8,128)(2,1)}, u32[]{:S(2)}, u32[]{:S(2)}) collective-permute-start(bf16[16,8,768]{2,1,0:T(8,128)(2,1)S(1)} %fusion.16), channel_id=1, source_target_pairs={{0,1},{1,0},{4,5},{5,4},{8,9},{9,8},{12,13},{13,12},{16,17},{17,16... | collective-permute-start | bytes 589832 | tf_op jit(solution)/shard_map/ppermute | solution.py:71
  11.9 0.1 fusion.122
  12.1 0.7 fusion.123
  12.7 1.2 %collective-permute-start.3 = (bf16[8,1024]{1,0:T(8,128)(2,1)}, bf16[8,1024]{1,0:T(8,128)(2,1)}, u32[]{:S(2)}, u32[]{:S(2)}) collective-permute-start(bf16[8,1024]{1,0:T(8,128)(2,1)} %fusion.123), channel_id=1, source_target_pairs={{2,6},{6,2},{10,14},{14,10},{18,22},{22,18},{26,30},{30,26},{3,7},... | collective-permute-start | bytes 49160 | tf_op jit(solution)/shard_map/ppermute | solution.py:69
  14.0 0.7 pad_maximum_fusion.2
  14.7 0.7 collective-permute-start.4
  15.4 0.3 collective-permute-done
  15.7 1.0 %add_convert_fusion.4 = bf16[16,8,768]{2,1,0:T(8,128)(2,1)S(1)} fusion(bf16[16,8,768]{2,1,0:T(8,128)(2,1)} %collective-permute-done, bf16[16,8,768]{2,1,0:T(8,128)(2,1)S(1)} %fusion.16, f32[8,4,4,768]{3,0,2,1:T(8,128)S(1)} %copy.9), kind=kLoop, calls=%fused_computation.95 | loop fusion | flops 688128 | bytes 983040 | tf_op jit(solution)/shard_map/convert_element_type | solution.py:104
  16.7 3.9 %collective-permute-start.1 = (bf16[16,8,768]{2,1,0:T(8,128)(2,1)S(1)}, bf16[16,8,768]{2,1,0:T(8,128)(2,1)S(1)}, u32[]{:S(2)}, u32[]{:S(2)}) collective-permute-start(bf16[16,8,768]{2,1,0:T(8,128)(2,1)S(1)} %add_convert_fusion.4), channel_id=1, source_target_pairs={{0,2},{2,0},{1,3},{3,1},{4,6},{6,4},{5,7},{7,5},{8,10},{10,8},{9,1... | collective-permute-start | bytes 589832 | tf_op jit(solution)/shard_map/ppermute | solution.py:11
  20.6 0.5 fusion.139
  21.1 1.4 %pad_maximum_fusion.1 = bf16[32,1024]{1,0:T(8,128)(2,1)} fusion(bf16[16,1024]{1,0:T(8,128)(2,1)S(1)} %collective-permute-done.4, bf16[8,1024]{1,0:T(8,128)(2,1)} %collective-permute-done.3, bf16[8,1024]{1,0:T(8,128)(2,1)} %fusion.123), kind=kLoop, calls=%fused_computation.161 | loop fusion | flops 196608 | bytes 131072 | tf_op jit(solution)/shard_map/concatenate | solution.py:84
  22.5 1.3 %collective-permute-start.5 = (bf16[32,1024]{1,0:T(8,128)(2,1)}, bf16[32,1024]{1,0:T(8,128)(2,1)}, u32[]{:S(2)}, u32[]{:S(2)}) collective-permute-start(bf16[32,1024]{1,0:T(8,128)(2,1)} %pad_maximum_fusion.1), channel_id=1, source_target_pairs={{2,18},{6,22},{10,26},{14,30},{18,2},{22,6},{26,10},{30,14},{3,19}... | collective-permute-start | bytes 196616 | tf_op jit(solution)/shard_map/ppermute | solution.py:69
  23.8 0.7 constant_dynamic-update-slice_fusion.31
  24.7 0.7 constant_dynamic-update-slice_fusion.28
  26.2 0.7 reduce_sum.153
  26.8 0.8 %broadcast_multiply_fusion.512 = f32[16,8]{1,0:T(8,128)S(1)} fusion(f32[16,8]{1,0:T(8,128)} %reduce_sum.153), kind=kLoop, calls=%fused_computation.708 | loop fusion | flops 128 | bytes 1024 | tf_op jit(solution)/shard_map/jvp()/div | solution.py:33
  27.7 0.2 multiply_reduce_fusion.2
  27.9 0.6 copy-done.21
  28.5 0.6 copy-done.5
  29.1 0.5 fusion.12
  29.7 0.6 fusion.19
  30.3 0.8 %collective-permute-start.2 = (bf16[16,8,768]{2,1,0:T(8,128)(2,1)S(1)}, bf16[16,8,768]{2,1,0:T(8,128)(2,1)S(1)}, u32[]{:S(2)}, u32[]{:S(2)}) collective-permute-start(bf16[16,8,768]{2,1,0:T(8,128)(2,1)S(1)} %fusion.19), channel_id=1, source_target_pairs={{2,3},{3,2},{6,7},{7,6},{10,11},{11,10},{14,15},{15,14},{18,19},{1... | collective-permute-start | bytes 589832 | tf_op jit(solution)/shard_map/ppermute | solution.py:71
  31.1 1.1 %fusion.135 = f32[8,1024]{1,0:T(8,128)S(1)} fusion(s32[64]{0:T(128)S(1)} %copy-done.29, s32[8]{0:T(128)S(1)} %copy-done.28, bf16[32,1024]{1,0:T(8,128)(2,1)} %collective-permute-done.5, bf16[16,1024]{1,0:T(8,128)(2,1)S(1)} %copy-done.24, bf16[8,1024]{1,0:T(8,128)(2,1)} %collective-permute-done.3, bf16[8,1024]{1,0:T(8,128)(2,1)} %fusion.123), kind=kOutput, calls=%fused_computation.710 | convolution fusion | flops 1573376 | bytes 164128 | tf_op jit(solution)/shard_map/dot_general | solution.py:125
  32.3 0.1 multiply_reduce_fusion.8
  32.4 0.2 multiply_reduce_fusion.7
  32.6 0.5 multiply_reduce_fusion.5
  33.1 1.2 %convert_reduce_fusion.1 = (f32[8]{0:T(128)S(1)}, bf16[8,64]{1,0:T(8,128)(2,1)S(1)}) fusion(bf16[32,1024]{1,0:T(8,128)(2,1)} %collective-permute-done.5, bf16[16,1024]{1,0:T(8,128)(2,1)S(1)} %copy-done.24, bf16[8,1024]{1,0:T(8,128)(2,1)} %collective-permute-done.3, bf16[8,1024]{1,0:T(8,128)(2,1)} %fusion.123, f32[8,1024]{1,0:T(8,128)S(1)} %get-tuple-element.842, ...), kind=kOutput, calls=%fused_computation.707 | convolution fusion | flops 1591288 | bytes 164928 | tf_op jit(solution)/shard_map/ie,je->ij/dot_general | solution.py:117
  34.3 1.1 %multiply_reduce_fusion.4 = (f32[8]{0:T(128)S(1)}, f32[8,1024]{1,0:T(8,128)S(1)}) fusion(f32[8,1024]{1,0:T(8,128)S(1)} %get-tuple-element.842, f32[8,1024]{1,0:T(8,128)S(1)} %fusion.135, f32[8]{0:T(128)S(1)} %get-tuple-element.843, bf16[8,64]{1,0:T(8,128)(2,1)S(1)} %get-tuple-element.844, bf16[32,1024]{1,0:T(8,128)(2,1)} %collective-permute-done.5, ...), kind=kOutput, calls=%fused_computation.170 | convolution fusion | flops 1613816 | bytes 230464 | tf_op jit(solution)/shard_map/dot_general | solution.py:122
  35.4 0.6 multiply_reduce_fusion.6
  36.0 0.2 fusion.165
  36.3 0.7 add_multiply_fusion
  36.9 3.6 %fusion.31 = bf16[16,8,768]{2,1,0:T(8,128)(2,1)S(1)} fusion(bf16[1,768,1536]{2,1,0:T(8,128)(2,1)S(1)} %copy-done, f32[128,1536]{1,0:T(8,128)} %copy-done.4, bf16[1,1536,768]{2,1,0:T(8,128)(2,1)} %param.12, f32[8,768]{1,0:T(8,128)} %add_multiply_fusion), kind=kOutput, calls=%fused_computation.23 | convolution fusion | flops 608108544 | bytes 5726208 | tf_op jit(solution)/shard_map/transpose(jvp())/dot_general | solution.py:44
  40.5 0.7 collective-permute-start.6
  41.2 0.2 multiply_reduce_fusion.1
  41.4 0.7 multiply_multiply_fusion.5
  42.1 1.0 %fusion.120 = f32[16,8]{1,0:T(8,128)S(1)} fusion(f32[16,8]{1,0:T(8,128)S(1)} %multiply_multiply_fusion.5, f32[16,8,768]{2,1,0:T(8,128)S(1)} %constant_dynamic-update-slice_fusion.16, f32[16,8]{1,0:T(8,128)S(1)} %broadcast_multiply_fusion.512, f32[16,8]{1,0:T(8,128)} %copy-done.5, f32[768]{0:T(1024)S(1)} %reduce.49, ...), kind=kLoop, calls=%fused_computation.126 | loop fusion | flops 1179520 | bytes 791552 | tf_op jit(solution)/shard_map/transpose(jvp())/reduce_sum | solution.py:33
  43.1 0.9 %broadcast_add_fusion.1 = f32[16,8,768]{2,1,0:T(8,128)S(1)} fusion(f32[16,8]{1,0:T(8,128)S(1)} %negate_multiply_fusion.1, f32[16,8]{1,0:T(8,128)S(1)} %multiply_multiply_fusion.5, f32[16,8,768]{2,1,0:T(8,128)S(1)} %constant_dynamic-update-slice_fusion.16, f32[16,8]{1,0:T(8,128)S(1)} %broadcast_multiply_fusion.512, f32[16,8]{1,0:T(8,128)} %copy-done.5, ...), kind=kLoop, calls=%fused_computation.117 | loop fusion | flops 1179648 | bytes 1184768 | tf_op jit(solution)/shard_map/transpose(jvp())/add_any | solution.py:33
  44.4 0.4 copy-done.8
  45.1 0.4 copy-done.19
  45.5 3.1 %fusion.164 = (bf16[16,8,768]{2,1,0:T(8,128)(2,1)S(1)}, f32[16,8,768]{2,1,0:T(8,128)}) fusion(f32[1,8,768]{2,1,0:T(8,128)S(1)} %get-tuple-element.337, f32[1,8,768]{2,1,0:T(8,128)S(1)} %get-tuple-element.562, f32[1,8,768]{2,1,0:T(8,128)S(1)} %get-tuple-element.576, f32[1,8,768]{2,1,0:T(8,128)S(1)} %get-tuple-element.584, ...), kind=kLoop, calls=%fused_computation.801 | loop fusion | flops 25264128 | bytes 7274496 | tf_op jit(solution)/shard_map/convert_element_type | solution.py:173
  48.7 13.3 %collective-permute-start.7 = (bf16[16,8,768]{2,1,0:T(8,128)(2,1)S(1)}, bf16[16,8,768]{2,1,0:T(8,128)(2,1)S(1)}, u32[]{:S(2)}, u32[]{:S(2)}) collective-permute-start(bf16[16,8,768]{2,1,0:T(8,128)(2,1)S(1)} %get-tuple-element.54), channel_id=1, source_target_pairs={{0,2},{2,0},{1,3},{3,1},{4,6},{6,4},{5,7},{7,5},{8,10},{10,8},{9,1... | collective-permute-start | bytes 589832 | tf_op jit(solution)/shard_map/ppermute | solution.py:11
  62.0 1.1 %collective-permute-done.7 = bf16[16,8,768]{2,1,0:T(8,128)(2,1)S(1)} collective-permute-done((bf16[16,8,768]{2,1,0:T(8,128)(2,1)S(1)}, bf16[16,8,768]{2,1,0:T(8,128)(2,1)S(1)}, u32[]{:S(2)}, u32[]{:S(2)}) %collective-permute-start.7) | collective-permute-done | bytes 196640 | tf_op jit(solution)/shard_map/ppermute | solution.py:11
  63.1 3.6 %fusion.28 = bf16[16,8,768]{2,1,0:T(8,128)(2,1)S(1)} fusion(bf16[1,768,1536]{2,1,0:T(8,128)(2,1)S(1)} %copy-done, f32[128,1536]{1,0:T(8,128)} %copy-done.3, bf16[1,1536,768]{2,1,0:T(8,128)(2,1)} %param.12, bf16[16,8,768]{2,1,0:T(8,128)(2,1)S(1)} %collective-permute-done.7), kind=kOutput, calls=%fused_computation.22 | convolution fusion | flops 608206848 | bytes 5898240 | tf_op jit(solution)/shard_map/transpose(jvp())/dot_general | solution.py:44
  66.6 3.4 %collective-permute-start.8 = (bf16[16,8,768]{2,1,0:T(8,128)(2,1)S(1)}, bf16[16,8,768]{2,1,0:T(8,128)(2,1)S(1)}, u32[]{:S(2)}, u32[]{:S(2)}) collective-permute-start(bf16[16,8,768]{2,1,0:T(8,128)(2,1)S(1)} %fusion.28), channel_id=1, source_target_pairs={{0,1},{1,0},{4,5},{5,4},{8,9},{9,8},{12,13},{13,12},{16,17},{17,16... | collective-permute-start | bytes 589832 | tf_op jit(solution)/shard_map/ppermute | solution.py:71
  70.1 4.1 %collective-permute-done.8 = bf16[16,8,768]{2,1,0:T(8,128)(2,1)S(1)} collective-permute-done((bf16[16,8,768]{2,1,0:T(8,128)(2,1)S(1)}, bf16[16,8,768]{2,1,0:T(8,128)(2,1)S(1)}, u32[]{:S(2)}, u32[]{:S(2)}) %collective-permute-start.8) | collective-permute-done | bytes 196640 | tf_op jit(solution)/shard_map/ppermute | solution.py:71
  74.2 0.2 multiply_reduce_fusion
  74.4 0.7 multiply_multiply_fusion.4
  75.1 0.2 fusion.121
  75.4 0.2 broadcast_add_fusion
  76.3 0.7 copy-done.2
  77.0 1.5 %add_select_fusion = f32[16,8,768]{2,1,0:T(8,128)S(1)} fusion(f32[16,8,768]{2,1,0:T(8,128)S(1)} %copy-done.2, f32[1,8,768]{2,1,0:T(8,128)S(1)} %get-tuple-element.79, f32[1,8,768]{2,1,0:T(8,128)S(1)} %get-tuple-element.657, f32[1,8,768]{2,1,0:T(8,128)S(1)} %get-tuple-element.671, f32[1,8,768]{2,1,0:T(8,128)S(1)} %get-tuple-element.679, ...), kind=kLoop, calls=%fused_computation.76 | loop fusion | flops 25362432 | bytes 7643137 | tf_op jit(solution)/shard_map/jit(_where)/select_n | solution.py:175
  78.5 0.9 %copy.10 = f32[1,8,4,4,768]{4,3,2,1,0:T(4,128)} copy(f32[1,8,4,4,768]{4,1,3,2,0:T(8,128)S(1)} %bitcast.92) | data formatting | bytes 786432 | tf_op jit(solution)/shard_map/broadcast_in_dim;reshape | solution.py:176
  (139 shorter events, 3.3 us)
Async XLA Ops:
  0.0 4.5 %copy-start = (bf16[1,768,1536]{2,1,0:T(8,128)(2,1)S(1)}, bf16[1,768,1536]{2,1,0:T(8,128)(2,1)}, u32[]{:S(2)}) copy-start(bf16[1,768,1536]{2,1,0:T(8,128)(2,1)} %param.11) | copy-start | bytes 7077892
  1.4 1.7 %copy-start.9 = (f32[768]{0:T(1024)}, f32[768]{0:T(1024)S(1)}, u32[]{:S(2)}) copy-start(f32[768]{0:T(1024)S(1)} %get-tuple-element.26) | copy-start | bytes 9220
  1.4 1.7 %copy-start.12 = (f32[768]{0:T(1024)}, f32[768]{0:T(1024)S(1)}, u32[]{:S(2)}) copy-start(f32[768]{0:T(1024)S(1)} %get-tuple-element.38) | copy-start | bytes 9220
  1.5 1.7 %copy-start.6 = (f32[768]{0:T(1024)}, f32[768]{0:T(1024)S(1)}, u32[]{:S(2)}) copy-start(f32[768]{0:T(1024)S(1)} %get-tuple-element.8) | copy-start | bytes 9220
  1.6 1.9 %copy-start.15 = (f32[768]{0:T(1024)}, f32[768]{0:T(1024)S(1)}, u32[]{:S(2)}) copy-start(f32[768]{0:T(1024)S(1)} %get-tuple-element.5) | copy-start | bytes 9220
  3.0 1.4 %copy-start.25 = (f32[1,768]{1,0:T(1,128)S(1)}, f32[1,768]{1,0:T(1,128)}, u32[]{:S(2)}) copy-start(f32[1,768]{1,0:T(1,128)} %param.10) | copy-start | bytes 9220
  3.8 0.6 copy-start.20
  4.5 2.0 %copy-start.26 = (bf16[1,1536,768]{2,1,0:T(8,128)(2,1)S(1)}, bf16[1,1536,768]{2,1,0:T(8,128)(2,1)}, u32[]{:S(2)}) copy-start(bf16[1,1536,768]{2,1,0:T(8,128)(2,1)} %param.12) | copy-start | bytes 7077892
  5.0 0.9 %copy-start.3 = (f32[128,1536]{1,0:T(8,128)}, f32[128,1536]{1,0:T(8,128)S(1)}, u32[]{:S(2)}) copy-start(f32[128,1536]{1,0:T(8,128)S(1)} %fusion.14) | copy-start | bytes 2359300
  6.4 5.5 %copy-start.22 = (bf16[8,1024]{1,0:T(8,128)(2,1)S(1)}, bf16[8,1024]{1,0:T(8,128)(2,1)}, u32[]{:S(2)}) copy-start(bf16[8,1024]{1,0:T(8,128)(2,1)} %param.14) | copy-start | bytes 49156
  7.0 8.7 %collective-permute-start = (bf16[16,8,768]{2,1,0:T(8,128)(2,1)S(1)}, bf16[16,8,768]{2,1,0:T(8,128)(2,1)}, u32[]{:S(2)}, u32[]{:S(2)}) collective-permute-start(bf16[16,8,768]{2,1,0:T(8,128)(2,1)S(1)} %fusion.16), channel_id=1, source_target_pairs={{0,1},{1,0},{4,5},{5,4},{8,9},{9,8},{12,13},{13,12},{16,17},{17,16... | collective-permute-start | bytes 589832 | tf_op jit(solution)/shard_map/ppermute | solution.py:71
  12.7 1.3 %collective-permute-start.3 = (bf16[8,1024]{1,0:T(8,128)(2,1)}, bf16[8,1024]{1,0:T(8,128)(2,1)}, u32[]{:S(2)}, u32[]{:S(2)}) collective-permute-start(bf16[8,1024]{1,0:T(8,128)(2,1)} %fusion.123), channel_id=1, source_target_pairs={{2,6},{6,2},{10,14},{14,10},{18,22},{22,18},{26,30},{30,26},{3,7},... | collective-permute-start | bytes 49160 | tf_op jit(solution)/shard_map/ppermute | solution.py:69
  14.7 6.4 %collective-permute-start.4 = (bf16[16,1024]{1,0:T(8,128)(2,1)S(1)}, bf16[16,1024]{1,0:T(8,128)(2,1)S(1)}, u32[]{:S(2)}, u32[]{:S(2)}) collective-permute-start(bf16[16,1024]{1,0:T(8,128)(2,1)S(1)} %pad_maximum_fusion.2), channel_id=1, source_target_pairs={{2,10},{6,14},{10,2},{14,6},{18,26},{22,30},{26,18},{30,22},{3,11}... | collective-permute-start | bytes 98312 | tf_op jit(solution)/shard_map/ppermute | solution.py:69
  16.7 7.1 %collective-permute-start.1 = (bf16[16,8,768]{2,1,0:T(8,128)(2,1)S(1)}, bf16[16,8,768]{2,1,0:T(8,128)(2,1)S(1)}, u32[]{:S(2)}, u32[]{:S(2)}) collective-permute-start(bf16[16,8,768]{2,1,0:T(8,128)(2,1)S(1)} %add_convert_fusion.4), channel_id=1, source_target_pairs={{0,2},{2,0},{1,3},{3,1},{4,6},{6,4},{5,7},{7,5},{8,10},{10,8},{9,1... | collective-permute-start | bytes 589832 | tf_op jit(solution)/shard_map/ppermute | solution.py:11
  21.1 4.6 %copy-start.23 = (bf16[16,1024]{1,0:T(8,128)(2,1)}, bf16[16,1024]{1,0:T(8,128)(2,1)S(1)}, u32[]{:S(2)}) copy-start(bf16[16,1024]{1,0:T(8,128)(2,1)S(1)} %collective-permute-done.4) | copy-start | bytes 98308
  22.5 8.6 %collective-permute-start.5 = (bf16[32,1024]{1,0:T(8,128)(2,1)}, bf16[32,1024]{1,0:T(8,128)(2,1)}, u32[]{:S(2)}, u32[]{:S(2)}) collective-permute-start(bf16[32,1024]{1,0:T(8,128)(2,1)} %pad_maximum_fusion.1), channel_id=1, source_target_pairs={{2,18},{6,22},{10,26},{14,30},{18,2},{22,6},{26,10},{30,14},{3,19}... | collective-permute-start | bytes 196616 | tf_op jit(solution)/shard_map/ppermute | solution.py:69
  24.6 1.3 %copy-start.7 = (f32[768]{0:T(1024)S(1)}, f32[768]{0:T(1024)}, u32[]{:S(2)}) copy-start(f32[768]{0:T(1024)} %copy-done.6) | copy-start | bytes 9220
  25.4 0.7 copy-start.16
  26.8 2.8 %copy-start.27 = (bf16[1,1536,768]{2,1,0:T(8,128)(2,1)S(1)}, bf16[1,1536,768]{2,1,0:T(8,128)(2,1)}, u32[]{:S(2)}) copy-start(bf16[1,1536,768]{2,1,0:T(8,128)(2,1)} %param.12) | copy-start | bytes 7077892
  27.9 0.6 copy-start.21
  28.5 0.6 copy-start.5
  29.6 2.6 %copy-start.4 = (f32[128,1536]{1,0:T(8,128)}, f32[128,1536]{1,0:T(8,128)S(1)}, u32[]{:S(2)}) copy-start(f32[128,1536]{1,0:T(8,128)S(1)} %fusion.12) | copy-start | bytes 2359300
  29.6 1.5 %copy-start.24 = (bf16[16,1024]{1,0:T(8,128)(2,1)S(1)}, bf16[16,1024]{1,0:T(8,128)(2,1)}, u32[]{:S(2)}) copy-start(bf16[16,1024]{1,0:T(8,128)(2,1)} %copy-done.23) | copy-start | bytes 98308
  29.6 1.5 %copy-start.28 = (s32[8]{0:T(128)S(1)}, s32[8]{0:T(128)}, u32[]{:S(2)}) copy-start(s32[8]{0:T(128)} %param.15) | copy-start | bytes 100
  29.6 1.5 %copy-start.29 = (s32[64]{0:T(128)S(1)}, s32[64]{0:T(128)}, u32[]{:S(2)}) copy-start(s32[64]{0:T(128)} %fusion.139) | copy-start | bytes 772
  29.7 2.9 %copy-start.1 = (bf16[768,1024]{1,0:T(8,128)(2,1)S(1)}, bf16[768,1024]{1,0:T(8,128)(2,1)}, u32[]{:S(2)}) copy-start(bf16[768,1024]{1,0:T(8,128)(2,1)} %param.13) | copy-start | bytes 4718596
  30.3 1.9 %collective-permute-start.2 = (bf16[16,8,768]{2,1,0:T(8,128)(2,1)S(1)}, bf16[16,8,768]{2,1,0:T(8,128)(2,1)S(1)}, u32[]{:S(2)}, u32[]{:S(2)}) collective-permute-start(bf16[16,8,768]{2,1,0:T(8,128)(2,1)S(1)} %fusion.19), channel_id=1, source_target_pairs={{2,3},{3,2},{6,7},{7,6},{10,11},{11,10},{14,15},{15,14},{18,19},{1... | collective-permute-start | bytes 589832 | tf_op jit(solution)/shard_map/ppermute | solution.py:71
  40.5 3.5 %copy-start.17 = (f32[768]{0:T(1024)S(1)}, f32[768]{0:T(1024)}, u32[]{:S(2)}) copy-start(f32[768]{0:T(1024)} %copy-done.15) | copy-start | bytes 9220
  40.5 0.7 collective-permute-start.6
  41.4 2.7 %copy-start.13 = (f32[768]{0:T(1024)S(1)}, f32[768]{0:T(1024)}, u32[]{:S(2)}) copy-start(f32[768]{0:T(1024)} %copy-done.12) | copy-start | bytes 9220
  42.1 2.0 %copy-start.10 = (f32[768]{0:T(1024)S(1)}, f32[768]{0:T(1024)}, u32[]{:S(2)}) copy-start(f32[768]{0:T(1024)} %copy-done.9) | copy-start | bytes 9220
  44.1 0.7 copy-start.8
  44.8 0.7 copy-start.19
  48.7 14.4 %collective-permute-start.7 = (bf16[16,8,768]{2,1,0:T(8,128)(2,1)S(1)}, bf16[16,8,768]{2,1,0:T(8,128)(2,1)S(1)}, u32[]{:S(2)}, u32[]{:S(2)}) collective-permute-start(bf16[16,8,768]{2,1,0:T(8,128)(2,1)S(1)} %get-tuple-element.54), channel_id=1, source_target_pairs={{0,2},{2,0},{1,3},{3,1},{4,6},{6,4},{5,7},{7,5},{8,10},{10,8},{9,1... | collective-permute-start | bytes 589832 | tf_op jit(solution)/shard_map/ppermute | solution.py:11
  66.6 8.9 %copy-start.18 = (f32[768]{0:T(1024)S(1)}, f32[768]{0:T(1024)}, u32[]{:S(2)}) copy-start(f32[768]{0:T(1024)} %copy-done.15) | copy-start | bytes 9220
  66.6 7.6 %collective-permute-start.8 = (bf16[16,8,768]{2,1,0:T(8,128)(2,1)S(1)}, bf16[16,8,768]{2,1,0:T(8,128)(2,1)S(1)}, u32[]{:S(2)}, u32[]{:S(2)}) collective-permute-start(bf16[16,8,768]{2,1,0:T(8,128)(2,1)S(1)} %fusion.28), channel_id=1, source_target_pairs={{0,1},{1,0},{4,5},{5,4},{8,9},{9,8},{12,13},{13,12},{16,17},{17,16... | collective-permute-start | bytes 589832 | tf_op jit(solution)/shard_map/ppermute | solution.py:71
  74.4 1.3 %copy-start.14 = (f32[768]{0:T(1024)S(1)}, f32[768]{0:T(1024)}, u32[]{:S(2)}) copy-start(f32[768]{0:T(1024)} %copy-done.12) | copy-start | bytes 9220
  75.1 0.7 copy-start.11
  76.0 1.0 %copy-start.2 = (f32[16,8,768]{2,1,0:T(8,128)S(1)}, f32[16,8,768]{2,1,0:T(8,128)}, u32[]{:S(2)}) copy-start(f32[16,8,768]{2,1,0:T(8,128)} %get-tuple-element.55) | copy-start | bytes 1179652

commit v5 on v3

--- a/solution.py
+++ b/solution.py
@@ -39,12 +39,25 @@
     return normalize_last(depthwise(values, kernel, side)) * gain_vec
 
 
+def expand_part(normed, expand):
+    flattened = normed.reshape(-1, normed.shape[-1]).astype(jnp.bfloat16)
+    return jnp.dot(flattened, expand, preferred_element_type=jnp.float32)
+
+
+def project_part(pre, project_out, shape):
+    hidden = jax.nn.gelu(pre).astype(jnp.bfloat16)
+    return jnp.dot(hidden, project_out, preferred_element_type=jnp.float32).reshape(shape)
+
+
 def mlp_part(normed, expand, project_out):
-    flattened = normed.reshape(-1, normed.shape[-1]).astype(jnp.bfloat16)
-    hidden = jax.nn.gelu(jnp.dot(flattened, expand, preferred_element_type=jnp.float32)).astype(
-        jnp.bfloat16
-    )
-    return jnp.dot(hidden, project_out, preferred_element_type=jnp.float32).reshape(normed.shape)
+    pre, expand_back = jax.vjp(lambda inner: expand_part(inner, expand), normed)
+    branch, project_back = jax.vjp(lambda inner: project_part(inner, project_out, normed.shape), pre)
+
+    def mlp_back(cotangent):
+        (pre_grad,) = project_back(cotangent)
+        return expand_back(lax.optimization_barrier(pre_grad))
+
+    return branch, mlp_back
 
 
 def head_part(values, head_weight):
@@ -89,7 +102,7 @@
 def section_forward(inputs_low, kernel, gain_vec, expand, project_out, side):
     widened = inputs_low.astype(jnp.float32)
     normed, front_back = jax.vjp(lambda inner: front_part(inner, kernel, gain_vec, side), widened)
-    partial_out, mlp_back = jax.vjp(lambda inner: mlp_part(inner, expand, project_out), normed)
+    partial_out, mlp_back = mlp_part(normed, expand, project_out)
     summed = hidden_total(partial_out)
     return ((widened + summed).astype(jnp.bfloat16), front_back, mlp_back)
 

time: 76.5 us -> 70.8 us (0.925)
  other arithmetic: 20.9 us -> 17.2 us
  local copies, waits for them, and re-layouts: 8.33 us -> 6.79 us
    unnamed x61 -> x57, local copies, waits for them, and re-layouts: 5.95 us -> 4.42 us
    dot_general x6 -> x8, matrix products: 9.33 us -> 9.45 us  [the longest x4 6.13 us: expand_part(): return jnp.dot(flattened, expand, preferred_element_type=jnp.float32)]
  transfers between devices with their start and end apart: 9 -> 9, of which waited for: 6 -> 6; matrix products, arithmetic and copies ran while one was open for 14% -> 16% of each run, Pallas kernels for 0% -> 0%
where the time goes in v5:
time: 70.8 us; the launch traced here: 70 us
  waiting for transfers between devices  20.9 us (30%)
  other arithmetic  17.2 us (24%)
  matrix products  13.8 us (19%)
  starting transfers between devices  10.5 us (15%)
  local copies, waits for them, and re-layouts  6.79 us (10%)
  between operations  0.76 us (1%)
    ppermute x9, waiting for transfers between devices, swapped(): lax.ppermute(value, axis, [(i, i ^ 1 << stride) for i in range(lax.axis_s...  20.9 us
    ppermute x9, starting transfers between devices, swapped(): lax.ppermute(value, axis, [(i, i ^ 1 << stride) for i in range(lax.axis_s...  10.5 us
    dot_general x4, matrix products, expand_part(): return jnp.dot(flattened, expand, preferred_element_type=jnp.float32)  6.13 us
    unnamed x57, local copies, waits for them, and re-layouts  4.42 us
    convert_element_type x1, other arithmetic, on_device(): returned = hand_over(grad_first_in.astype(jnp.bfloat16))  3.73 us
    dot_general x4, matrix products, project_part(): jnp.dot(hidden, project_out, preferred_element_type=jnp.float32)  3.31 us
    unnamed x31, other arithmetic  2.35 us
    concatenate x2, other arithmetic, gather_rows(): block = jnp.concatenate([block, swapped(block, axis, stride)], axis=0)  2.08 us
  transfers between devices with their start and end apart: 9, of which 6 were waited for; matrix products, arithmetic and copies ran while one was open for 16% of the time, Pallas kernels for 0%

profile of v5, /device:TPU:0, one launch (start us, length us, event | category | flops | bytes accessed | tf_op | source)
XLA Modules:
  0.0 70.0 jit_solution(6200120899458816841)
XLA Ops:
  0.0 1.1 %copy.13 = f32[1,7,7,768]{3,2,0,1:T(8,128)S(1)} copy(f32[1,7,7,768]{3,0,2,1:T(1,128)} %param.9) | data formatting | bytes 301056
  1.1 0.1 slice_reduce_fusion.47
  1.2 0.2 slice_reduce_fusion.20
  1.4 0.2 slice_reduce_fusion
  1.6 1.0 %copy.9 = f32[8,4,4,768]{3,0,2,1:T(8,128)S(1)} copy(bf16[8,4,4,768]{3,2,1,0:T(4,128)(2,1)} %param.8) | data formatting | bytes 589824 | tf_op jit(solution)/shard_map/convert_element_type | solution.py:103
  3.5 0.1 reduce_sum.148
  3.6 0.2 multiply_reduce_fusion.3
  3.9 0.5 copy-done.21
  4.5 2.2 %fusion.14 = f32[128,1536]{1,0:T(8,128)S(1)} fusion(bf16[1,768,1536]{2,1,0:T(8,128)(2,1)} %param.11, f32[16,8,768]{2,1,0:T(8,128)S(1)} %constant_dynamic-update-slice_fusion, f32[768]{0:T(1024)S(1)} %reduce.49, f32[16,8]{1,0:T(8,128)S(1)} %fusion.88, f32[16,8]{1,0:T(8,128)S(1)} %broadcast_multiply_fusion.513), kind=kOutput, calls=%fused_computation.16 | convolution fusion | flops 302383104 | bytes 3543040 | tf_op jit(solution)/shard_map/jvp()/dot_general | solution.py:44
  6.7 0.9 %copy-done.4 = f32[128,1536]{1,0:T(8,128)} copy-done((f32[128,1536]{1,0:T(8,128)}, f32[128,1536]{1,0:T(8,128)S(1)}, u32[]{:S(2)}) %copy-start.4) | copy-done | bytes 786456
  7.6 0.6 fusion.16
  8.1 3.1 %collective-permute-start = (bf16[16,8,768]{2,1,0:T(8,128)(2,1)S(1)}, bf16[16,8,768]{2,1,0:T(8,128)(2,1)}, u32[]{:S(2)}, u32[]{:S(2)}) collective-permute-start(bf16[16,8,768]{2,1,0:T(8,128)(2,1)S(1)} %fusion.16), channel_id=1, source_target_pairs={{0,1},{1,0},{2,3},{3,2},{4,5},{5,4},{6,7},{7,6},{8,9},{9,8},{10,11... | collective-permute-start | bytes 589832 | tf_op jit(solution)/shard_map/ppermute | solution.py:11
  11.2 0.1 fusion.77
  11.3 0.1 fusion.78
  11.4 1.5 %collective-permute-start.3 = (bf16[8,1024]{1,0:T(8,128)(2,1)S(1)}, bf16[8,1024]{1,0:T(8,128)(2,1)}, u32[]{:S(2)}, u32[]{:S(2)}) collective-permute-start(bf16[8,1024]{1,0:T(8,128)(2,1)S(1)} %fusion.78), channel_id=1, source_target_pairs={{0,4},{4,0},{8,12},{12,8},{16,20},{20,16},{24,28},{28,24},{1,5},{5... | collective-permute-start | bytes 49160 | tf_op jit(solution)/shard_map/ppermute | solution.py:11
  12.9 2.3 %collective-permute-done.3 = bf16[8,1024]{1,0:T(8,128)(2,1)} collective-permute-done((bf16[8,1024]{1,0:T(8,128)(2,1)S(1)}, bf16[8,1024]{1,0:T(8,128)(2,1)}, u32[]{:S(2)}, u32[]{:S(2)}) %collective-permute-start.3) | collective-permute-done | bytes 16416 | tf_op jit(solution)/shard_map/ppermute | solution.py:11
  15.3 0.7 %pad_maximum_fusion.2 = bf16[16,1024]{1,0:T(8,128)(2,1)S(1)} fusion(bf16[8,1024]{1,0:T(8,128)(2,1)} %collective-permute-done.3, bf16[8,1024]{1,0:T(8,128)(2,1)S(1)} %fusion.78), kind=kLoop, calls=%fused_computation.134 | loop fusion | flops 65536 | bytes 65536 | tf_op jit(solution)/shard_map/concatenate | solution.py:87
  16.0 1.6 %collective-permute-start.4 = (bf16[16,1024]{1,0:T(8,128)(2,1)S(1)}, bf16[16,1024]{1,0:T(8,128)(2,1)S(1)}, u32[]{:S(2)}, u32[]{:S(2)}) collective-permute-start(bf16[16,1024]{1,0:T(8,128)(2,1)S(1)} %pad_maximum_fusion.2), channel_id=1, source_target_pairs={{0,8},{4,12},{8,0},{12,4},{16,24},{20,28},{24,16},{28,20},{1,9},{5... | collective-permute-start | bytes 98312 | tf_op jit(solution)/shard_map/ppermute | solution.py:11
  17.6 1.0 %add_convert_fusion.4 = bf16[16,8,768]{2,1,0:T(8,128)(2,1)S(1)} fusion(bf16[16,8,768]{2,1,0:T(8,128)(2,1)} %collective-permute-done, bf16[16,8,768]{2,1,0:T(8,128)(2,1)S(1)} %fusion.16, f32[8,4,4,768]{3,0,2,1:T(8,128)S(1)} %copy.9), kind=kLoop, calls=%fused_computation.69 | loop fusion | flops 688128 | bytes 983040 | tf_op jit(solution)/shard_map/convert_element_type | solution.py:107
  18.6 0.1 collective-permute-start.1
  18.7 0.6 fusion.94
  19.2 0.7 collective-permute-done.4
  19.9 1.4 %pad_maximum_fusion.1 = bf16[32,1024]{1,0:T(8,128)(2,1)} fusion(bf16[16,1024]{1,0:T(8,128)(2,1)S(1)} %collective-permute-done.4, bf16[8,1024]{1,0:T(8,128)(2,1)} %collective-permute-done.3, bf16[8,1024]{1,0:T(8,128)(2,1)S(1)} %fusion.78), kind=kLoop, calls=%fused_computation.127 | loop fusion | flops 196608 | bytes 131072 | tf_op jit(solution)/shard_map/concatenate | solution.py:87
  21.3 2.6 %collective-permute-start.5 = (bf16[32,1024]{1,0:T(8,128)(2,1)}, bf16[32,1024]{1,0:T(8,128)(2,1)}, u32[]{:S(2)}, u32[]{:S(2)}) collective-permute-start(bf16[32,1024]{1,0:T(8,128)(2,1)} %pad_maximum_fusion.1), channel_id=1, source_target_pairs={{0,16},{4,20},{8,24},{12,28},{16,0},{20,4},{24,8},{28,12},{1,17},{... | collective-permute-start | bytes 196616 | tf_op jit(solution)/shard_map/ppermute | solution.py:11
  23.9 0.7 %constant_dynamic-update-slice_fusion.31 = f32[16,8,768]{2,1,0:T(8,128)S(1)} fusion(f32[768]{0:T(1024)} %copy-done.14, f32[768]{0:T(1024)S(1)} %get-tuple-element.39, f32[768]{0:T(1024)S(1)} %get-tuple-element.40, f32[768]{0:T(1024)S(1)} %get-tuple-element.41, f32[768]{0:T(1024)S(1)} %get-tuple-element.42, f32[768]{0:T(1024)S(1)} %get-tuple-element.44, ...), kind=kLoop, calls=%fused_computation.126 | loop fusion | flops 190463 | bytes 466944
  25.6 0.7 reduce_sum.153
  26.3 0.7 broadcast_multiply_fusion.512
  27.0 0.2 multiply_reduce_fusion.2
  27.2 2.2 %fusion.12 = f32[128,1536]{1,0:T(8,128)S(1)} fusion(bf16[1,768,1536]{2,1,0:T(8,128)(2,1)} %param.11, f32[16,8,768]{2,1,0:T(8,128)S(1)} %constant_dynamic-update-slice_fusion.16, f32[16,8]{1,0:T(8,128)S(1)} %fusion.89, f32[16,8]{1,0:T(8,128)S(1)} %broadcast_multiply_fusion.512, f32[768]{0:T(1024)S(1)} %reduce.49), kind=kOutput, calls=%fused_computation.14 | convolution fusion | flops 302383104 | bytes 3543040 | tf_op jit(solution)/shard_map/jvp()/dot_general | solution.py:44
  29.4 0.6 fusion.19
  30.0 0.6 collective-permute-start.2
  30.6 1.0 %fusion.90 = f32[8,1024]{1,0:T(8,128)S(1)} fusion(s32[64]{0:T(128)S(1)} %copy-done.27, s32[8]{0:T(128)S(1)} %copy-done.26, bf16[32,1024]{1,0:T(8,128)(2,1)} %collective-permute-done.5, bf16[16,1024]{1,0:T(8,128)(2,1)S(1)} %copy-done.24, bf16[8,1024]{1,0:T(8,128)(2,1)} %collective-permute-done.3, bf16[8,1024]{1,0:T(8,128)(2,1)S(1)} %fusion.78), kind=kOutput, calls=%fused_computation.676 | convolution fusion | flops 1573376 | bytes 164128 | tf_op jit(solution)/shard_map/dot_general | solution.py:128
  31.7 4.8 %collective-permute-done.2 = bf16[16,8,768]{2,1,0:T(8,128)(2,1)S(1)} collective-permute-done((bf16[16,8,768]{2,1,0:T(8,128)(2,1)S(1)}, bf16[16,8,768]{2,1,0:T(8,128)(2,1)S(1)}, u32[]{:S(2)}, u32[]{:S(2)}) %collective-permute-start.2) | collective-permute-done | bytes 196640 | tf_op jit(solution)/shard_map/ppermute | solution.py:11
  36.5 0.1 convert_reduce_fusion
  36.6 0.1 multiply_reduce_fusion.8
  36.7 0.2 multiply_reduce_fusion.7
  36.9 0.5 multiply_reduce_fusion.5
  37.4 1.2 %convert_reduce_fusion.1 = (f32[8]{0:T(128)S(1)}, bf16[8,64]{1,0:T(8,128)(2,1)S(1)}) fusion(bf16[32,1024]{1,0:T(8,128)(2,1)} %collective-permute-done.5, bf16[16,1024]{1,0:T(8,128)(2,1)S(1)} %copy-done.24, bf16[8,1024]{1,0:T(8,128)(2,1)} %collective-permute-done.3, bf16[8,1024]{1,0:T(8,128)(2,1)S(1)} %fusion.78, f32[8,1024]{1,0:T(8,128)S(1)} %get-tuple-element.842, ...), kind=kOutput, calls=%fused_computation.673 | convolution fusion | flops 1591288 | bytes 164928 | tf_op jit(solution)/shard_map/ie,je->ij/dot_general | solution.py:120
  38.5 1.1 %multiply_reduce_fusion.4 = (f32[8]{0:T(128)S(1)}, f32[8,1024]{1,0:T(8,128)S(1)}) fusion(f32[8,1024]{1,0:T(8,128)S(1)} %get-tuple-element.842, f32[8,1024]{1,0:T(8,128)S(1)} %fusion.90, f32[8]{0:T(128)S(1)} %get-tuple-element.843, bf16[8,64]{1,0:T(8,128)(2,1)S(1)} %get-tuple-element.844, bf16[32,1024]{1,0:T(8,128)(2,1)} %collective-permute-done.5, ...), kind=kOutput, calls=%fused_computation.136 | convolution fusion | flops 1613816 | bytes 230464 | tf_op jit(solution)/shard_map/dot_general | solution.py:125
  39.6 0.6 multiply_reduce_fusion.6
  40.3 0.2 fusion.108
  40.5 0.1 add_multiply_fusion
  40.6 1.1 %fusion.49 = bf16[128,1536]{1,0:T(8,128)(2,1)S(1)} fusion(f32[128,1536]{1,0:T(8,128)S(1)} %fusion.12, bf16[1,1536,768]{2,1,0:T(8,128)(2,1)S(1)} %copy-done, f32[8,768]{1,0:T(8,128)S(1)} %add_multiply_fusion), kind=kOutput, calls=%fused_computation.46 | convolution fusion | flops 306118656 | bytes 3563520 | tf_op jit(solution)/shard_map/transpose(jvp())/dot_general | solution.py:49
  41.7 0.6 copy-done.1
  42.3 0.9 %fusion.31 = bf16[16,8,768]{2,1,0:T(8,128)(2,1)S(1)} fusion(bf16[128,1536]{1,0:T(8,128)(2,1)S(1)} %fusion.49, bf16[1,768,1536]{2,1,0:T(8,128)(2,1)S(1)} %copy-done.1), kind=kOutput, calls=%fused_computation.23 | convolution fusion | flops 301989888 | bytes 2949120 | tf_op jit(solution)/shard_map/transpose(jvp())/dot_general | solution.py:44
  43.1 0.6 collective-permute-start.6
  43.7 5.2 %collective-permute-done.6 = bf16[16,8,768]{2,1,0:T(8,128)(2,1)S(1)} collective-permute-done((bf16[16,8,768]{2,1,0:T(8,128)(2,1)S(1)}, bf16[16,8,768]{2,1,0:T(8,128)(2,1)S(1)}, u32[]{:S(2)}, u32[]{:S(2)}) %collective-permute-start.6) | collective-permute-done | bytes 196640 | tf_op jit(solution)/shard_map/ppermute | solution.py:11
  48.9 0.2 multiply_reduce_fusion.1
  49.1 0.3 fusion.75
  49.4 0.2 broadcast_add_fusion.1
  50.0 0.4 copy-done.10
  50.7 3.7 %fusion.107 = (bf16[16,8,768]{2,1,0:T(8,128)(2,1)S(1)}, f32[16,8,768]{2,1,0:T(8,128)}) fusion(f32[1,8,768]{2,1,0:T(8,128)S(1)} %get-tuple-element.337, f32[1,8,768]{2,1,0:T(8,128)S(1)} %get-tuple-element.562, f32[1,8,768]{2,1,0:T(8,128)S(1)} %get-tuple-element.576, f32[1,8,768]{2,1,0:T(8,128)S(1)} %get-tuple-element.584, ...), kind=kLoop, calls=%fused_computation.755 | loop fusion | flops 25264128 | bytes 7274496 | tf_op jit(solution)/shard_map/convert_element_type | solution.py:176
  54.4 1.4 %collective-permute-done.7 = bf16[16,8,768]{2,1,0:T(8,128)(2,1)S(1)} collective-permute-done((bf16[16,8,768]{2,1,0:T(8,128)(2,1)S(1)}, bf16[16,8,768]{2,1,0:T(8,128)(2,1)S(1)}, u32[]{:S(2)}, u32[]{:S(2)}) %collective-permute-start.7) | collective-permute-done | bytes 196640 | tf_op jit(solution)/shard_map/ppermute | solution.py:11
  55.9 1.1 %fusion.43 = bf16[128,1536]{1,0:T(8,128)(2,1)S(1)} fusion(f32[128,1536]{1,0:T(8,128)S(1)} %copy-done.5, bf16[1,1536,768]{2,1,0:T(8,128)(2,1)S(1)} %copy-done, bf16[16,8,768]{2,1,0:T(8,128)(2,1)S(1)} %collective-permute-done.7), kind=kOutput, calls=%fused_computation.40 | convolution fusion | flops 306315264 | bytes 3735552 | tf_op jit(solution)/shard_map/transpose(jvp())/dot_general | solution.py:49
  57.0 0.9 %fusion.28 = bf16[16,8,768]{2,1,0:T(8,128)(2,1)S(1)} fusion(bf16[128,1536]{1,0:T(8,128)(2,1)S(1)} %fusion.43, bf16[1,768,1536]{2,1,0:T(8,128)(2,1)S(1)} %copy-done.1), kind=kOutput, calls=%fused_computation.22 | convolution fusion | flops 301989888 | bytes 2949120 | tf_op jit(solution)/shard_map/transpose(jvp())/dot_general | solution.py:44
  57.8 0.6 collective-permute-start.8
  58.4 6.4 %collective-permute-done.8 = bf16[16,8,768]{2,1,0:T(8,128)(2,1)S(1)} collective-permute-done((bf16[16,8,768]{2,1,0:T(8,128)(2,1)S(1)}, bf16[16,8,768]{2,1,0:T(8,128)(2,1)S(1)}, u32[]{:S(2)}, u32[]{:S(2)}) %collective-permute-start.8) | collective-permute-done | bytes 196640 | tf_op jit(solution)/shard_map/ppermute | solution.py:11
  64.9 0.2 multiply_reduce_fusion
  65.1 0.7 %multiply_multiply_fusion.4 = f32[16,8]{1,0:T(8,128)S(1)} fusion(f32[16,8]{1,0:T(8,128)S(1)} %multiply_reduce_fusion, f32[16,8]{1,0:T(8,128)} %copy-done.21), kind=kLoop, calls=%fused_computation.666 | loop fusion | flops 768 | bytes 1536 | tf_op jit(solution)/shard_map/transpose(jvp())/div | solution.py:34
  65.8 0.2 fusion.76
  66.0 0.2 broadcast_add_fusion
  67.0 0.7 copy-done.3
  67.7 1.5 %add_select_fusion = f32[16,8,768]{2,1,0:T(8,128)S(1)} fusion(f32[16,8,768]{2,1,0:T(8,128)S(1)} %copy-done.3, f32[1,8,768]{2,1,0:T(8,128)S(1)} %get-tuple-element.79, f32[1,8,768]{2,1,0:T(8,128)S(1)} %get-tuple-element.657, f32[1,8,768]{2,1,0:T(8,128)S(1)} %get-tuple-element.671, f32[1,8,768]{2,1,0:T(8,128)S(1)} %get-tuple-element.679, ...), kind=kLoop, calls=%fused_computation.54 | loop fusion | flops 25362432 | bytes 7643137 | tf_op jit(solution)/shard_map/jit(_where)/select_n | solution.py:178
  69.1 0.9 %copy.10 = f32[1,8,4,4,768]{4,3,2,1,0:T(4,128)} copy(f32[1,8,4,4,768]{4,1,3,2,0:T(8,128)S(1)} %bitcast.88) | data formatting | bytes 786432 | tf_op jit(solution)/shard_map/broadcast_in_dim;reshape | solution.py:179
  (137 shorter events, 3.4 us)
Async XLA Ops:
  0.0 7.6 %copy-start = (bf16[1,1536,768]{2,1,0:T(8,128)(2,1)S(1)}, bf16[1,1536,768]{2,1,0:T(8,128)(2,1)}, u32[]{:S(2)}) copy-start(bf16[1,1536,768]{2,1,0:T(8,128)(2,1)} %param.12) | copy-start | bytes 7077892
  1.4 1.7 %copy-start.11 = (f32[768]{0:T(1024)}, f32[768]{0:T(1024)S(1)}, u32[]{:S(2)}) copy-start(f32[768]{0:T(1024)S(1)} %get-tuple-element.26) | copy-start | bytes 9220
  1.4 2.2 %copy-start.14 = (f32[768]{0:T(1024)}, f32[768]{0:T(1024)S(1)}, u32[]{:S(2)}) copy-start(f32[768]{0:T(1024)S(1)} %get-tuple-element.38) | copy-start | bytes 9220
  1.5 1.7 %copy-start.8 = (f32[768]{0:T(1024)}, f32[768]{0:T(1024)S(1)}, u32[]{:S(2)}) copy-start(f32[768]{0:T(1024)S(1)} %get-tuple-element.8) | copy-start | bytes 9220
  1.6 1.9 %copy-start.17 = (f32[768]{0:T(1024)}, f32[768]{0:T(1024)S(1)}, u32[]{:S(2)}) copy-start(f32[768]{0:T(1024)S(1)} %get-tuple-element.5) | copy-start | bytes 9220
  3.0 0.8 %copy-start.25 = (f32[1,768]{1,0:T(1,128)S(1)}, f32[1,768]{1,0:T(1,128)}, u32[]{:S(2)}) copy-start(f32[1,768]{1,0:T(1,128)} %param.10) | copy-start | bytes 9220
  3.8 0.6 copy-start.21
  3.9 0.6 copy-start.6
  6.7 0.9 %copy-start.4 = (f32[128,1536]{1,0:T(8,128)}, f32[128,1536]{1,0:T(8,128)S(1)}, u32[]{:S(2)}) copy-start(f32[128,1536]{1,0:T(8,128)S(1)} %fusion.14) | copy-start | bytes 2359300
  7.6 3.7 %copy-start.22 = (bf16[8,1024]{1,0:T(8,128)(2,1)S(1)}, bf16[8,1024]{1,0:T(8,128)(2,1)}, u32[]{:S(2)}) copy-start(bf16[8,1024]{1,0:T(8,128)(2,1)} %param.14) | copy-start | bytes 49156
  8.1 9.4 %collective-permute-start = (bf16[16,8,768]{2,1,0:T(8,128)(2,1)S(1)}, bf16[16,8,768]{2,1,0:T(8,128)(2,1)}, u32[]{:S(2)}, u32[]{:S(2)}) collective-permute-start(bf16[16,8,768]{2,1,0:T(8,128)(2,1)S(1)} %fusion.16), channel_id=1, source_target_pairs={{0,1},{1,0},{2,3},{3,2},{4,5},{5,4},{6,7},{7,6},{8,9},{9,8},{10,11... | collective-permute-start | bytes 589832 | tf_op jit(solution)/shard_map/ppermute | solution.py:11
  11.4 3.9 %collective-permute-start.3 = (bf16[8,1024]{1,0:T(8,128)(2,1)S(1)}, bf16[8,1024]{1,0:T(8,128)(2,1)}, u32[]{:S(2)}, u32[]{:S(2)}) collective-permute-start(bf16[8,1024]{1,0:T(8,128)(2,1)S(1)} %fusion.78), channel_id=1, source_target_pairs={{0,4},{4,0},{8,12},{12,8},{16,20},{20,16},{24,28},{28,24},{1,5},{5... | collective-permute-start | bytes 49160 | tf_op jit(solution)/shard_map/ppermute | solution.py:11
  12.9 11.8 %copy-start.12 = (f32[768]{0:T(1024)S(1)}, f32[768]{0:T(1024)}, u32[]{:S(2)}) copy-start(f32[768]{0:T(1024)} %copy-done.11) | copy-start | bytes 9220
  16.0 3.9 %collective-permute-start.4 = (bf16[16,1024]{1,0:T(8,128)(2,1)S(1)}, bf16[16,1024]{1,0:T(8,128)(2,1)S(1)}, u32[]{:S(2)}, u32[]{:S(2)}) collective-permute-start(bf16[16,1024]{1,0:T(8,128)(2,1)S(1)} %pad_maximum_fusion.2), channel_id=1, source_target_pairs={{0,8},{4,12},{8,0},{12,4},{16,24},{20,28},{24,16},{28,20},{1,9},{5... | collective-permute-start | bytes 98312 | tf_op jit(solution)/shard_map/ppermute | solution.py:11
  18.6 5.3 %collective-permute-start.1 = (bf16[16,8,768]{2,1,0:T(8,128)(2,1)S(1)}, bf16[16,8,768]{2,1,0:T(8,128)(2,1)S(1)}, u32[]{:S(2)}, u32[]{:S(2)}) collective-permute-start(bf16[16,8,768]{2,1,0:T(8,128)(2,1)S(1)} %add_convert_fusion.4), channel_id=1, source_target_pairs={{0,2},{2,0},{1,3},{3,1},{4,6},{6,4},{5,7},{7,5},{8,10},{10,8},{9,1... | collective-permute-start | bytes 589832 | tf_op jit(solution)/shard_map/ppermute | solution.py:11
  19.9 5.2 %copy-start.23 = (bf16[16,1024]{1,0:T(8,128)(2,1)}, bf16[16,1024]{1,0:T(8,128)(2,1)S(1)}, u32[]{:S(2)}) copy-start(bf16[16,1024]{1,0:T(8,128)(2,1)S(1)} %collective-permute-done.4) | copy-start | bytes 98308
  21.3 9.4 %collective-permute-start.5 = (bf16[32,1024]{1,0:T(8,128)(2,1)}, bf16[32,1024]{1,0:T(8,128)(2,1)}, u32[]{:S(2)}, u32[]{:S(2)}) collective-permute-start(bf16[32,1024]{1,0:T(8,128)(2,1)} %pad_maximum_fusion.1), channel_id=1, source_target_pairs={{0,16},{4,20},{8,24},{12,28},{16,0},{20,4},{24,8},{28,12},{1,17},{... | collective-permute-start | bytes 196616 | tf_op jit(solution)/shard_map/ppermute | solution.py:11
  24.7 0.7 copy-start.9
  24.9 0.7 copy-start.18
  29.4 1.2 %copy-start.24 = (bf16[16,1024]{1,0:T(8,128)(2,1)S(1)}, bf16[16,1024]{1,0:T(8,128)(2,1)}, u32[]{:S(2)}) copy-start(bf16[16,1024]{1,0:T(8,128)(2,1)} %copy-done.23) | copy-start | bytes 98308
  29.4 1.2 %copy-start.26 = (s32[8]{0:T(128)S(1)}, s32[8]{0:T(128)}, u32[]{:S(2)}) copy-start(s32[8]{0:T(128)} %param.15) | copy-start | bytes 100
  29.4 1.2 %copy-start.27 = (s32[64]{0:T(128)S(1)}, s32[64]{0:T(128)}, u32[]{:S(2)}) copy-start(s32[64]{0:T(128)} %fusion.94) | copy-start | bytes 772
  29.4 7.5 %copy-start.2 = (bf16[768,1024]{1,0:T(8,128)(2,1)S(1)}, bf16[768,1024]{1,0:T(8,128)(2,1)}, u32[]{:S(2)}) copy-start(bf16[768,1024]{1,0:T(8,128)(2,1)} %param.13) | copy-start | bytes 4718596
  30.0 6.4 %collective-permute-start.2 = (bf16[16,8,768]{2,1,0:T(8,128)(2,1)S(1)}, bf16[16,8,768]{2,1,0:T(8,128)(2,1)S(1)}, u32[]{:S(2)}, u32[]{:S(2)}) collective-permute-start(bf16[16,8,768]{2,1,0:T(8,128)(2,1)S(1)} %fusion.19), channel_id=1, source_target_pairs={{0,1},{1,0},{2,3},{3,2},{4,5},{5,4},{6,7},{7,6},{8,9},{9,8},{10,11... | collective-permute-start | bytes 589832 | tf_op jit(solution)/shard_map/ppermute | solution.py:11
  40.6 1.7 %copy-start.1 = (bf16[1,768,1536]{2,1,0:T(8,128)(2,1)S(1)}, bf16[1,768,1536]{2,1,0:T(8,128)(2,1)}, u32[]{:S(2)}) copy-start(bf16[1,768,1536]{2,1,0:T(8,128)(2,1)} %param.11) | copy-start | bytes 7077892
  42.3 7.3 %copy-start.19 = (f32[768]{0:T(1024)S(1)}, f32[768]{0:T(1024)}, u32[]{:S(2)}) copy-start(f32[768]{0:T(1024)} %copy-done.17) | copy-start | bytes 9220
  43.1 5.7 %collective-permute-start.6 = (bf16[16,8,768]{2,1,0:T(8,128)(2,1)S(1)}, bf16[16,8,768]{2,1,0:T(8,128)(2,1)S(1)}, u32[]{:S(2)}, u32[]{:S(2)}) collective-permute-start(bf16[16,8,768]{2,1,0:T(8,128)(2,1)S(1)} %fusion.31), channel_id=1, source_target_pairs={{0,1},{1,0},{2,3},{3,2},{4,5},{5,4},{6,7},{7,6},{8,9},{9,8},{10,11... | collective-permute-start | bytes 589832 | tf_op jit(solution)/shard_map/ppermute | solution.py:11
  49.1 0.7 copy-start.15
  49.1 0.7 copy-start.13
  49.7 0.7 copy-start.10
  50.7 5.2 %copy-start.5 = (f32[128,1536]{1,0:T(8,128)S(1)}, f32[128,1536]{1,0:T(8,128)}, u32[]{:S(2)}) copy-start(f32[128,1536]{1,0:T(8,128)} %copy-done.4) | copy-start | bytes 2359300
  54.4 1.4 %collective-permute-start.7 = (bf16[16,8,768]{2,1,0:T(8,128)(2,1)S(1)}, bf16[16,8,768]{2,1,0:T(8,128)(2,1)S(1)}, u32[]{:S(2)}, u32[]{:S(2)}) collective-permute-start(bf16[16,8,768]{2,1,0:T(8,128)(2,1)S(1)} %get-tuple-element.54), channel_id=1, source_target_pairs={{0,2},{2,0},{1,3},{3,1},{4,6},{6,4},{5,7},{7,5},{8,10},{10,8},{9,1... | collective-permute-start | bytes 589832 | tf_op jit(solution)/shard_map/ppermute | solution.py:11
  57.0 8.8 %copy-start.7 = (f32[16,8]{1,0:T(8,128)S(1)}, f32[16,8]{1,0:T(8,128)}, u32[]{:S(2)}) copy-start(f32[16,8]{1,0:T(8,128)} %copy-done.6) | copy-start | bytes 1540
  57.8 7.0 %collective-permute-start.8 = (bf16[16,8,768]{2,1,0:T(8,128)(2,1)S(1)}, bf16[16,8,768]{2,1,0:T(8,128)(2,1)S(1)}, u32[]{:S(2)}, u32[]{:S(2)}) collective-permute-start(bf16[16,8,768]{2,1,0:T(8,128)(2,1)S(1)} %fusion.28), channel_id=1, source_target_pairs={{0,1},{1,0},{2,3},{3,2},{4,5},{5,4},{6,7},{7,6},{8,9},{9,8},{10,11... | collective-permute-start | bytes 589832 | tf_op jit(solution)/shard_map/ppermute | solution.py:11
  58.4 7.8 %copy-start.20 = (f32[768]{0:T(1024)S(1)}, f32[768]{0:T(1024)}, u32[]{:S(2)}) copy-start(f32[768]{0:T(1024)} %copy-done.17) | copy-start | bytes 9220
  65.0 1.3 %copy-start.16 = (f32[768]{0:T(1024)S(1)}, f32[768]{0:T(1024)}, u32[]{:S(2)}) copy-start(f32[768]{0:T(1024)} %copy-done.14) | copy-start | bytes 9220
  66.7 1.0 %copy-start.3 = (f32[16,8,768]{2,1,0:T(8,128)S(1)}, f32[16,8,768]{2,1,0:T(8,128)}, u32[]{:S(2)}) copy-start(f32[16,8,768]{2,1,0:T(8,128)} %get-tuple-element.55) | copy-start | bytes 1179652

commit v6 on v5

--- a/solution.py
+++ b/solution.py
@@ -50,12 +50,14 @@
 
 
 def mlp_part(normed, expand, project_out):
-    pre, expand_back = jax.vjp(lambda inner: expand_part(inner, expand), normed)
+    low = lax.optimization_barrier(normed.astype(jnp.bfloat16))
+    pre, expand_back = jax.vjp(lambda inner: expand_part(inner, expand), low)
     branch, project_back = jax.vjp(lambda inner: project_part(inner, project_out, normed.shape), pre)
 
     def mlp_back(cotangent):
         (pre_grad,) = project_back(cotangent)
-        return expand_back(lax.optimization_barrier(pre_grad))
+        (low_grad,) = expand_back(lax.optimization_barrier(pre_grad))
+        return (low_grad.astype(jnp.float32),)
 
     return branch, mlp_back
 
@@ -99,9 +101,21 @@
     return swapped(values, "phase", 0)
 
 
+def front_split(widened, kernel, gain_vec, side):
+    conv = lax.optimization_barrier(depthwise(widened, kernel, side))
+    flipped = kernel[::-1, ::-1]
+    normed, norm_back = jax.vjp(lambda inner: normalize_last(inner) * gain_vec, conv)
+
+    def front_back(cotangent):
+        (conv_grad,) = norm_back(cotangent)
+        return (depthwise(lax.optimization_barrier(conv_grad), flipped, side),)
+
+    return normed, front_back
+
+
 def section_forward(inputs_low, kernel, gain_vec, expand, project_out, side):
     widened = inputs_low.astype(jnp.float32)
-    normed, front_back = jax.vjp(lambda inner: front_part(inner, kernel, gain_vec, side), widened)
+    normed, front_back = front_split(widened, kernel, gain_vec, side)
     partial_out, mlp_back = mlp_part(normed, expand, project_out)
     summed = hidden_total(partial_out)
     return ((widened + summed).astype(jnp.bfloat16), front_back, mlp_back)

time: 70.8 us -> 65.6 us (0.927)
  other arithmetic: 17.2 us -> 12.3 us
    convert_element_type x1, other arithmetic: 3.73 us -> 0.03 us  [on_device(): returned = hand_over(grad_first_in.astype(jnp.bfloat16))]
    unnamed x31 -> x61, other arithmetic: 2.35 us -> 4.02 us
    select_n x1, other arithmetic: 1.45 us -> 0.05 us  [on_device(): chosen = jnp.where(phase_pick == 0, grad_images, grad_first_in)]
    mul x34 -> x0, other arithmetic: 1.14 us -> none  [depthwise(): term = kernel[d_row + margin, d_col + margin][None, :] * values[i]]
    unnamed x57 -> x61, local copies, waits for them, and re-layouts: 4.42 us -> 4.44 us
  transfers between devices with their start and end apart: 9 -> 9, of which waited for: 6 -> 6; matrix products, arithmetic and copies ran while one was open for 16% -> 17% of each run, Pallas kernels for 0% -> 0%
where the time goes in v6:
time: 65.6 us; the launch traced here: 64.9 us
  waiting for transfers between devices  20.9 us (32%)
  matrix products  13.7 us (21%)
  other arithmetic  12.3 us (19%)
  starting transfers between devices  10.6 us (16%)
  local copies, waits for them, and re-layouts  6.76 us (10%)
    ppermute x9, waiting for transfers between devices, swapped(): lax.ppermute(value, axis, [(i, i ^ 1 << stride) for i in range(lax.axis_s...  20.9 us
    ppermute x9, starting transfers between devices, swapped(): lax.ppermute(value, axis, [(i, i ^ 1 << stride) for i in range(lax.axis_s...  10.6 us
    dot_general x4, matrix products, expand_part(): return jnp.dot(flattened, expand, preferred_element_type=jnp.float32)  6.02 us
    unnamed x61, local copies, waits for them, and re-layouts  4.44 us
    unnamed x61, other arithmetic  4.02 us
    dot_general x4, matrix products, project_part(): jnp.dot(hidden, project_out, preferred_element_type=jnp.float32)  3.31 us
    concatenate x2, other arithmetic, gather_rows(): block = jnp.concatenate([block, swapped(block, axis, stride)], axis=0)  2.08 us
    reduce_sum x6, other arithmetic, normalize_last(): centred = values - jnp.mean(values, axis=-1, keepdims=True)  1.61 us
  transfers between devices with their start and end apart: 9, of which 6 were waited for; matrix products, arithmetic and copies ran while one was open for 17% of the time, Pallas kernels for 0%

profile of v6, /device:TPU:0, one launch (start us, length us, event | category | flops | bytes accessed | tf_op | source)
XLA Modules:
  0.0 64.9 jit_solution(1467447936018741859)
XLA Ops:
  0.0 1.1 %copy.13 = f32[1,7,7,768]{3,2,0,1:T(8,128)S(1)} copy(f32[1,7,7,768]{3,0,2,1:T(1,128)} %param.9) | data formatting | bytes 301056
  1.1 0.1 slice_reduce_fusion.47
  1.2 0.2 slice_reduce_fusion.19
  1.4 0.2 slice_reduce_fusion.5
  1.6 1.0 %copy.9 = f32[8,4,4,768]{3,0,2,1:T(8,128)S(1)} copy(bf16[8,4,4,768]{3,2,1,0:T(4,128)(2,1)} %param.8) | data formatting | bytes 589824 | tf_op jit(solution)/shard_map/convert_element_type | solution.py:117
  3.5 0.1 reduce_sum.148
  3.6 0.2 multiply_reduce_fusion.3
  3.9 0.1 multiply_convert_fusion.5
  4.0 0.4 copy-done.22
  4.5 2.1 %fusion.14 = f32[128,1536]{1,0:T(8,128)S(1)} fusion(bf16[1,768,1536]{2,1,0:T(8,128)(2,1)} %param.11, bf16[16,8,768]{2,1,0:T(8,128)(2,1)S(1)} %multiply_convert_fusion.5), kind=kOutput, calls=%fused_computation.16 | convolution fusion | flops 301989888 | bytes 3342336 | tf_op jit(solution)/shard_map/jvp()/dot_general | solution.py:44
  6.6 0.9 %copy-done.5 = f32[128,1536]{1,0:T(8,128)} copy-done((f32[128,1536]{1,0:T(8,128)}, f32[128,1536]{1,0:T(8,128)S(1)}, u32[]{:S(2)}) %copy-start.5) | copy-done | bytes 786456
  7.5 0.6 fusion.16
  8.1 3.1 %collective-permute-start = (bf16[16,8,768]{2,1,0:T(8,128)(2,1)S(1)}, bf16[16,8,768]{2,1,0:T(8,128)(2,1)}, u32[]{:S(2)}, u32[]{:S(2)}) collective-permute-start(bf16[16,8,768]{2,1,0:T(8,128)(2,1)S(1)} %fusion.16), channel_id=1, source_target_pairs={{0,1},{1,0},{2,3},{3,2},{4,5},{5,4},{6,7},{7,6},{8,9},{9,8},{10,11... | collective-permute-start | bytes 589832 | tf_op jit(solution)/shard_map/ppermute | solution.py:11
  11.1 0.1 fusion.69
  11.3 0.1 fusion.70
  11.3 1.5 %collective-permute-start.3 = (bf16[8,1024]{1,0:T(8,128)(2,1)S(1)}, bf16[8,1024]{1,0:T(8,128)(2,1)}, u32[]{:S(2)}, u32[]{:S(2)}) collective-permute-start(bf16[8,1024]{1,0:T(8,128)(2,1)S(1)} %fusion.70), channel_id=1, source_target_pairs={{0,4},{4,0},{8,12},{12,8},{16,20},{20,16},{24,28},{28,24},{1,5},{5... | collective-permute-start | bytes 49160 | tf_op jit(solution)/shard_map/ppermute | solution.py:11
  12.8 2.4 %collective-permute-done.3 = bf16[8,1024]{1,0:T(8,128)(2,1)} collective-permute-done((bf16[8,1024]{1,0:T(8,128)(2,1)S(1)}, bf16[8,1024]{1,0:T(8,128)(2,1)}, u32[]{:S(2)}, u32[]{:S(2)}) %collective-permute-start.3) | collective-permute-done | bytes 16416 | tf_op jit(solution)/shard_map/ppermute | solution.py:11
  15.2 0.7 %pad_maximum_fusion.2 = bf16[16,1024]{1,0:T(8,128)(2,1)S(1)} fusion(bf16[8,1024]{1,0:T(8,128)(2,1)} %collective-permute-done.3, bf16[8,1024]{1,0:T(8,128)(2,1)S(1)} %fusion.70), kind=kLoop, calls=%fused_computation.158 | loop fusion | flops 65536 | bytes 65536 | tf_op jit(solution)/shard_map/concatenate | solution.py:89
  15.9 1.6 %collective-permute-start.4 = (bf16[16,1024]{1,0:T(8,128)(2,1)S(1)}, bf16[16,1024]{1,0:T(8,128)(2,1)S(1)}, u32[]{:S(2)}, u32[]{:S(2)}) collective-permute-start(bf16[16,1024]{1,0:T(8,128)(2,1)S(1)} %pad_maximum_fusion.2), channel_id=1, source_target_pairs={{0,8},{4,12},{8,0},{12,4},{16,24},{20,28},{24,16},{28,20},{1,9},{5... | collective-permute-start | bytes 98312 | tf_op jit(solution)/shard_map/ppermute | solution.py:11
  17.5 1.0 %add_convert_fusion.4 = bf16[16,8,768]{2,1,0:T(8,128)(2,1)S(1)} fusion(bf16[16,8,768]{2,1,0:T(8,128)(2,1)} %collective-permute-done, bf16[16,8,768]{2,1,0:T(8,128)(2,1)S(1)} %fusion.16, f32[8,4,4,768]{3,0,2,1:T(8,128)S(1)} %copy.9), kind=kLoop, calls=%fused_computation.66 | loop fusion | flops 688128 | bytes 983040 | tf_op jit(solution)/shard_map/convert_element_type | solution.py:121
  18.5 0.1 collective-permute-start.1
  18.6 0.6 fusion.86
  19.2 0.7 %collective-permute-done.4 = bf16[16,1024]{1,0:T(8,128)(2,1)S(1)} collective-permute-done((bf16[16,1024]{1,0:T(8,128)(2,1)S(1)}, bf16[16,1024]{1,0:T(8,128)(2,1)S(1)}, u32[]{:S(2)}, u32[]{:S(2)}) %collective-permute-start.4) | collective-permute-done | bytes 32800 | tf_op jit(solution)/shard_map/ppermute | solution.py:11
  19.8 1.4 %pad_maximum_fusion.1 = bf16[32,1024]{1,0:T(8,128)(2,1)} fusion(bf16[16,1024]{1,0:T(8,128)(2,1)S(1)} %collective-permute-done.4, bf16[8,1024]{1,0:T(8,128)(2,1)} %collective-permute-done.3, bf16[8,1024]{1,0:T(8,128)(2,1)S(1)} %fusion.70), kind=kLoop, calls=%fused_computation.151 | loop fusion | flops 196608 | bytes 131072 | tf_op jit(solution)/shard_map/concatenate | solution.py:89
  21.2 2.6 %collective-permute-start.5 = (bf16[32,1024]{1,0:T(8,128)(2,1)}, bf16[32,1024]{1,0:T(8,128)(2,1)}, u32[]{:S(2)}, u32[]{:S(2)}) collective-permute-start(bf16[32,1024]{1,0:T(8,128)(2,1)} %pad_maximum_fusion.1), channel_id=1, source_target_pairs={{0,16},{4,20},{8,24},{12,28},{16,0},{20,4},{24,8},{28,12},{1,17},{... | collective-permute-start | bytes 196616 | tf_op jit(solution)/shard_map/ppermute | solution.py:11
  23.8 0.7 %constant_dynamic-update-slice_fusion.31 = f32[16,8,768]{2,1,0:T(8,128)S(1)} fusion(f32[768]{0:T(1024)} %copy-done.11, f32[768]{0:T(1024)S(1)} %get-tuple-element.39, f32[768]{0:T(1024)S(1)} %get-tuple-element.40, f32[768]{0:T(1024)S(1)} %get-tuple-element.41, f32[768]{0:T(1024)S(1)} %get-tuple-element.42, f32[768]{0:T(1024)S(1)} %get-tuple-element.44, ...), kind=kLoop, calls=%fused_computation.117 | loop fusion | flops 190463 | bytes 466944
  25.5 0.7 %reduce_sum.153 = f32[16,8]{1,0:T(8,128)} reduce(f32[16,8,768]{2,1,0:T(8,128)S(1)} %constant_dynamic-update-slice_fusion.16, f32[]{:T(128)} %constant.67.clone.1), dimensions={2}, to_apply=%region_2.0 | reduce | flops 98176 | bytes 393732 | tf_op jit(solution)/shard_map/jvp()/reduce_sum | solution.py:33
  26.2 0.7 %broadcast_multiply_fusion = f32[16,8]{1,0:T(8,128)S(1)} fusion(f32[16,8]{1,0:T(8,128)} %reduce_sum.153), kind=kLoop, calls=%fused_computation.186 | loop fusion | flops 128 | bytes 1024 | tf_op jit(solution)/shard_map/jvp()/div | solution.py:33
  26.9 0.2 multiply_reduce_fusion.2
  27.1 0.1 multiply_convert_fusion.2
  27.3 2.1 %fusion.12 = f32[128,1536]{1,0:T(8,128)S(1)} fusion(bf16[1,768,1536]{2,1,0:T(8,128)(2,1)} %param.11, bf16[16,8,768]{2,1,0:T(8,128)(2,1)S(1)} %multiply_convert_fusion.2), kind=kOutput, calls=%fused_computation.14 | convolution fusion | flops 301989888 | bytes 3342336 | tf_op jit(solution)/shard_map/jvp()/dot_general | solution.py:44
  29.5 0.6 fusion.19
  30.1 0.6 collective-permute-start.2
  30.6 1.0 %fusion.82 = f32[8,1024]{1,0:T(8,128)S(1)} fusion(s32[64]{0:T(128)S(1)} %copy-done.29, s32[8]{0:T(128)S(1)} %copy-done.28, bf16[32,1024]{1,0:T(8,128)(2,1)} %collective-permute-done.5, bf16[16,1024]{1,0:T(8,128)(2,1)S(1)} %copy-done.26, bf16[8,1024]{1,0:T(8,128)(2,1)} %collective-permute-done.3, bf16[8,1024]{1,0:T(8,128)(2,1)S(1)} %fusion.70), kind=kOutput, calls=%fused_computation.188 | convolution fusion | flops 1573376 | bytes 164128 | tf_op jit(solution)/shard_map/dot_general | solution.py:142
  31.7 4.8 %collective-permute-done.2 = bf16[16,8,768]{2,1,0:T(8,128)(2,1)S(1)} collective-permute-done((bf16[16,8,768]{2,1,0:T(8,128)(2,1)S(1)}, bf16[16,8,768]{2,1,0:T(8,128)(2,1)S(1)}, u32[]{:S(2)}, u32[]{:S(2)}) %collective-permute-start.2) | collective-permute-done | bytes 196640 | tf_op jit(solution)/shard_map/ppermute | solution.py:11
  36.5 0.1 convert_reduce_fusion
  36.6 0.1 multiply_reduce_fusion.8
  36.7 0.2 multiply_reduce_fusion.7
  36.9 0.5 multiply_reduce_fusion.5
  37.4 1.2 %convert_reduce_fusion.1 = (f32[8]{0:T(128)S(1)}, bf16[8,64]{1,0:T(8,128)(2,1)S(1)}) fusion(bf16[32,1024]{1,0:T(8,128)(2,1)} %collective-permute-done.5, bf16[16,1024]{1,0:T(8,128)(2,1)S(1)} %copy-done.26, bf16[8,1024]{1,0:T(8,128)(2,1)} %collective-permute-done.3, bf16[8,1024]{1,0:T(8,128)(2,1)S(1)} %fusion.70, f32[8,1024]{1,0:T(8,128)S(1)} %get-tuple-element.59, ...), kind=kOutput, calls=%fused_computation.185 | convolution fusion | flops 1591288 | bytes 164928 | tf_op jit(solution)/shard_map/ie,je->ij/dot_general | solution.py:134
  38.5 1.1 %multiply_reduce_fusion.4 = (f32[8]{0:T(128)S(1)}, f32[8,1024]{1,0:T(8,128)S(1)}) fusion(f32[8,1024]{1,0:T(8,128)S(1)} %get-tuple-element.59, f32[8,1024]{1,0:T(8,128)S(1)} %fusion.82, f32[8]{0:T(128)S(1)} %get-tuple-element.60, bf16[8,64]{1,0:T(8,128)(2,1)S(1)} %get-tuple-element.61, bf16[32,1024]{1,0:T(8,128)(2,1)} %collective-permute-done.5, ...), kind=kOutput, calls=%fused_computation.160 | convolution fusion | flops 1613816 | bytes 230464 | tf_op jit(solution)/shard_map/dot_general | solution.py:139
  39.6 0.6 multiply_reduce_fusion.6
  40.3 0.2 fusion.99
  40.5 0.1 add_multiply_fusion
  40.6 1.1 %fusion.49 = bf16[128,1536]{1,0:T(8,128)(2,1)S(1)} fusion(f32[128,1536]{1,0:T(8,128)S(1)} %fusion.12, bf16[1,1536,768]{2,1,0:T(8,128)(2,1)S(1)} %copy-done, f32[8,768]{1,0:T(8,128)S(1)} %add_multiply_fusion), kind=kOutput, calls=%fused_computation.46 | convolution fusion | flops 306118656 | bytes 3563520 | tf_op jit(solution)/shard_map/transpose(jvp())/dot_general | solution.py:49
  41.7 0.6 copy-done.1
  42.3 0.9 %fusion.31 = bf16[16,8,768]{2,1,0:T(8,128)(2,1)S(1)} fusion(bf16[128,1536]{1,0:T(8,128)(2,1)S(1)} %fusion.49, bf16[1,768,1536]{2,1,0:T(8,128)(2,1)S(1)} %copy-done.1), kind=kOutput, calls=%fused_computation.23 | convolution fusion | flops 301989888 | bytes 2949120 | tf_op jit(solution)/shard_map/transpose(jvp())/dot_general | solution.py:44
  43.2 0.6 collective-permute-start.6
  43.7 5.2 %collective-permute-done.6 = bf16[16,8,768]{2,1,0:T(8,128)(2,1)S(1)} collective-permute-done((bf16[16,8,768]{2,1,0:T(8,128)(2,1)S(1)}, bf16[16,8,768]{2,1,0:T(8,128)(2,1)S(1)}, u32[]{:S(2)}, u32[]{:S(2)}) %collective-permute-start.6) | collective-permute-done | bytes 196640 | tf_op jit(solution)/shard_map/ppermute | solution.py:11
  48.9 0.2 multiply_reduce_fusion.1
  49.1 0.3 fusion.67
  49.4 0.2 broadcast_add_fusion.1
  50.6 0.7 %copy-done.3 = f32[16,8,768]{2,1,0:T(8,128)} copy-done((f32[16,8,768]{2,1,0:T(8,128)}, f32[16,8,768]{2,1,0:T(8,128)S(1)}, u32[]{:S(2)}) %copy-start.3) | copy-done | bytes 393240
  51.4 0.1 collective-permute-start.7
  51.4 1.4 %collective-permute-done.7 = bf16[16,8,768]{2,1,0:T(8,128)(2,1)S(1)} collective-permute-done((bf16[16,8,768]{2,1,0:T(8,128)(2,1)S(1)}, bf16[16,8,768]{2,1,0:T(8,128)(2,1)S(1)}, u32[]{:S(2)}, u32[]{:S(2)}) %collective-permute-start.7) | collective-permute-done | bytes 196640 | tf_op jit(solution)/shard_map/ppermute | solution.py:11
  52.9 1.1 %fusion.43 = bf16[128,1536]{1,0:T(8,128)(2,1)S(1)} fusion(f32[128,1536]{1,0:T(8,128)S(1)} %copy-done.6, bf16[1,1536,768]{2,1,0:T(8,128)(2,1)S(1)} %copy-done, bf16[16,8,768]{2,1,0:T(8,128)(2,1)S(1)} %collective-permute-done.7), kind=kOutput, calls=%fused_computation.40 | convolution fusion | flops 306315264 | bytes 3735552 | tf_op jit(solution)/shard_map/transpose(jvp())/dot_general | solution.py:49
  54.0 0.9 %fusion.28 = bf16[16,8,768]{2,1,0:T(8,128)(2,1)S(1)} fusion(bf16[128,1536]{1,0:T(8,128)(2,1)S(1)} %fusion.43, bf16[1,768,1536]{2,1,0:T(8,128)(2,1)S(1)} %copy-done.1), kind=kOutput, calls=%fused_computation.22 | convolution fusion | flops 301989888 | bytes 2949120 | tf_op jit(solution)/shard_map/transpose(jvp())/dot_general | solution.py:44
  54.9 0.6 collective-permute-start.8
  55.4 6.4 %collective-permute-done.8 = bf16[16,8,768]{2,1,0:T(8,128)(2,1)S(1)} collective-permute-done((bf16[16,8,768]{2,1,0:T(8,128)(2,1)S(1)}, bf16[16,8,768]{2,1,0:T(8,128)(2,1)S(1)}, u32[]{:S(2)}, u32[]{:S(2)}) %collective-permute-start.8) | collective-permute-done | bytes 196640 | tf_op jit(solution)/shard_map/ppermute | solution.py:11
  61.9 0.2 multiply_reduce_fusion
  62.1 0.2 fusion.68
  62.4 0.2 broadcast_add_fusion
  63.5 0.4 copy-done.4
  64.0 0.9 %copy.10 = f32[1,8,4,4,768]{4,3,2,1,0:T(4,128)} copy(f32[1,8,4,4,768]{4,1,3,2,0:T(8,128)S(1)} %bitcast.88) | data formatting | bytes 786432 | tf_op jit(solution)/shard_map/broadcast_in_dim;reshape | solution.py:193
  (139 shorter events, 4.1 us)
Async XLA Ops:
  0.0 7.5 %copy-start = (bf16[1,1536,768]{2,1,0:T(8,128)(2,1)S(1)}, bf16[1,1536,768]{2,1,0:T(8,128)(2,1)}, u32[]{:S(2)}) copy-start(bf16[1,1536,768]{2,1,0:T(8,128)(2,1)} %param.12) | copy-start | bytes 7077892
  1.4 1.7 %copy-start.13 = (f32[768]{0:T(1024)}, f32[768]{0:T(1024)S(1)}, u32[]{:S(2)}) copy-start(f32[768]{0:T(1024)S(1)} %get-tuple-element.26) | copy-start | bytes 9220
  1.4 2.6 %copy-start.11 = (f32[768]{0:T(1024)}, f32[768]{0:T(1024)S(1)}, u32[]{:S(2)}) copy-start(f32[768]{0:T(1024)S(1)} %get-tuple-element.38) | copy-start | bytes 9220
  1.5 1.7 %copy-start.16 = (f32[768]{0:T(1024)}, f32[768]{0:T(1024)S(1)}, u32[]{:S(2)}) copy-start(f32[768]{0:T(1024)S(1)} %get-tuple-element.9) | copy-start | bytes 9220
  1.6 1.9 %copy-start.19 = (f32[768]{0:T(1024)}, f32[768]{0:T(1024)S(1)}, u32[]{:S(2)}) copy-start(f32[768]{0:T(1024)S(1)} %get-tuple-element.6) | copy-start | bytes 9220
  3.0 0.8 %copy-start.27 = (f32[1,768]{1,0:T(1,128)S(1)}, f32[1,768]{1,0:T(1,128)}, u32[]{:S(2)}) copy-start(f32[1,768]{1,0:T(1,128)} %param.10) | copy-start | bytes 9220
  3.8 0.6 copy-start.22
  3.9 0.6 copy-start.9
  6.6 0.9 %copy-start.5 = (f32[128,1536]{1,0:T(8,128)}, f32[128,1536]{1,0:T(8,128)S(1)}, u32[]{:S(2)}) copy-start(f32[128,1536]{1,0:T(8,128)S(1)} %fusion.14) | copy-start | bytes 2359300
  7.5 3.6 %copy-start.24 = (bf16[8,1024]{1,0:T(8,128)(2,1)S(1)}, bf16[8,1024]{1,0:T(8,128)(2,1)}, u32[]{:S(2)}) copy-start(bf16[8,1024]{1,0:T(8,128)(2,1)} %param.14) | copy-start | bytes 49156
  8.1 9.4 %collective-permute-start = (bf16[16,8,768]{2,1,0:T(8,128)(2,1)S(1)}, bf16[16,8,768]{2,1,0:T(8,128)(2,1)}, u32[]{:S(2)}, u32[]{:S(2)}) collective-permute-start(bf16[16,8,768]{2,1,0:T(8,128)(2,1)S(1)} %fusion.16), channel_id=1, source_target_pairs={{0,1},{1,0},{2,3},{3,2},{4,5},{5,4},{6,7},{7,6},{8,9},{9,8},{10,11... | collective-permute-start | bytes 589832 | tf_op jit(solution)/shard_map/ppermute | solution.py:11
  11.3 3.9 %collective-permute-start.3 = (bf16[8,1024]{1,0:T(8,128)(2,1)S(1)}, bf16[8,1024]{1,0:T(8,128)(2,1)}, u32[]{:S(2)}, u32[]{:S(2)}) collective-permute-start(bf16[8,1024]{1,0:T(8,128)(2,1)S(1)} %fusion.70), channel_id=1, source_target_pairs={{0,4},{4,0},{8,12},{12,8},{16,20},{20,16},{24,28},{28,24},{1,5},{5... | collective-permute-start | bytes 49160 | tf_op jit(solution)/shard_map/ppermute | solution.py:11
  12.8 11.8 %copy-start.14 = (f32[768]{0:T(1024)S(1)}, f32[768]{0:T(1024)}, u32[]{:S(2)}) copy-start(f32[768]{0:T(1024)} %copy-done.13) | copy-start | bytes 9220
  15.9 3.9 %collective-permute-start.4 = (bf16[16,1024]{1,0:T(8,128)(2,1)S(1)}, bf16[16,1024]{1,0:T(8,128)(2,1)S(1)}, u32[]{:S(2)}, u32[]{:S(2)}) collective-permute-start(bf16[16,1024]{1,0:T(8,128)(2,1)S(1)} %pad_maximum_fusion.2), channel_id=1, source_target_pairs={{0,8},{4,12},{8,0},{12,4},{16,24},{20,28},{24,16},{28,20},{1,9},{5... | collective-permute-start | bytes 98312 | tf_op jit(solution)/shard_map/ppermute | solution.py:11
  18.5 5.3 %collective-permute-start.1 = (bf16[16,8,768]{2,1,0:T(8,128)(2,1)S(1)}, bf16[16,8,768]{2,1,0:T(8,128)(2,1)S(1)}, u32[]{:S(2)}, u32[]{:S(2)}) collective-permute-start(bf16[16,8,768]{2,1,0:T(8,128)(2,1)S(1)} %add_convert_fusion.4), channel_id=1, source_target_pairs={{0,2},{2,0},{1,3},{3,1},{4,6},{6,4},{5,7},{7,5},{8,10},{10,8},{9,1... | collective-permute-start | bytes 589832 | tf_op jit(solution)/shard_map/ppermute | solution.py:11
  19.8 5.2 %copy-start.25 = (bf16[16,1024]{1,0:T(8,128)(2,1)}, bf16[16,1024]{1,0:T(8,128)(2,1)S(1)}, u32[]{:S(2)}) copy-start(bf16[16,1024]{1,0:T(8,128)(2,1)S(1)} %collective-permute-done.4) | copy-start | bytes 98308
  21.2 9.4 %collective-permute-start.5 = (bf16[32,1024]{1,0:T(8,128)(2,1)}, bf16[32,1024]{1,0:T(8,128)(2,1)}, u32[]{:S(2)}, u32[]{:S(2)}) collective-permute-start(bf16[32,1024]{1,0:T(8,128)(2,1)} %pad_maximum_fusion.1), channel_id=1, source_target_pairs={{0,16},{4,20},{8,24},{12,28},{16,0},{20,4},{24,8},{28,12},{1,17},{... | collective-permute-start | bytes 196616 | tf_op jit(solution)/shard_map/ppermute | solution.py:11
  24.6 0.7 %copy-start.17 = (f32[768]{0:T(1024)S(1)}, f32[768]{0:T(1024)}, u32[]{:S(2)}) copy-start(f32[768]{0:T(1024)} %copy-done.16) | copy-start | bytes 9220
  24.8 0.7 %copy-start.20 = (f32[768]{0:T(1024)S(1)}, f32[768]{0:T(1024)}, u32[]{:S(2)}) copy-start(f32[768]{0:T(1024)} %copy-done.19) | copy-start | bytes 9220
  29.4 1.2 %copy-start.26 = (bf16[16,1024]{1,0:T(8,128)(2,1)S(1)}, bf16[16,1024]{1,0:T(8,128)(2,1)}, u32[]{:S(2)}) copy-start(bf16[16,1024]{1,0:T(8,128)(2,1)} %copy-done.25) | copy-start | bytes 98308
  29.4 1.2 %copy-start.28 = (s32[8]{0:T(128)S(1)}, s32[8]{0:T(128)}, u32[]{:S(2)}) copy-start(s32[8]{0:T(128)} %param.15) | copy-start | bytes 100
  29.4 1.2 %copy-start.29 = (s32[64]{0:T(128)S(1)}, s32[64]{0:T(128)}, u32[]{:S(2)}) copy-start(s32[64]{0:T(128)} %fusion.86) | copy-start | bytes 772
  29.4 7.4 %copy-start.2 = (bf16[768,1024]{1,0:T(8,128)(2,1)S(1)}, bf16[768,1024]{1,0:T(8,128)(2,1)}, u32[]{:S(2)}) copy-start(bf16[768,1024]{1,0:T(8,128)(2,1)} %param.13) | copy-start | bytes 4718596
  30.1 6.4 %collective-permute-start.2 = (bf16[16,8,768]{2,1,0:T(8,128)(2,1)S(1)}, bf16[16,8,768]{2,1,0:T(8,128)(2,1)S(1)}, u32[]{:S(2)}, u32[]{:S(2)}) collective-permute-start(bf16[16,8,768]{2,1,0:T(8,128)(2,1)S(1)} %fusion.19), channel_id=1, source_target_pairs={{0,1},{1,0},{2,3},{3,2},{4,5},{5,4},{6,7},{7,6},{8,9},{9,8},{10,11... | collective-permute-start | bytes 589832 | tf_op jit(solution)/shard_map/ppermute | solution.py:11
  40.6 1.7 %copy-start.1 = (bf16[1,768,1536]{2,1,0:T(8,128)(2,1)S(1)}, bf16[1,768,1536]{2,1,0:T(8,128)(2,1)}, u32[]{:S(2)}) copy-start(bf16[1,768,1536]{2,1,0:T(8,128)(2,1)} %param.11) | copy-start | bytes 7077892
  42.3 7.3 %copy-start.21 = (f32[768]{0:T(1024)S(1)}, f32[768]{0:T(1024)}, u32[]{:S(2)}) copy-start(f32[768]{0:T(1024)} %copy-done.19) | copy-start | bytes 9220
  43.1 6.6 %copy-start.18 = (f32[768]{0:T(1024)S(1)}, f32[768]{0:T(1024)}, u32[]{:S(2)}) copy-start(f32[768]{0:T(1024)} %copy-done.16) | copy-start | bytes 9220
  43.2 5.7 %collective-permute-start.6 = (bf16[16,8,768]{2,1,0:T(8,128)(2,1)S(1)}, bf16[16,8,768]{2,1,0:T(8,128)(2,1)S(1)}, u32[]{:S(2)}, u32[]{:S(2)}) collective-permute-start(bf16[16,8,768]{2,1,0:T(8,128)(2,1)S(1)} %fusion.31), channel_id=1, source_target_pairs={{0,1},{1,0},{2,3},{3,2},{4,5},{5,4},{6,7},{7,6},{8,9},{9,8},{10,11... | collective-permute-start | bytes 589832 | tf_op jit(solution)/shard_map/ppermute | solution.py:11
  49.7 0.7 %copy-start.15 = (f32[768]{0:T(1024)S(1)}, f32[768]{0:T(1024)}, u32[]{:S(2)}) copy-start(f32[768]{0:T(1024)} %copy-done.13) | copy-start | bytes 9220
  49.9 0.7 %copy-start.12 = (f32[768]{0:T(1024)S(1)}, f32[768]{0:T(1024)}, u32[]{:S(2)}) copy-start(f32[768]{0:T(1024)} %copy-done.11) | copy-start | bytes 9220
  50.0 2.8 %copy-start.6 = (f32[128,1536]{1,0:T(8,128)S(1)}, f32[128,1536]{1,0:T(8,128)}, u32[]{:S(2)}) copy-start(f32[128,1536]{1,0:T(8,128)} %copy-done.5) | copy-start | bytes 2359300
  50.6 0.7 %copy-start.3 = (f32[16,8,768]{2,1,0:T(8,128)}, f32[16,8,768]{2,1,0:T(8,128)S(1)}, u32[]{:S(2)}) copy-start(f32[16,8,768]{2,1,0:T(8,128)S(1)} %constant_dynamic-update-slice_fusion.32) | copy-start | bytes 1179652
  51.4 1.5 %collective-permute-start.7 = (bf16[16,8,768]{2,1,0:T(8,128)(2,1)S(1)}, bf16[16,8,768]{2,1,0:T(8,128)(2,1)S(1)}, u32[]{:S(2)}, u32[]{:S(2)}) collective-permute-start(bf16[16,8,768]{2,1,0:T(8,128)(2,1)S(1)} %add_convert_fusion.6), channel_id=1, source_target_pairs={{0,2},{2,0},{1,3},{3,1},{4,6},{6,4},{5,7},{7,5},{8,10},{10,8},{9,1... | collective-permute-start | bytes 589832 | tf_op jit(solution)/shard_map/ppermute | solution.py:11
  52.9 1.1 %copy-start.7 = (bf16[16,8,768]{2,1,0:T(8,128)(2,1)}, bf16[16,8,768]{2,1,0:T(8,128)(2,1)S(1)}, u32[]{:S(2)}) copy-start(bf16[16,8,768]{2,1,0:T(8,128)(2,1)S(1)} %collective-permute-done.7) | copy-start | bytes 589828
  54.0 8.1 %copy-start.23 = (f32[16,8]{1,0:T(8,128)S(1)}, f32[16,8]{1,0:T(8,128)}, u32[]{:S(2)}) copy-start(f32[16,8]{1,0:T(8,128)} %copy-done.22) | copy-start | bytes 1540
  54.0 8.1 %copy-start.10 = (f32[16,8]{1,0:T(8,128)S(1)}, f32[16,8]{1,0:T(8,128)}, u32[]{:S(2)}) copy-start(f32[16,8]{1,0:T(8,128)} %copy-done.9) | copy-start | bytes 1540
  54.9 7.0 %collective-permute-start.8 = (bf16[16,8,768]{2,1,0:T(8,128)(2,1)S(1)}, bf16[16,8,768]{2,1,0:T(8,128)(2,1)S(1)}, u32[]{:S(2)}, u32[]{:S(2)}) collective-permute-start(bf16[16,8,768]{2,1,0:T(8,128)(2,1)S(1)} %fusion.28), channel_id=1, source_target_pairs={{0,1},{1,0},{2,3},{3,2},{4,5},{5,4},{6,7},{7,6},{8,9},{9,8},{10,11... | collective-permute-start | bytes 589832 | tf_op jit(solution)/shard_map/ppermute | solution.py:11
  62.9 1.0 %copy-start.4 = (f32[16,8,768]{2,1,0:T(8,128)S(1)}, f32[16,8,768]{2,1,0:T(8,128)}, u32[]{:S(2)}) copy-start(f32[16,8,768]{2,1,0:T(8,128)} %copy-done.3) | copy-start | bytes 1179652
  62.9 1.0 %copy-start.8 = (bf16[16,8,768]{2,1,0:T(8,128)(2,1)S(1)}, bf16[16,8,768]{2,1,0:T(8,128)(2,1)}, u32[]{:S(2)}) copy-start(bf16[16,8,768]{2,1,0:T(8,128)(2,1)} %copy-done.7) | copy-start | bytes 589828

commit v7 on v6

--- a/solution.py
+++ b/solution.py
@@ -113,10 +113,12 @@
     return normed, front_back
 
 
-def section_forward(inputs_low, kernel, gain_vec, expand, project_out, side):
+def section_forward(inputs_low, kernel, gain_vec, expand, project_out, side, tie=None):
     widened = inputs_low.astype(jnp.float32)
     normed, front_back = front_split(widened, kernel, gain_vec, side)
     partial_out, mlp_back = mlp_part(normed, expand, project_out)
+    if tie is not None:
+        partial_out = tie(partial_out)
     summed = hidden_total(partial_out)
     return ((widened + summed).astype(jnp.bfloat16), front_back, mlp_back)
 
@@ -156,14 +158,29 @@
     count, side = images.shape[0], images.shape[1]
     width = images.shape[3]
     cell_major = images.reshape(count, side * side, width).transpose(1, 0, 2)
+    caption_unit_vectors = unit_text(texts)
+    text_block = jnp.concatenate([caption_unit_vectors, swapped(caption_unit_vectors, "batch", 0)], axis=0)
     first_out, front_one, mlp_one = section_forward(cell_major, kernel, gain_vec, expand, project_out, side)
+    first_out, text_block = lax.optimization_barrier((first_out, text_block))
     handed = hand_over(first_out)
-    second_out, front_two, mlp_two = section_forward(handed, kernel, gain_vec, expand, project_out, side)
+    riding = {}
+
+    def tie(partial_out):
+        partial_out, riding["block"] = lax.optimization_barrier((partial_out, text_block))
+        return partial_out
+
+    second_out, front_two, mlp_two = section_forward(
+        handed, kernel, gain_vec, expand, project_out, side, tie
+    )
+    all_texts = riding["block"]
+    stride = 1
+    while (1 << stride) < lax.axis_size("batch"):
+        all_texts = jnp.concatenate([all_texts, swapped(all_texts, "batch", stride)], axis=0)
+        stride += 1
     embed, head_back = jax.vjp(
         lambda inner: head_part(inner, head_weight), second_out.astype(jnp.float32)
     )
     vector_lowered_total = embed.astype(jnp.bfloat16)
-    caption_unit_vectors = unit_text(texts)
     image_rows = embed.shape[0]
     embed_width = embed.shape[1]
     text_rows = caption_unit_vectors.shape[0]
@@ -180,7 +197,7 @@
     )
     fold_texts = make_fold(vector_lowered_total, pair_index, share_map)
     softmax_denominators, softmax_scaled_captions, diagonal_matched_scores = fold_texts(
-        start_state, gather_rows(caption_unit_vectors, "batch"), jnp.int32(0)
+        start_state, all_texts, jnp.int32(0)
     )
     encoder_output_slope = inverse_softness_factor * (
         softmax_scaled_captions / softmax_denominators[:, None] - diagonal_matched_scores

time: 65.6 us -> 59.6 us (0.909)
  starting transfers between devices: 10.6 us -> 14.4 us
  waiting for transfers between devices: 20.9 us -> 17.2 us
  matrix products: 13.7 us -> 11.2 us
  other arithmetic: 12.3 us -> 9.97 us
  local copies, waits for them, and re-layouts: 6.76 us -> 5.9 us
    ppermute x9, starting transfers between devices: 10.6 us -> 14.4 us  [swapped(): lax.ppermute(value, axis, [(i, i ^ 1 << stride) for i in range(lax.axis_s...]
    ppermute x9, waiting for transfers between devices: 20.9 us -> 17.2 us  [swapped(): lax.ppermute(value, axis, [(i, i ^ 1 << stride) for i in range(lax.axis_s...]
    concatenate x2, other arithmetic: 2.08 us -> 0.61 us  [the longest x1 0.6 us: on_device(): jnp.concatenate([caption_unit_vectors, swapped(caption_unit_vectors, 'bat...]
    unnamed x61 -> x47, local copies, waits for them, and re-layouts: 4.44 us -> 3.57 us
    dot_general x1, matrix products: 1.03 us -> 0.19 us  [fold_texts(): jnp.dot(onehot, text_block, preferred_element_type=jnp.float32)]
    dot_general x1, matrix products: 1.1 us -> 0.26 us  [fold_texts(): jnp.dot(weights, text_block, preferred_element_type=jnp.float32)]
    dot_general x1, matrix products: 1.16 us -> 0.32 us  [fold_texts(): jnp.einsum('ie,je->ij', vector_lowered_total, text_block, preferred_eleme...]
  transfers between devices with their start and end apart: 9 -> 9, of which waited for: 6 -> 8; matrix products, arithmetic and copies ran while one was open for 17% -> 3% of each run, Pallas kernels for 0% -> 0%
where the time goes in v7:
time: 59.6 us; the launch traced here: 59.2 us
  waiting for transfers between devices  17.2 us (29%)
  starting transfers between devices  14.4 us (24%)
  matrix products  11.2 us (19%)
  other arithmetic  9.97 us (17%)
  local copies, waits for them, and re-layouts  5.9 us (10%)
    ppermute x9, waiting for transfers between devices, swapped(): lax.ppermute(value, axis, [(i, i ^ 1 << stride) for i in range(lax.axis_s...  17.2 us
    ppermute x9, starting transfers between devices, swapped(): lax.ppermute(value, axis, [(i, i ^ 1 << stride) for i in range(lax.axis_s...  14.4 us
    dot_general x4, matrix products, expand_part(): return jnp.dot(flattened, expand, preferred_element_type=jnp.float32)  6.02 us
    unnamed x47, local copies, waits for them, and re-layouts  3.57 us
    unnamed x61, other arithmetic  3.37 us
    dot_general x4, matrix products, project_part(): jnp.dot(hidden, project_out, preferred_element_type=jnp.float32)  3.31 us
    reduce_sum x6, other arithmetic, normalize_last(): centred = values - jnp.mean(values, axis=-1, keepdims=True)  1.61 us
  transfers between devices with their start and end apart: 9, of which 8 were waited for; matrix products, arithmetic and copies ran while one was open for 3% of the time, Pallas kernels for 0%

profile of v7, /device:TPU:0, one launch (start us, length us, event | category | flops | bytes accessed | tf_op | source)
XLA Modules:
  0.0 59.2 jit_solution(5689934025713518755)
XLA Ops:
  0.0 1.1 %copy.13 = f32[1,7,7,768]{3,2,0,1:T(8,128)S(1)} copy(f32[1,7,7,768]{3,0,2,1:T(1,128)} %param.9) | data formatting | bytes 301056
  1.1 0.2 slice_reduce_fusion.5
  1.3 0.2 slice_reduce_fusion.19
  1.4 0.1 slice_reduce_fusion.47
  1.5 1.0 %copy.9 = f32[8,4,4,768]{3,0,2,1:T(8,128)S(1)} copy(bf16[8,4,4,768]{3,2,1,0:T(4,128)(2,1)} %param.8) | data formatting | bytes 589824 | tf_op jit(solution)/shard_map/convert_element_type | solution.py:117
  3.5 0.1 reduce_sum.148
  3.6 0.2 multiply_reduce_fusion.3
  3.8 0.1 multiply_convert_fusion.5
  4.0 0.4 copy-done.16
  4.4 2.1 %fusion.14 = f32[128,1536]{1,0:T(8,128)S(1)} fusion(bf16[1,768,1536]{2,1,0:T(8,128)(2,1)} %param.11, bf16[16,8,768]{2,1,0:T(8,128)(2,1)S(1)} %multiply_convert_fusion.5), kind=kOutput, calls=%fused_computation.16 | convolution fusion | flops 301989888 | bytes 3342336 | tf_op jit(solution)/shard_map/jvp()/dot_general | solution.py:44
  6.6 0.6 fusion.16
  7.2 3.1 %collective-permute-start = (bf16[16,8,768]{2,1,0:T(8,128)(2,1)S(1)}, bf16[16,8,768]{2,1,0:T(8,128)(2,1)S(1)}, u32[]{:S(2)}, u32[]{:S(2)}) collective-permute-start(bf16[16,8,768]{2,1,0:T(8,128)(2,1)S(1)} %fusion.16), channel_id=1, source_target_pairs={{0,1},{1,0},{2,3},{3,2},{4,5},{5,4},{6,7},{7,6},{8,9},{9,8},{10,11... | collective-permute-start | bytes 589832 | tf_op jit(solution)/shard_map/ppermute | solution.py:11
  10.2 0.1 fusion.66
  10.4 0.1 fusion.67
  10.4 1.5 %collective-permute-start.1 = (bf16[8,1024]{1,0:T(8,128)(2,1)S(1)}, bf16[8,1024]{1,0:T(8,128)(2,1)S(1)}, u32[]{:S(2)}, u32[]{:S(2)}) collective-permute-start(bf16[8,1024]{1,0:T(8,128)(2,1)S(1)} %fusion.67), channel_id=1, source_target_pairs={{0,4},{4,0},{8,12},{12,8},{16,20},{20,16},{24,28},{28,24},{1,5},{5... | collective-permute-start | bytes 49160 | tf_op jit(solution)/shard_map/ppermute | solution.py:11
  11.9 2.3 %collective-permute-done.1 = bf16[8,1024]{1,0:T(8,128)(2,1)S(1)} collective-permute-done((bf16[8,1024]{1,0:T(8,128)(2,1)S(1)}, bf16[8,1024]{1,0:T(8,128)(2,1)S(1)}, u32[]{:S(2)}, u32[]{:S(2)}) %collective-permute-start.1) | collective-permute-done | bytes 16416 | tf_op jit(solution)/shard_map/ppermute | solution.py:11
  14.2 0.6 %pad_maximum_fusion.1 = bf16[16,1024]{1,0:T(8,128)(2,1)} fusion(bf16[8,1024]{1,0:T(8,128)(2,1)S(1)} %collective-permute-done.1, bf16[8,1024]{1,0:T(8,128)(2,1)S(1)} %fusion.67), kind=kLoop, calls=%fused_computation.159 | loop fusion | flops 65536 | bytes 65536 | tf_op jit(solution)/shard_map/concatenate | solution.py:162
  14.8 0.3 collective-permute-done
  15.1 0.7 %add_convert_fusion.4 = bf16[16,8,768]{2,1,0:T(8,128)(2,1)} fusion(bf16[16,8,768]{2,1,0:T(8,128)(2,1)S(1)} %collective-permute-done, bf16[16,8,768]{2,1,0:T(8,128)(2,1)S(1)} %fusion.16, f32[8,4,4,768]{3,0,2,1:T(8,128)S(1)} %copy.9), kind=kLoop, calls=%fused_computation.65 | loop fusion | flops 688128 | bytes 983040 | tf_op jit(solution)/shard_map/convert_element_type | solution.py:123
  15.9 0.6 fusion.83
  16.4 1.1 %collective-permute-done.2 = bf16[16,8,768]{2,1,0:T(8,128)(2,1)S(1)} collective-permute-done((bf16[16,8,768]{2,1,0:T(8,128)(2,1)}, bf16[16,8,768]{2,1,0:T(8,128)(2,1)S(1)}, u32[]{:S(2)}, u32[]{:S(2)}) %collective-permute-start.2) | collective-permute-done | bytes 196640 | tf_op jit(solution)/shard_map/ppermute | solution.py:11
  18.3 0.1 copy-done.11
  18.6 0.7 %reduce_sum.154 = f32[16,8]{1,0:T(8,128)} reduce(f32[16,8,768]{2,1,0:T(8,128)S(1)} %constant_dynamic-update-slice_fusion.16, f32[]{:T(128)} %constant.67.clone.1), dimensions={2}, to_apply=%region_3.0 | reduce | flops 98176 | bytes 393732 | tf_op jit(solution)/shard_map/jvp()/reduce_sum | solution.py:33
  19.3 0.7 %broadcast_multiply_fusion = f32[16,8]{1,0:T(8,128)S(1)} fusion(f32[16,8]{1,0:T(8,128)} %reduce_sum.154), kind=kLoop, calls=%fused_computation.187 | loop fusion | flops 128 | bytes 1024 | tf_op jit(solution)/shard_map/jvp()/div | solution.py:33
  20.0 0.2 multiply_reduce_fusion.2
  20.2 0.1 multiply_convert_fusion.2
  20.3 2.1 %fusion.12 = f32[128,1536]{1,0:T(8,128)S(1)} fusion(bf16[1,768,1536]{2,1,0:T(8,128)(2,1)} %param.11, bf16[16,8,768]{2,1,0:T(8,128)(2,1)S(1)} %multiply_convert_fusion.2), kind=kOutput, calls=%fused_computation.14 | convolution fusion | flops 301989888 | bytes 3342336 | tf_op jit(solution)/shard_map/jvp()/dot_general | solution.py:44
  22.5 0.6 %fusion.2 = bf16[16,8,768]{2,1,0:T(8,128)(2,1)S(1)} fusion(bf16[1,1536,768]{2,1,0:T(8,128)(2,1)S(1)} %copy-done, f32[128,1536]{1,0:T(8,128)S(1)} %fusion.12), kind=kOutput, calls=%fused_computation.4 | convolution fusion | flops 303759360 | bytes 3342336 | tf_op jit(solution)/shard_map/jvp()/dot_general | solution.py:49
  23.1 0.1 copy-done.7
  23.2 1.8 %collective-permute-start.4 = (bf16[16,1024]{1,0:T(8,128)(2,1)S(1)}, bf16[16,1024]{1,0:T(8,128)(2,1)S(1)}, u32[]{:S(2)}, u32[]{:S(2)}) collective-permute-start(bf16[16,1024]{1,0:T(8,128)(2,1)S(1)} %copy-done.7), channel_id=1, source_target_pairs={{0,8},{4,12},{8,0},{12,4},{16,24},{20,28},{24,16},{28,20},{1,9},{5... | collective-permute-start | bytes 98312 | tf_op jit(solution)/shard_map/ppermute | solution.py:11
  25.0 1.5 %collective-permute-start.3 = (bf16[16,8,768]{2,1,0:T(8,128)(2,1)S(1)}, bf16[16,8,768]{2,1,0:T(8,128)(2,1)S(1)}, u32[]{:S(2)}, u32[]{:S(2)}) collective-permute-start(bf16[16,8,768]{2,1,0:T(8,128)(2,1)S(1)} %fusion.2), channel_id=1, source_target_pairs={{0,1},{1,0},{2,3},{3,2},{4,5},{5,4},{6,7},{7,6},{8,9},{9,8},{10,11... | collective-permute-start | bytes 589832 | tf_op jit(solution)/shard_map/ppermute | solution.py:11
  26.5 0.6 %collective-permute-done.4 = bf16[16,1024]{1,0:T(8,128)(2,1)S(1)} collective-permute-done((bf16[16,1024]{1,0:T(8,128)(2,1)S(1)}, bf16[16,1024]{1,0:T(8,128)(2,1)S(1)}, u32[]{:S(2)}, u32[]{:S(2)}) %collective-permute-start.4) | collective-permute-done | bytes 32800 | tf_op jit(solution)/shard_map/ppermute | solution.py:11
  27.1 2.8 %collective-permute-start.5 = (bf16[32,1024]{1,0:T(8,128)(2,1)S(1)}, bf16[32,1024]{1,0:T(8,128)(2,1)S(1)}, u32[]{:S(2)}, u32[]{:S(2)}) collective-permute-start(bf16[32,1024]{1,0:T(8,128)(2,1)S(1)} %pad_maximum_fusion), channel_id=1, source_target_pairs={{0,16},{4,20},{8,24},{12,28},{16,0},{20,4},{24,8},{28,12},{1,17},{... | collective-permute-start | bytes 196616 | tf_op jit(solution)/shard_map/ppermute | solution.py:11
  30.0 2.3 %collective-permute-done.5 = bf16[32,1024]{1,0:T(8,128)(2,1)S(1)} collective-permute-done((bf16[32,1024]{1,0:T(8,128)(2,1)S(1)}, bf16[32,1024]{1,0:T(8,128)(2,1)S(1)}, u32[]{:S(2)}, u32[]{:S(2)}) %collective-permute-start.5) | collective-permute-done | bytes 65568 | tf_op jit(solution)/shard_map/ppermute | solution.py:11
  32.3 0.2 fusion.79
  32.5 0.1 convert_reduce_fusion
  32.6 0.1 multiply_reduce_fusion.8
  32.7 0.2 multiply_reduce_fusion.7
  32.9 0.5 multiply_reduce_fusion.5
  33.4 0.3 convert_reduce_fusion.1
  33.7 0.3 multiply_reduce_fusion.4
  34.0 0.6 %multiply_reduce_fusion.6 = (f32[8]{0:T(128)S(1)}, f32[8,768]{1,0:T(8,128)S(1)}) fusion(f32[8,768]{1,0:T(8,128)S(1)} %convert_reduce_fusion, f32[8]{0:T(128)S(1)} %broadcast_multiply_fusion.3, bf16[768,1024]{1,0:T(8,128)(2,1)S(1)} %copy-done.2, f32[8,1024]{1,0:T(8,128)S(1)} %get-tuple-element.67, f32[8,1024]{1,0:T(8,128)S(1)} %get-tuple-element.71, ...), kind=kOutput, calls=%fused_computation.166 | convolution fusion | flops 12652536 | bytes 1687680 | tf_op jit(solution)/shard_map/transpose(jvp())/dot_general | solution.py:68
  34.7 0.2 fusion.96
  34.9 0.1 add_multiply_fusion
  35.0 1.1 %fusion.46 = bf16[128,1536]{1,0:T(8,128)(2,1)S(1)} fusion(f32[128,1536]{1,0:T(8,128)S(1)} %fusion.12, bf16[1,1536,768]{2,1,0:T(8,128)(2,1)S(1)} %copy-done, f32[8,768]{1,0:T(8,128)S(1)} %add_multiply_fusion), kind=kOutput, calls=%fused_computation.45 | convolution fusion | flops 306118656 | bytes 3563520 | tf_op jit(solution)/shard_map/transpose(jvp())/dot_general | solution.py:49
  36.0 0.6 %copy-done.1 = bf16[1,768,1536]{2,1,0:T(8,128)(2,1)S(1)} copy-done((bf16[1,768,1536]{2,1,0:T(8,128)(2,1)S(1)}, bf16[1,768,1536]{2,1,0:T(8,128)(2,1)}, u32[]{:S(2)}) %copy-start.1) | copy-done | bytes 2359320
  36.6 0.9 %fusion.28 = bf16[16,8,768]{2,1,0:T(8,128)(2,1)S(1)} fusion(bf16[128,1536]{1,0:T(8,128)(2,1)S(1)} %fusion.46, bf16[1,768,1536]{2,1,0:T(8,128)(2,1)S(1)} %copy-done.1), kind=kOutput, calls=%fused_computation.22 | convolution fusion | flops 301989888 | bytes 2949120 | tf_op jit(solution)/shard_map/transpose(jvp())/dot_general | solution.py:44
  37.5 1.8 %collective-permute-start.6 = (bf16[16,8,768]{2,1,0:T(8,128)(2,1)S(1)}, bf16[16,8,768]{2,1,0:T(8,128)(2,1)S(1)}, u32[]{:S(2)}, u32[]{:S(2)}) collective-permute-start(bf16[16,8,768]{2,1,0:T(8,128)(2,1)S(1)} %fusion.28), channel_id=1, source_target_pairs={{0,1},{1,0},{2,3},{3,2},{4,5},{5,4},{6,7},{7,6},{8,9},{9,8},{10,11... | collective-permute-start | bytes 589832 | tf_op jit(solution)/shard_map/ppermute | solution.py:11
  39.3 3.9 %collective-permute-done.6 = bf16[16,8,768]{2,1,0:T(8,128)(2,1)S(1)} collective-permute-done((bf16[16,8,768]{2,1,0:T(8,128)(2,1)S(1)}, bf16[16,8,768]{2,1,0:T(8,128)(2,1)S(1)}, u32[]{:S(2)}, u32[]{:S(2)}) %collective-permute-start.6) | collective-permute-done | bytes 196640 | tf_op jit(solution)/shard_map/ppermute | solution.py:11
  43.3 0.2 multiply_reduce_fusion.1
  43.5 0.2 fusion.64
  43.7 0.2 broadcast_add_fusion.1
  44.9 0.7 %copy-done.3 = f32[16,8,768]{2,1,0:T(8,128)} copy-done((f32[16,8,768]{2,1,0:T(8,128)}, f32[16,8,768]{2,1,0:T(8,128)S(1)}, u32[]{:S(2)}) %copy-start.3) | copy-done | bytes 393240
  45.7 1.4 %collective-permute-done.7 = bf16[16,8,768]{2,1,0:T(8,128)(2,1)S(1)} collective-permute-done((bf16[16,8,768]{2,1,0:T(8,128)(2,1)S(1)}, bf16[16,8,768]{2,1,0:T(8,128)(2,1)S(1)}, u32[]{:S(2)}, u32[]{:S(2)}) %collective-permute-start.7) | collective-permute-done | bytes 196640 | tf_op jit(solution)/shard_map/ppermute | solution.py:11
  47.1 1.1 %fusion.40 = bf16[128,1536]{1,0:T(8,128)(2,1)S(1)} fusion(f32[128,1536]{1,0:T(8,128)S(1)} %copy-done.6, bf16[1,1536,768]{2,1,0:T(8,128)(2,1)S(1)} %copy-done, bf16[16,8,768]{2,1,0:T(8,128)(2,1)S(1)} %collective-permute-done.7), kind=kOutput, calls=%fused_computation.39 | convolution fusion | flops 306315264 | bytes 3735552 | tf_op jit(solution)/shard_map/transpose(jvp())/dot_general | solution.py:49
  48.2 0.9 %fusion.25 = bf16[16,8,768]{2,1,0:T(8,128)(2,1)S(1)} fusion(bf16[128,1536]{1,0:T(8,128)(2,1)S(1)} %fusion.40, bf16[1,768,1536]{2,1,0:T(8,128)(2,1)S(1)} %copy-done.1), kind=kOutput, calls=%fused_computation.21 | convolution fusion | flops 301989888 | bytes 2949120 | tf_op jit(solution)/shard_map/transpose(jvp())/dot_general | solution.py:44
  49.1 1.8 %collective-permute-start.8 = (bf16[16,8,768]{2,1,0:T(8,128)(2,1)S(1)}, bf16[16,8,768]{2,1,0:T(8,128)(2,1)S(1)}, u32[]{:S(2)}, u32[]{:S(2)}) collective-permute-start(bf16[16,8,768]{2,1,0:T(8,128)(2,1)S(1)} %fusion.25), channel_id=1, source_target_pairs={{0,1},{1,0},{2,3},{3,2},{4,5},{5,4},{6,7},{7,6},{8,9},{9,8},{10,11... | collective-permute-start | bytes 589832 | tf_op jit(solution)/shard_map/ppermute | solution.py:11
  50.9 5.2 %collective-permute-done.8 = bf16[16,8,768]{2,1,0:T(8,128)(2,1)S(1)} collective-permute-done((bf16[16,8,768]{2,1,0:T(8,128)(2,1)S(1)}, bf16[16,8,768]{2,1,0:T(8,128)(2,1)S(1)}, u32[]{:S(2)}, u32[]{:S(2)}) %collective-permute-start.8) | collective-permute-done | bytes 196640 | tf_op jit(solution)/shard_map/ppermute | solution.py:11
  56.1 0.2 multiply_reduce_fusion
  56.3 0.3 fusion.65
  56.6 0.2 broadcast_add_fusion
  57.7 0.4 copy-done.4
  58.2 0.1 add_select_fusion
  58.3 0.9 %copy.10 = f32[1,8,4,4,768]{4,3,2,1,0:T(4,128)} copy(f32[1,8,4,4,768]{4,1,3,2,0:T(8,128)S(1)} %bitcast.89) | data formatting | bytes 786432 | tf_op jit(solution)/shard_map/broadcast_in_dim;reshape | solution.py:210
  (126 shorter events, 4.0 us)
Async XLA Ops:
  0.0 6.5 %copy-start = (bf16[1,1536,768]{2,1,0:T(8,128)(2,1)S(1)}, bf16[1,1536,768]{2,1,0:T(8,128)(2,1)}, u32[]{:S(2)}) copy-start(bf16[1,1536,768]{2,1,0:T(8,128)(2,1)} %param.12) | copy-start | bytes 7077892
  1.3 2.0 %copy-start.10 = (f32[768]{0:T(1024)}, f32[768]{0:T(1024)S(1)}, u32[]{:S(2)}) copy-start(f32[768]{0:T(1024)S(1)} %get-tuple-element.17) | copy-start | bytes 9220
  1.3 2.2 %copy-start.13 = (f32[768]{0:T(1024)}, f32[768]{0:T(1024)S(1)}, u32[]{:S(2)}) copy-start(f32[768]{0:T(1024)S(1)} %get-tuple-element.14) | copy-start | bytes 9220
  3.0 0.8 %copy-start.19 = (f32[1,768]{1,0:T(1,128)S(1)}, f32[1,768]{1,0:T(1,128)}, u32[]{:S(2)}) copy-start(f32[1,768]{1,0:T(1,128)} %param.10) | copy-start | bytes 9220
  3.8 0.6 %copy-start.16 = (f32[16,8]{1,0:T(8,128)}, f32[16,8]{1,0:T(8,128)S(1)}, u32[]{:S(2)}) copy-start(f32[16,8]{1,0:T(8,128)S(1)} %multiply_reduce_fusion.3) | copy-start | bytes 1540
  6.5 9.3 %copy-start.5 = (f32[128,1536]{1,0:T(8,128)}, f32[128,1536]{1,0:T(8,128)S(1)}, u32[]{:S(2)}) copy-start(f32[128,1536]{1,0:T(8,128)S(1)} %fusion.14) | copy-start | bytes 2359300
  6.6 3.7 %copy-start.18 = (bf16[8,1024]{1,0:T(8,128)(2,1)S(1)}, bf16[8,1024]{1,0:T(8,128)(2,1)}, u32[]{:S(2)}) copy-start(bf16[8,1024]{1,0:T(8,128)(2,1)} %param.14) | copy-start | bytes 49156
  7.2 8.0 %collective-permute-start = (bf16[16,8,768]{2,1,0:T(8,128)(2,1)S(1)}, bf16[16,8,768]{2,1,0:T(8,128)(2,1)S(1)}, u32[]{:S(2)}, u32[]{:S(2)}) collective-permute-start(bf16[16,8,768]{2,1,0:T(8,128)(2,1)S(1)} %fusion.16), channel_id=1, source_target_pairs={{0,1},{1,0},{2,3},{3,2},{4,5},{5,4},{6,7},{7,6},{8,9},{9,8},{10,11... | collective-permute-start | bytes 589832 | tf_op jit(solution)/shard_map/ppermute | solution.py:11
  10.4 3.7 %collective-permute-start.1 = (bf16[8,1024]{1,0:T(8,128)(2,1)S(1)}, bf16[8,1024]{1,0:T(8,128)(2,1)S(1)}, u32[]{:S(2)}, u32[]{:S(2)}) collective-permute-start(bf16[8,1024]{1,0:T(8,128)(2,1)S(1)} %fusion.67), channel_id=1, source_target_pairs={{0,4},{4,0},{8,12},{12,8},{16,20},{20,16},{24,28},{28,24},{1,5},{5... | collective-permute-start | bytes 49160 | tf_op jit(solution)/shard_map/ppermute | solution.py:11
  15.9 1.7 %collective-permute-start.2 = (bf16[16,8,768]{2,1,0:T(8,128)(2,1)}, bf16[16,8,768]{2,1,0:T(8,128)(2,1)S(1)}, u32[]{:S(2)}, u32[]{:S(2)}) collective-permute-start(bf16[16,8,768]{2,1,0:T(8,128)(2,1)} %add_convert_fusion.4), channel_id=1, source_target_pairs={{0,2},{2,0},{1,3},{3,1},{4,6},{6,4},{5,7},{7,5},{8,10},{10,8},{9,1... | collective-permute-start | bytes 589832 | tf_op jit(solution)/shard_map/ppermute | solution.py:11
  17.7 0.7 %copy-start.11 = (f32[768]{0:T(1024)S(1)}, f32[768]{0:T(1024)}, u32[]{:S(2)}) copy-start(f32[768]{0:T(1024)} %copy-done.10) | copy-start | bytes 9220
  17.9 0.7 %copy-start.14 = (f32[768]{0:T(1024)S(1)}, f32[768]{0:T(1024)}, u32[]{:S(2)}) copy-start(f32[768]{0:T(1024)} %copy-done.13) | copy-start | bytes 9220
  22.5 0.8 %copy-start.7 = (bf16[16,1024]{1,0:T(8,128)(2,1)S(1)}, bf16[16,1024]{1,0:T(8,128)(2,1)}, u32[]{:S(2)}) copy-start(bf16[16,1024]{1,0:T(8,128)(2,1)} %pad_maximum_fusion.1) | copy-start | bytes 98308
  22.5 9.8 %copy-start.20 = (s32[8]{0:T(128)S(1)}, s32[8]{0:T(128)}, u32[]{:S(2)}) copy-start(s32[8]{0:T(128)} %param.15) | copy-start | bytes 100
  22.5 9.8 %copy-start.21 = (s32[64]{0:T(128)S(1)}, s32[64]{0:T(128)}, u32[]{:S(2)}) copy-start(s32[64]{0:T(128)} %fusion.83) | copy-start | bytes 772
  22.5 10.4 %copy-start.2 = (bf16[768,1024]{1,0:T(8,128)(2,1)S(1)}, bf16[768,1024]{1,0:T(8,128)(2,1)}, u32[]{:S(2)}) copy-start(bf16[768,1024]{1,0:T(8,128)(2,1)} %param.13) | copy-start | bytes 4718596
  23.2 3.9 %collective-permute-start.4 = (bf16[16,1024]{1,0:T(8,128)(2,1)S(1)}, bf16[16,1024]{1,0:T(8,128)(2,1)S(1)}, u32[]{:S(2)}, u32[]{:S(2)}) collective-permute-start(bf16[16,1024]{1,0:T(8,128)(2,1)S(1)} %copy-done.7), channel_id=1, source_target_pairs={{0,8},{4,12},{8,0},{12,4},{16,24},{20,28},{24,16},{28,20},{1,9},{5... | collective-permute-start | bytes 98312 | tf_op jit(solution)/shard_map/ppermute | solution.py:11
  25.0 7.5 %collective-permute-start.3 = (bf16[16,8,768]{2,1,0:T(8,128)(2,1)S(1)}, bf16[16,8,768]{2,1,0:T(8,128)(2,1)S(1)}, u32[]{:S(2)}, u32[]{:S(2)}) collective-permute-start(bf16[16,8,768]{2,1,0:T(8,128)(2,1)S(1)} %fusion.2), channel_id=1, source_target_pairs={{0,1},{1,0},{2,3},{3,2},{4,5},{5,4},{6,7},{7,6},{8,9},{9,8},{10,11... | collective-permute-start | bytes 589832 | tf_op jit(solution)/shard_map/ppermute | solution.py:11
  27.1 5.2 %collective-permute-start.5 = (bf16[32,1024]{1,0:T(8,128)(2,1)S(1)}, bf16[32,1024]{1,0:T(8,128)(2,1)S(1)}, u32[]{:S(2)}, u32[]{:S(2)}) collective-permute-start(bf16[32,1024]{1,0:T(8,128)(2,1)S(1)} %pad_maximum_fusion), channel_id=1, source_target_pairs={{0,16},{4,20},{8,24},{12,28},{16,0},{20,4},{24,8},{28,12},{1,17},{... | collective-permute-start | bytes 196616 | tf_op jit(solution)/shard_map/ppermute | solution.py:11
  35.0 1.7 %copy-start.1 = (bf16[1,768,1536]{2,1,0:T(8,128)(2,1)S(1)}, bf16[1,768,1536]{2,1,0:T(8,128)(2,1)}, u32[]{:S(2)}) copy-start(bf16[1,768,1536]{2,1,0:T(8,128)(2,1)} %param.11) | copy-start | bytes 7077892
  36.6 7.3 %copy-start.15 = (f32[768]{0:T(1024)S(1)}, f32[768]{0:T(1024)}, u32[]{:S(2)}) copy-start(f32[768]{0:T(1024)} %copy-done.13) | copy-start | bytes 9220
  37.5 6.6 %copy-start.12 = (f32[768]{0:T(1024)S(1)}, f32[768]{0:T(1024)}, u32[]{:S(2)}) copy-start(f32[768]{0:T(1024)} %copy-done.10) | copy-start | bytes 9220
  37.5 5.7 %collective-permute-start.6 = (bf16[16,8,768]{2,1,0:T(8,128)(2,1)S(1)}, bf16[16,8,768]{2,1,0:T(8,128)(2,1)S(1)}, u32[]{:S(2)}, u32[]{:S(2)}) collective-permute-start(bf16[16,8,768]{2,1,0:T(8,128)(2,1)S(1)} %fusion.28), channel_id=1, source_target_pairs={{0,1},{1,0},{2,3},{3,2},{4,5},{5,4},{6,7},{7,6},{8,9},{9,8},{10,11... | collective-permute-start | bytes 589832 | tf_op jit(solution)/shard_map/ppermute | solution.py:11
  44.4 2.8 %copy-start.6 = (f32[128,1536]{1,0:T(8,128)S(1)}, f32[128,1536]{1,0:T(8,128)}, u32[]{:S(2)}) copy-start(f32[128,1536]{1,0:T(8,128)} %copy-done.5) | copy-start | bytes 2359300
  44.9 0.7 %copy-start.3 = (f32[16,8,768]{2,1,0:T(8,128)}, f32[16,8,768]{2,1,0:T(8,128)S(1)}, u32[]{:S(2)}) copy-start(f32[16,8,768]{2,1,0:T(8,128)S(1)} %constant_dynamic-update-slice_fusion.35) | copy-start | bytes 1179652
  45.6 1.5 %collective-permute-start.7 = (bf16[16,8,768]{2,1,0:T(8,128)(2,1)S(1)}, bf16[16,8,768]{2,1,0:T(8,128)(2,1)S(1)}, u32[]{:S(2)}, u32[]{:S(2)}) collective-permute-start(bf16[16,8,768]{2,1,0:T(8,128)(2,1)S(1)} %add_convert_fusion.6), channel_id=1, source_target_pairs={{0,2},{2,0},{1,3},{3,1},{4,6},{6,4},{5,7},{7,5},{8,10},{10,8},{9,1... | collective-permute-start | bytes 589832 | tf_op jit(solution)/shard_map/ppermute | solution.py:11
  47.1 1.1 %copy-start.8 = (bf16[16,8,768]{2,1,0:T(8,128)(2,1)}, bf16[16,8,768]{2,1,0:T(8,128)(2,1)S(1)}, u32[]{:S(2)}) copy-start(bf16[16,8,768]{2,1,0:T(8,128)(2,1)S(1)} %collective-permute-done.7) | copy-start | bytes 589828
  48.2 8.1 %copy-start.17 = (f32[16,8]{1,0:T(8,128)S(1)}, f32[16,8]{1,0:T(8,128)}, u32[]{:S(2)}) copy-start(f32[16,8]{1,0:T(8,128)} %copy-done.16) | copy-start | bytes 1540
  49.1 7.0 %collective-permute-start.8 = (bf16[16,8,768]{2,1,0:T(8,128)(2,1)S(1)}, bf16[16,8,768]{2,1,0:T(8,128)(2,1)S(1)}, u32[]{:S(2)}, u32[]{:S(2)}) collective-permute-start(bf16[16,8,768]{2,1,0:T(8,128)(2,1)S(1)} %fusion.25), channel_id=1, source_target_pairs={{0,1},{1,0},{2,3},{3,2},{4,5},{5,4},{6,7},{7,6},{8,9},{9,8},{10,11... | collective-permute-start | bytes 589832 | tf_op jit(solution)/shard_map/ppermute | solution.py:11
  57.1 1.0 %copy-start.4 = (f32[16,8,768]{2,1,0:T(8,128)S(1)}, f32[16,8,768]{2,1,0:T(8,128)}, u32[]{:S(2)}) copy-start(f32[16,8,768]{2,1,0:T(8,128)} %copy-done.3) | copy-start | bytes 1179652
  57.1 1.0 %copy-start.9 = (bf16[16,8,768]{2,1,0:T(8,128)(2,1)S(1)}, bf16[16,8,768]{2,1,0:T(8,128)(2,1)}, u32[]{:S(2)}) copy-start(bf16[16,8,768]{2,1,0:T(8,128)(2,1)} %copy-done.8) | copy-start | bytes 589828

commit v8 on v7

--- a/solution.py
+++ b/solution.py
@@ -172,14 +172,17 @@
     second_out, front_two, mlp_two = section_forward(
         handed, kernel, gain_vec, expand, project_out, side, tie
     )
+    embed, head_back = jax.vjp(
+        lambda inner: head_part(inner, head_weight), second_out.astype(jnp.float32)
+    )
     all_texts = riding["block"]
     stride = 1
     while (1 << stride) < lax.axis_size("batch"):
-        all_texts = jnp.concatenate([all_texts, swapped(all_texts, "batch", stride)], axis=0)
+        other = swapped(all_texts, "batch", stride)
         stride += 1
-    embed, head_back = jax.vjp(
-        lambda inner: head_part(inner, head_weight), second_out.astype(jnp.float32)
-    )
+        if (1 << stride) >= lax.axis_size("batch"):
+            embed, other = lax.optimization_barrier((embed, other))
+        all_texts = jnp.concatenate([all_texts, other], axis=0)
     vector_lowered_total = embed.astype(jnp.bfloat16)
     image_rows = embed.shape[0]
     embed_width = embed.shape[1]

time: 59.6 us -> 59.1 us (level)
  transfers between devices with their start and end apart: 9 -> 9, of which waited for: 8 -> 8; matrix products, arithmetic and copies ran while one was open for 3% -> 4% of each run, Pallas kernels for 0% -> 0%
where the time goes in v8:
time: 59.1 us; the launch traced here: 58.7 us
  waiting for transfers between devices  17.2 us (29%)
  starting transfers between devices  13.9 us (24%)
  matrix products  11.1 us (19%)
  other arithmetic  10 us (17%)
  local copies, waits for them, and re-layouts  5.92 us (10%)
    ppermute x9, waiting for transfers between devices, swapped(): lax.ppermute(value, axis, [(i, i ^ 1 << stride) for i in range(lax.axis_s...  17.2 us
    ppermute x9, starting transfers between devices, swapped(): lax.ppermute(value, axis, [(i, i ^ 1 << stride) for i in range(lax.axis_s...  13.9 us
    dot_general x4, matrix products, expand_part(): return jnp.dot(flattened, expand, preferred_element_type=jnp.float32)  6.02 us
    unnamed x47, local copies, waits for them, and re-layouts  3.59 us
    unnamed x61, other arithmetic  3.37 us
    dot_general x4, matrix products, project_part(): jnp.dot(hidden, project_out, preferred_element_type=jnp.float32)  3.3 us
    reduce_sum x6, other arithmetic, normalize_last(): centred = values - jnp.mean(values, axis=-1, keepdims=True)  1.61 us
  transfers between devices with their start and end apart: 9, of which 8 were waited for; matrix products, arithmetic and copies ran while one was open for 4% of the time, Pallas kernels for 0%

profile of v8, /device:TPU:0, one launch (start us, length us, event | category | flops | bytes accessed | tf_op | source)
XLA Modules:
  0.0 58.7 jit_solution(5967819981400582796)
XLA Ops:
  0.0 1.1 %copy.13 = f32[1,7,7,768]{3,2,0,1:T(8,128)S(1)} copy(f32[1,7,7,768]{3,0,2,1:T(1,128)} %param.9) | data formatting | bytes 301056
  1.1 0.2 slice_reduce_fusion.5
  1.3 0.2 slice_reduce_fusion.19
  1.4 0.1 slice_reduce_fusion.47
  1.5 1.0 %copy.9 = f32[8,4,4,768]{3,0,2,1:T(8,128)S(1)} copy(bf16[8,4,4,768]{3,2,1,0:T(4,128)(2,1)} %param.8) | data formatting | bytes 589824 | tf_op jit(solution)/shard_map/convert_element_type | solution.py:117
  3.5 0.1 reduce_sum.148
  3.6 0.2 multiply_reduce_fusion.3
  3.8 0.1 multiply_convert_fusion.5
  4.0 0.4 copy-done.16
  4.4 2.1 %fusion.14 = f32[128,1536]{1,0:T(8,128)S(1)} fusion(bf16[1,768,1536]{2,1,0:T(8,128)(2,1)} %param.11, bf16[16,8,768]{2,1,0:T(8,128)(2,1)S(1)} %multiply_convert_fusion.5), kind=kOutput, calls=%fused_computation.16 | convolution fusion | flops 301989888 | bytes 3342336 | tf_op jit(solution)/shard_map/jvp()/dot_general | solution.py:44
  6.6 0.6 fusion.16
  7.2 3.1 %collective-permute-start = (bf16[16,8,768]{2,1,0:T(8,128)(2,1)S(1)}, bf16[16,8,768]{2,1,0:T(8,128)(2,1)S(1)}, u32[]{:S(2)}, u32[]{:S(2)}) collective-permute-start(bf16[16,8,768]{2,1,0:T(8,128)(2,1)S(1)} %fusion.16), channel_id=1, source_target_pairs={{0,1},{1,0},{2,3},{3,2},{4,5},{5,4},{6,7},{7,6},{8,9},{9,8},{10,11... | collective-permute-start | bytes 589832 | tf_op jit(solution)/shard_map/ppermute | solution.py:11
  10.2 0.1 fusion.66
  10.4 0.1 fusion.67
  10.4 1.5 %collective-permute-start.1 = (bf16[8,1024]{1,0:T(8,128)(2,1)S(1)}, bf16[8,1024]{1,0:T(8,128)(2,1)S(1)}, u32[]{:S(2)}, u32[]{:S(2)}) collective-permute-start(bf16[8,1024]{1,0:T(8,128)(2,1)S(1)} %fusion.67), channel_id=1, source_target_pairs={{0,4},{4,0},{8,12},{12,8},{16,20},{20,16},{24,28},{28,24},{1,5},{5... | collective-permute-start | bytes 49160 | tf_op jit(solution)/shard_map/ppermute | solution.py:11
  11.9 2.3 %collective-permute-done.1 = bf16[8,1024]{1,0:T(8,128)(2,1)S(1)} collective-permute-done((bf16[8,1024]{1,0:T(8,128)(2,1)S(1)}, bf16[8,1024]{1,0:T(8,128)(2,1)S(1)}, u32[]{:S(2)}, u32[]{:S(2)}) %collective-permute-start.1) | collective-permute-done | bytes 16416 | tf_op jit(solution)/shard_map/ppermute | solution.py:11
  14.2 0.6 %pad_maximum_fusion.1 = bf16[16,1024]{1,0:T(8,128)(2,1)} fusion(bf16[8,1024]{1,0:T(8,128)(2,1)S(1)} %collective-permute-done.1, bf16[8,1024]{1,0:T(8,128)(2,1)S(1)} %fusion.67), kind=kLoop, calls=%fused_computation.159 | loop fusion | flops 65536 | bytes 65536 | tf_op jit(solution)/shard_map/concatenate | solution.py:162
  14.8 0.3 collective-permute-done
  15.1 0.7 %add_convert_fusion.4 = bf16[16,8,768]{2,1,0:T(8,128)(2,1)} fusion(bf16[16,8,768]{2,1,0:T(8,128)(2,1)S(1)} %collective-permute-done, bf16[16,8,768]{2,1,0:T(8,128)(2,1)S(1)} %fusion.16, f32[8,4,4,768]{3,0,2,1:T(8,128)S(1)} %copy.9), kind=kLoop, calls=%fused_computation.65 | loop fusion | flops 688128 | bytes 983040 | tf_op jit(solution)/shard_map/convert_element_type | solution.py:123
  15.9 0.6 fusion.83
  16.4 1.1 %collective-permute-done.2 = bf16[16,8,768]{2,1,0:T(8,128)(2,1)S(1)} collective-permute-done((bf16[16,8,768]{2,1,0:T(8,128)(2,1)}, bf16[16,8,768]{2,1,0:T(8,128)(2,1)S(1)}, u32[]{:S(2)}, u32[]{:S(2)}) %collective-permute-start.2) | collective-permute-done | bytes 196640 | tf_op jit(solution)/shard_map/ppermute | solution.py:11
  18.3 0.1 copy-done.11
  18.6 0.7 %reduce_sum.154 = f32[16,8]{1,0:T(8,128)} reduce(f32[16,8,768]{2,1,0:T(8,128)S(1)} %constant_dynamic-update-slice_fusion.16, f32[]{:T(128)} %constant.67.clone.1), dimensions={2}, to_apply=%region_3.0 | reduce | flops 98176 | bytes 393732 | tf_op jit(solution)/shard_map/jvp()/reduce_sum | solution.py:33
  19.3 0.7 %broadcast_multiply_fusion.1 = f32[16,8]{1,0:T(8,128)S(1)} fusion(f32[16,8]{1,0:T(8,128)} %reduce_sum.154), kind=kLoop, calls=%fused_computation.187 | loop fusion | flops 128 | bytes 1024 | tf_op jit(solution)/shard_map/jvp()/div | solution.py:33
  20.0 0.2 multiply_reduce_fusion.2
  20.2 0.1 multiply_convert_fusion.2
  20.3 2.1 %fusion.12 = f32[128,1536]{1,0:T(8,128)S(1)} fusion(bf16[1,768,1536]{2,1,0:T(8,128)(2,1)} %param.11, bf16[16,8,768]{2,1,0:T(8,128)(2,1)S(1)} %multiply_convert_fusion.2), kind=kOutput, calls=%fused_computation.14 | convolution fusion | flops 301989888 | bytes 3342336 | tf_op jit(solution)/shard_map/jvp()/dot_general | solution.py:44
  22.5 0.6 %fusion.2 = bf16[16,8,768]{2,1,0:T(8,128)(2,1)S(1)} fusion(bf16[1,1536,768]{2,1,0:T(8,128)(2,1)S(1)} %copy-done, f32[128,1536]{1,0:T(8,128)S(1)} %fusion.12), kind=kOutput, calls=%fused_computation.4 | convolution fusion | flops 303759360 | bytes 3342336 | tf_op jit(solution)/shard_map/jvp()/dot_general | solution.py:49
  23.1 0.1 copy-done.7
  23.2 1.8 %collective-permute-start.4 = (bf16[16,1024]{1,0:T(8,128)(2,1)S(1)}, bf16[16,1024]{1,0:T(8,128)(2,1)S(1)}, u32[]{:S(2)}, u32[]{:S(2)}) collective-permute-start(bf16[16,1024]{1,0:T(8,128)(2,1)S(1)} %copy-done.7), channel_id=1, source_target_pairs={{0,8},{4,12},{8,0},{12,4},{16,24},{20,28},{24,16},{28,20},{1,9},{5... | collective-permute-start | bytes 98312 | tf_op jit(solution)/shard_map/ppermute | solution.py:11
  25.0 1.5 %collective-permute-start.3 = (bf16[16,8,768]{2,1,0:T(8,128)(2,1)S(1)}, bf16[16,8,768]{2,1,0:T(8,128)(2,1)S(1)}, u32[]{:S(2)}, u32[]{:S(2)}) collective-permute-start(bf16[16,8,768]{2,1,0:T(8,128)(2,1)S(1)} %fusion.2), channel_id=1, source_target_pairs={{0,1},{1,0},{2,3},{3,2},{4,5},{5,4},{6,7},{7,6},{8,9},{9,8},{10,11... | collective-permute-start | bytes 589832 | tf_op jit(solution)/shard_map/ppermute | solution.py:11
  26.5 0.6 %collective-permute-done.4 = bf16[16,1024]{1,0:T(8,128)(2,1)S(1)} collective-permute-done((bf16[16,1024]{1,0:T(8,128)(2,1)S(1)}, bf16[16,1024]{1,0:T(8,128)(2,1)S(1)}, u32[]{:S(2)}, u32[]{:S(2)}) %collective-permute-start.4) | collective-permute-done | bytes 32800 | tf_op jit(solution)/shard_map/ppermute | solution.py:11
  27.1 2.8 %collective-permute-start.5 = (bf16[32,1024]{1,0:T(8,128)(2,1)S(1)}, bf16[32,1024]{1,0:T(8,128)(2,1)S(1)}, u32[]{:S(2)}, u32[]{:S(2)}) collective-permute-start(bf16[32,1024]{1,0:T(8,128)(2,1)S(1)} %pad_maximum_fusion), channel_id=1, source_target_pairs={{0,16},{4,20},{8,24},{12,28},{16,0},{20,4},{24,8},{28,12},{1,17},{... | collective-permute-start | bytes 196616 | tf_op jit(solution)/shard_map/ppermute | solution.py:11
  30.0 1.7 %collective-permute-done.3 = bf16[16,8,768]{2,1,0:T(8,128)(2,1)S(1)} collective-permute-done((bf16[16,8,768]{2,1,0:T(8,128)(2,1)S(1)}, bf16[16,8,768]{2,1,0:T(8,128)(2,1)S(1)}, u32[]{:S(2)}, u32[]{:S(2)}) %collective-permute-start.3) | collective-permute-done | bytes 196640 | tf_op jit(solution)/shard_map/ppermute | solution.py:11
  31.7 0.1 convert_reduce_fusion
  31.8 0.1 multiply_reduce_fusion.8
  31.9 0.2 multiply_reduce_fusion.7
  32.1 0.5 multiply_reduce_fusion.5
  32.7 0.3 convert_reduce_fusion.1
  33.0 0.2 fusion.79
  33.2 0.2 multiply_reduce_fusion.4
  33.4 0.6 %multiply_reduce_fusion.6 = (f32[8]{0:T(128)S(1)}, f32[8,768]{1,0:T(8,128)S(1)}) fusion(f32[8,768]{1,0:T(8,128)S(1)} %convert_reduce_fusion, f32[8]{0:T(128)S(1)} %broadcast_multiply_fusion.4, bf16[768,1024]{1,0:T(8,128)(2,1)S(1)} %copy-done.2, f32[8,1024]{1,0:T(8,128)S(1)} %get-tuple-element.71, f32[8,1024]{1,0:T(8,128)S(1)} %get-tuple-element.75, ...), kind=kOutput, calls=%fused_computation.165 | convolution fusion | flops 12652536 | bytes 1687680 | tf_op jit(solution)/shard_map/transpose(jvp())/dot_general | solution.py:68
  34.1 0.2 fusion.96
  34.3 0.1 add_multiply_fusion
  34.4 1.1 %fusion.46 = bf16[128,1536]{1,0:T(8,128)(2,1)S(1)} fusion(f32[128,1536]{1,0:T(8,128)S(1)} %fusion.12, bf16[1,1536,768]{2,1,0:T(8,128)(2,1)S(1)} %copy-done, f32[8,768]{1,0:T(8,128)S(1)} %add_multiply_fusion), kind=kOutput, calls=%fused_computation.45 | convolution fusion | flops 306118656 | bytes 3563520 | tf_op jit(solution)/shard_map/transpose(jvp())/dot_general | solution.py:49
  35.4 0.6 %copy-done.1 = bf16[1,768,1536]{2,1,0:T(8,128)(2,1)S(1)} copy-done((bf16[1,768,1536]{2,1,0:T(8,128)(2,1)S(1)}, bf16[1,768,1536]{2,1,0:T(8,128)(2,1)}, u32[]{:S(2)}) %copy-start.1) | copy-done | bytes 2359320
  36.0 0.9 %fusion.28 = bf16[16,8,768]{2,1,0:T(8,128)(2,1)S(1)} fusion(bf16[128,1536]{1,0:T(8,128)(2,1)S(1)} %fusion.46, bf16[1,768,1536]{2,1,0:T(8,128)(2,1)S(1)} %copy-done.1), kind=kOutput, calls=%fused_computation.22 | convolution fusion | flops 301989888 | bytes 2949120 | tf_op jit(solution)/shard_map/transpose(jvp())/dot_general | solution.py:44
  36.9 1.6 %collective-permute-start.6 = (bf16[16,8,768]{2,1,0:T(8,128)(2,1)S(1)}, bf16[16,8,768]{2,1,0:T(8,128)(2,1)S(1)}, u32[]{:S(2)}, u32[]{:S(2)}) collective-permute-start(bf16[16,8,768]{2,1,0:T(8,128)(2,1)S(1)} %fusion.28), channel_id=1, source_target_pairs={{0,1},{1,0},{2,3},{3,2},{4,5},{5,4},{6,7},{7,6},{8,9},{9,8},{10,11... | collective-permute-start | bytes 589832 | tf_op jit(solution)/shard_map/ppermute | solution.py:11
  38.5 4.3 %collective-permute-done.6 = bf16[16,8,768]{2,1,0:T(8,128)(2,1)S(1)} collective-permute-done((bf16[16,8,768]{2,1,0:T(8,128)(2,1)S(1)}, bf16[16,8,768]{2,1,0:T(8,128)(2,1)S(1)}, u32[]{:S(2)}, u32[]{:S(2)}) %collective-permute-start.6) | collective-permute-done | bytes 196640 | tf_op jit(solution)/shard_map/ppermute | solution.py:11
  42.8 0.2 multiply_reduce_fusion.1
  43.0 0.2 fusion.64
  43.3 0.2 broadcast_add_fusion.1
  44.4 0.7 %copy-done.3 = f32[16,8,768]{2,1,0:T(8,128)} copy-done((f32[16,8,768]{2,1,0:T(8,128)}, f32[16,8,768]{2,1,0:T(8,128)S(1)}, u32[]{:S(2)}) %copy-start.3) | copy-done | bytes 393240
  45.3 1.4 %collective-permute-done.7 = bf16[16,8,768]{2,1,0:T(8,128)(2,1)S(1)} collective-permute-done((bf16[16,8,768]{2,1,0:T(8,128)(2,1)S(1)}, bf16[16,8,768]{2,1,0:T(8,128)(2,1)S(1)}, u32[]{:S(2)}, u32[]{:S(2)}) %collective-permute-start.7) | collective-permute-done | bytes 196640 | tf_op jit(solution)/shard_map/ppermute | solution.py:11
  46.7 1.1 %fusion.40 = bf16[128,1536]{1,0:T(8,128)(2,1)S(1)} fusion(f32[128,1536]{1,0:T(8,128)S(1)} %copy-done.6, bf16[1,1536,768]{2,1,0:T(8,128)(2,1)S(1)} %copy-done, bf16[16,8,768]{2,1,0:T(8,128)(2,1)S(1)} %collective-permute-done.7), kind=kOutput, calls=%fused_computation.39 | convolution fusion | flops 306315264 | bytes 3735552 | tf_op jit(solution)/shard_map/transpose(jvp())/dot_general | solution.py:49
  47.8 0.9 %fusion.25 = bf16[16,8,768]{2,1,0:T(8,128)(2,1)S(1)} fusion(bf16[128,1536]{1,0:T(8,128)(2,1)S(1)} %fusion.40, bf16[1,768,1536]{2,1,0:T(8,128)(2,1)S(1)} %copy-done.1), kind=kOutput, calls=%fused_computation.21 | convolution fusion | flops 301989888 | bytes 2949120 | tf_op jit(solution)/shard_map/transpose(jvp())/dot_general | solution.py:44
  48.7 1.6 %collective-permute-start.8 = (bf16[16,8,768]{2,1,0:T(8,128)(2,1)S(1)}, bf16[16,8,768]{2,1,0:T(8,128)(2,1)S(1)}, u32[]{:S(2)}, u32[]{:S(2)}) collective-permute-start(bf16[16,8,768]{2,1,0:T(8,128)(2,1)S(1)} %fusion.25), channel_id=1, source_target_pairs={{0,1},{1,0},{2,3},{3,2},{4,5},{5,4},{6,7},{7,6},{8,9},{9,8},{10,11... | collective-permute-start | bytes 589832 | tf_op jit(solution)/shard_map/ppermute | solution.py:11
  50.2 5.4 %collective-permute-done.8 = bf16[16,8,768]{2,1,0:T(8,128)(2,1)S(1)} collective-permute-done((bf16[16,8,768]{2,1,0:T(8,128)(2,1)S(1)}, bf16[16,8,768]{2,1,0:T(8,128)(2,1)S(1)}, u32[]{:S(2)}, u32[]{:S(2)}) %collective-permute-start.8) | collective-permute-done | bytes 196640 | tf_op jit(solution)/shard_map/ppermute | solution.py:11
  55.7 0.2 multiply_reduce_fusion
  55.9 0.3 fusion.65
  56.2 0.2 broadcast_add_fusion
  57.3 0.4 copy-done.4
  57.7 0.1 add_select_fusion
  57.8 0.9 %copy.10 = f32[1,8,4,4,768]{4,3,2,1,0:T(4,128)} copy(f32[1,8,4,4,768]{4,1,3,2,0:T(8,128)S(1)} %bitcast.90) | data formatting | bytes 786432 | tf_op jit(solution)/shard_map/broadcast_in_dim;reshape | solution.py:213
  (127 shorter events, 4.1 us)
Async XLA Ops:
  0.0 6.5 %copy-start = (bf16[1,1536,768]{2,1,0:T(8,128)(2,1)S(1)}, bf16[1,1536,768]{2,1,0:T(8,128)(2,1)}, u32[]{:S(2)}) copy-start(bf16[1,1536,768]{2,1,0:T(8,128)(2,1)} %param.12) | copy-start | bytes 7077892
  1.3 2.0 %copy-start.10 = (f32[768]{0:T(1024)}, f32[768]{0:T(1024)S(1)}, u32[]{:S(2)}) copy-start(f32[768]{0:T(1024)S(1)} %get-tuple-element.21) | copy-start | bytes 9220
  1.3 2.2 %copy-start.13 = (f32[768]{0:T(1024)}, f32[768]{0:T(1024)S(1)}, u32[]{:S(2)}) copy-start(f32[768]{0:T(1024)S(1)} %get-tuple-element.18) | copy-start | bytes 9220
  3.0 0.8 %copy-start.19 = (f32[1,768]{1,0:T(1,128)S(1)}, f32[1,768]{1,0:T(1,128)}, u32[]{:S(2)}) copy-start(f32[1,768]{1,0:T(1,128)} %param.10) | copy-start | bytes 9220
  3.8 0.6 %copy-start.16 = (f32[16,8]{1,0:T(8,128)}, f32[16,8]{1,0:T(8,128)S(1)}, u32[]{:S(2)}) copy-start(f32[16,8]{1,0:T(8,128)S(1)} %multiply_reduce_fusion.3) | copy-start | bytes 1540
  6.5 9.3 %copy-start.5 = (f32[128,1536]{1,0:T(8,128)}, f32[128,1536]{1,0:T(8,128)S(1)}, u32[]{:S(2)}) copy-start(f32[128,1536]{1,0:T(8,128)S(1)} %fusion.14) | copy-start | bytes 2359300
  6.6 3.7 %copy-start.18 = (bf16[8,1024]{1,0:T(8,128)(2,1)S(1)}, bf16[8,1024]{1,0:T(8,128)(2,1)}, u32[]{:S(2)}) copy-start(bf16[8,1024]{1,0:T(8,128)(2,1)} %param.14) | copy-start | bytes 49156
  7.2 8.0 %collective-permute-start = (bf16[16,8,768]{2,1,0:T(8,128)(2,1)S(1)}, bf16[16,8,768]{2,1,0:T(8,128)(2,1)S(1)}, u32[]{:S(2)}, u32[]{:S(2)}) collective-permute-start(bf16[16,8,768]{2,1,0:T(8,128)(2,1)S(1)} %fusion.16), channel_id=1, source_target_pairs={{0,1},{1,0},{2,3},{3,2},{4,5},{5,4},{6,7},{7,6},{8,9},{9,8},{10,11... | collective-permute-start | bytes 589832 | tf_op jit(solution)/shard_map/ppermute | solution.py:11
  10.4 3.7 %collective-permute-start.1 = (bf16[8,1024]{1,0:T(8,128)(2,1)S(1)}, bf16[8,1024]{1,0:T(8,128)(2,1)S(1)}, u32[]{:S(2)}, u32[]{:S(2)}) collective-permute-start(bf16[8,1024]{1,0:T(8,128)(2,1)S(1)} %fusion.67), channel_id=1, source_target_pairs={{0,4},{4,0},{8,12},{12,8},{16,20},{20,16},{24,28},{28,24},{1,5},{5... | collective-permute-start | bytes 49160 | tf_op jit(solution)/shard_map/ppermute | solution.py:11
  15.9 1.7 %collective-permute-start.2 = (bf16[16,8,768]{2,1,0:T(8,128)(2,1)}, bf16[16,8,768]{2,1,0:T(8,128)(2,1)S(1)}, u32[]{:S(2)}, u32[]{:S(2)}) collective-permute-start(bf16[16,8,768]{2,1,0:T(8,128)(2,1)} %add_convert_fusion.4), channel_id=1, source_target_pairs={{0,2},{2,0},{1,3},{3,1},{4,6},{6,4},{5,7},{7,5},{8,10},{10,8},{9,1... | collective-permute-start | bytes 589832 | tf_op jit(solution)/shard_map/ppermute | solution.py:11
  17.7 0.7 %copy-start.11 = (f32[768]{0:T(1024)S(1)}, f32[768]{0:T(1024)}, u32[]{:S(2)}) copy-start(f32[768]{0:T(1024)} %copy-done.10) | copy-start | bytes 9220
  17.9 0.7 %copy-start.14 = (f32[768]{0:T(1024)S(1)}, f32[768]{0:T(1024)}, u32[]{:S(2)}) copy-start(f32[768]{0:T(1024)} %copy-done.13) | copy-start | bytes 9220
  22.5 0.8 %copy-start.7 = (bf16[16,1024]{1,0:T(8,128)(2,1)S(1)}, bf16[16,1024]{1,0:T(8,128)(2,1)}, u32[]{:S(2)}) copy-start(bf16[16,1024]{1,0:T(8,128)(2,1)} %pad_maximum_fusion.1) | copy-start | bytes 98308
  22.5 9.6 %copy-start.2 = (bf16[768,1024]{1,0:T(8,128)(2,1)S(1)}, bf16[768,1024]{1,0:T(8,128)(2,1)}, u32[]{:S(2)}) copy-start(bf16[768,1024]{1,0:T(8,128)(2,1)} %param.13) | copy-start | bytes 4718596
  23.2 9.7 %copy-start.20 = (s32[8]{0:T(128)S(1)}, s32[8]{0:T(128)}, u32[]{:S(2)}) copy-start(s32[8]{0:T(128)} %param.15) | copy-start | bytes 100
  23.2 9.7 %copy-start.21 = (s32[64]{0:T(128)S(1)}, s32[64]{0:T(128)}, u32[]{:S(2)}) copy-start(s32[64]{0:T(128)} %fusion.83) | copy-start | bytes 772
  23.2 3.9 %collective-permute-start.4 = (bf16[16,1024]{1,0:T(8,128)(2,1)S(1)}, bf16[16,1024]{1,0:T(8,128)(2,1)S(1)}, u32[]{:S(2)}, u32[]{:S(2)}) collective-permute-start(bf16[16,1024]{1,0:T(8,128)(2,1)S(1)} %copy-done.7), channel_id=1, source_target_pairs={{0,8},{4,12},{8,0},{12,4},{16,24},{20,28},{24,16},{28,20},{1,9},{5... | collective-permute-start | bytes 98312 | tf_op jit(solution)/shard_map/ppermute | solution.py:11
  25.0 6.7 %collective-permute-start.3 = (bf16[16,8,768]{2,1,0:T(8,128)(2,1)S(1)}, bf16[16,8,768]{2,1,0:T(8,128)(2,1)S(1)}, u32[]{:S(2)}, u32[]{:S(2)}) collective-permute-start(bf16[16,8,768]{2,1,0:T(8,128)(2,1)S(1)} %fusion.2), channel_id=1, source_target_pairs={{0,1},{1,0},{2,3},{3,2},{4,5},{5,4},{6,7},{7,6},{8,9},{9,8},{10,11... | collective-permute-start | bytes 589832 | tf_op jit(solution)/shard_map/ppermute | solution.py:11
  27.1 5.5 %collective-permute-start.5 = (bf16[32,1024]{1,0:T(8,128)(2,1)S(1)}, bf16[32,1024]{1,0:T(8,128)(2,1)S(1)}, u32[]{:S(2)}, u32[]{:S(2)}) collective-permute-start(bf16[32,1024]{1,0:T(8,128)(2,1)S(1)} %pad_maximum_fusion), channel_id=1, source_target_pairs={{0,16},{4,20},{8,24},{12,28},{16,0},{20,4},{24,8},{28,12},{1,17},{... | collective-permute-start | bytes 196616 | tf_op jit(solution)/shard_map/ppermute | solution.py:11
  34.4 1.7 %copy-start.1 = (bf16[1,768,1536]{2,1,0:T(8,128)(2,1)S(1)}, bf16[1,768,1536]{2,1,0:T(8,128)(2,1)}, u32[]{:S(2)}) copy-start(bf16[1,768,1536]{2,1,0:T(8,128)(2,1)} %param.11) | copy-start | bytes 7077892
  36.0 7.4 %copy-start.15 = (f32[768]{0:T(1024)S(1)}, f32[768]{0:T(1024)}, u32[]{:S(2)}) copy-start(f32[768]{0:T(1024)} %copy-done.13) | copy-start | bytes 9220
  36.9 6.7 %copy-start.12 = (f32[768]{0:T(1024)S(1)}, f32[768]{0:T(1024)}, u32[]{:S(2)}) copy-start(f32[768]{0:T(1024)} %copy-done.10) | copy-start | bytes 9220
  36.9 5.9 %collective-permute-start.6 = (bf16[16,8,768]{2,1,0:T(8,128)(2,1)S(1)}, bf16[16,8,768]{2,1,0:T(8,128)(2,1)S(1)}, u32[]{:S(2)}, u32[]{:S(2)}) collective-permute-start(bf16[16,8,768]{2,1,0:T(8,128)(2,1)S(1)} %fusion.28), channel_id=1, source_target_pairs={{0,1},{1,0},{2,3},{3,2},{4,5},{5,4},{6,7},{7,6},{8,9},{9,8},{10,11... | collective-permute-start | bytes 589832 | tf_op jit(solution)/shard_map/ppermute | solution.py:11
  43.9 2.8 %copy-start.6 = (f32[128,1536]{1,0:T(8,128)S(1)}, f32[128,1536]{1,0:T(8,128)}, u32[]{:S(2)}) copy-start(f32[128,1536]{1,0:T(8,128)} %copy-done.5) | copy-start | bytes 2359300
  44.4 0.7 %copy-start.3 = (f32[16,8,768]{2,1,0:T(8,128)}, f32[16,8,768]{2,1,0:T(8,128)S(1)}, u32[]{:S(2)}) copy-start(f32[16,8,768]{2,1,0:T(8,128)S(1)} %constant_dynamic-update-slice_fusion.35) | copy-start | bytes 1179652
  45.2 1.5 %collective-permute-start.7 = (bf16[16,8,768]{2,1,0:T(8,128)(2,1)S(1)}, bf16[16,8,768]{2,1,0:T(8,128)(2,1)S(1)}, u32[]{:S(2)}, u32[]{:S(2)}) collective-permute-start(bf16[16,8,768]{2,1,0:T(8,128)(2,1)S(1)} %add_convert_fusion.6), channel_id=1, source_target_pairs={{0,2},{2,0},{1,3},{3,1},{4,6},{6,4},{5,7},{7,5},{8,10},{10,8},{9,1... | collective-permute-start | bytes 589832 | tf_op jit(solution)/shard_map/ppermute | solution.py:11
  46.7 1.1 %copy-start.8 = (bf16[16,8,768]{2,1,0:T(8,128)(2,1)}, bf16[16,8,768]{2,1,0:T(8,128)(2,1)S(1)}, u32[]{:S(2)}) copy-start(bf16[16,8,768]{2,1,0:T(8,128)(2,1)S(1)} %collective-permute-done.7) | copy-start | bytes 589828
  47.8 8.1 %copy-start.17 = (f32[16,8]{1,0:T(8,128)S(1)}, f32[16,8]{1,0:T(8,128)}, u32[]{:S(2)}) copy-start(f32[16,8]{1,0:T(8,128)} %copy-done.16) | copy-start | bytes 1540
  48.7 7.0 %collective-permute-start.8 = (bf16[16,8,768]{2,1,0:T(8,128)(2,1)S(1)}, bf16[16,8,768]{2,1,0:T(8,128)(2,1)S(1)}, u32[]{:S(2)}, u32[]{:S(2)}) collective-permute-start(bf16[16,8,768]{2,1,0:T(8,128)(2,1)S(1)} %fusion.25), channel_id=1, source_target_pairs={{0,1},{1,0},{2,3},{3,2},{4,5},{5,4},{6,7},{7,6},{8,9},{9,8},{10,11... | collective-permute-start | bytes 589832 | tf_op jit(solution)/shard_map/ppermute | solution.py:11
  56.7 1.0 %copy-start.4 = (f32[16,8,768]{2,1,0:T(8,128)S(1)}, f32[16,8,768]{2,1,0:T(8,128)}, u32[]{:S(2)}) copy-start(f32[16,8,768]{2,1,0:T(8,128)} %copy-done.3) | copy-start | bytes 1179652
  56.7 1.0 %copy-start.9 = (bf16[16,8,768]{2,1,0:T(8,128)(2,1)S(1)}, bf16[16,8,768]{2,1,0:T(8,128)(2,1)}, u32[]{:S(2)}) copy-start(bf16[16,8,768]{2,1,0:T(8,128)(2,1)} %copy-done.8) | copy-start | bytes 589828

commit v9 on v8

--- a/solution.py
+++ b/solution.py
@@ -52,10 +52,16 @@
 def mlp_part(normed, expand, project_out):
     low = lax.optimization_barrier(normed.astype(jnp.bfloat16))
     pre, expand_back = jax.vjp(lambda inner: expand_part(inner, expand), low)
-    branch, project_back = jax.vjp(lambda inner: project_part(inner, project_out, normed.shape), pre)
+    hidden = jax.nn.gelu(pre).astype(jnp.bfloat16)
+    branch, hidden_back = jax.vjp(
+        lambda inner: jnp.dot(inner, project_out, preferred_element_type=jnp.float32).reshape(normed.shape),
+        hidden,
+    )
+    slope = lax.optimization_barrier(jax.jvp(jax.nn.gelu, (pre,), (jnp.ones_like(pre),))[1])
 
     def mlp_back(cotangent):
-        (pre_grad,) = project_back(cotangent)
+        (hidden_grad,) = hidden_back(cotangent)
+        pre_grad = hidden_grad.astype(jnp.float32) * slope
         (low_grad,) = expand_back(lax.optimization_barrier(pre_grad))
         return (low_grad.astype(jnp.float32),)
 

time: 59.1 us -> 57.6 us (0.975)
  matrix products: 11.1 us -> 8.93 us
  other arithmetic: 10 us -> 11.6 us
  local copies, waits for them, and re-layouts: 5.92 us -> 4.85 us
    dot_general x4, matrix products: 6.02 us -> 4.11 us  [expand_part(): return jnp.dot(flattened, expand, preferred_element_type=jnp.float32)]
    unnamed x47 -> x49, local copies, waits for them, and re-layouts: 3.59 us -> 2.52 us
    add_any x2, other arithmetic: 0.36 us -> 1.07 us  [normalize_last(): centred = values - jnp.mean(values, axis=-1, keepdims=True)]
    reduce_sum x2, other arithmetic: 0.38 us -> 1.08 us  [normalize_last(): return centred * lax.rsqrt(variance + 1e-06)]
    div x6, other arithmetic: 0.72 us -> 0.03 us  [normalize_last(): centred = values - jnp.mean(values, axis=-1, keepdims=True)]
    div x3, other arithmetic: 0.04 us -> 0.73 us  [normalize_last(): variance = jnp.mean(centred * centred, axis=-1, keepdims=True)]
where the time goes in v9:
time: 57.6 us; the launch traced here: 57.1 us
  waiting for transfers between devices  17.1 us (30%)
  starting transfers between devices  14 us (24%)
  other arithmetic  11.6 us (20%)
  matrix products  8.93 us (16%)
  local copies, waits for them, and re-layouts  4.85 us (8%)
  between operations  0.58 us (1%)
    ppermute x9, waiting for transfers between devices, swapped(): lax.ppermute(value, axis, [(i, i ^ 1 << stride) for i in range(lax.axis_s...  17.1 us
    ppermute x9, starting transfers between devices, swapped(): lax.ppermute(value, axis, [(i, i ^ 1 << stride) for i in range(lax.axis_s...  14 us
    dot_general x4, matrix products, expand_part(): return jnp.dot(flattened, expand, preferred_element_type=jnp.float32)  4.11 us
    unnamed x61, other arithmetic  3.38 us
    dot_general x4, matrix products, mlp_part(): jnp.dot(inner, project_out, preferred_element_type=jnp.float32)  3.01 us
    unnamed x49, local copies, waits for them, and re-layouts  2.52 us
    reduce_sum x6, other arithmetic, normalize_last(): centred = values - jnp.mean(values, axis=-1, keepdims=True)  1.73 us
  transfers between devices with their start and end apart: 9, of which 8 were waited for; matrix products, arithmetic and copies ran while one was open for 4% of the time, Pallas kernels for 0%

profile of v9, /device:TPU:0, one launch (start us, length us, event | category | flops | bytes accessed | tf_op | source)
XLA Modules:
  0.0 57.1 jit_solution(8998931581289478988)
XLA Ops:
  0.0 1.1 %copy.13 = f32[1,7,7,768]{3,2,0,1:T(8,128)S(1)} copy(f32[1,7,7,768]{3,0,2,1:T(1,128)} %param.9) | data formatting | bytes 301056
  1.1 0.2 slice_reduce_fusion.5
  1.3 0.2 slice_reduce_fusion.19
  1.5 0.1 slice_reduce_fusion.47
  1.6 1.0 %copy.9 = f32[8,4,4,768]{3,0,2,1:T(8,128)S(1)} copy(bf16[8,4,4,768]{3,2,1,0:T(4,128)(2,1)} %param.8) | data formatting | bytes 589824 | tf_op jit(solution)/shard_map/convert_element_type | solution.py:123
  2.8 0.1 constant_dynamic-update-slice_fusion.10
  3.5 0.1 reduce_sum.148
  3.6 0.2 multiply_reduce_fusion.3
  3.9 0.1 multiply_convert_fusion.5
  4.0 1.6 %fusion.46 = (f32[128,1536]{1,0:T(8,128)}, f32[128,1536]{1,0:T(8,128)S(1)}) fusion(bf16[1,768,1536]{2,1,0:T(8,128)(2,1)S(1)} %copy-done, bf16[16,8,768]{2,1,0:T(8,128)(2,1)S(1)} %multiply_convert_fusion.5), kind=kOutput, calls=%fused_computation.45 | convolution fusion | flops 305135616 | bytes 4128768 | tf_op jit(solution)/shard_map/jvp()/dot_general | solution.py:44
  5.7 0.6 %fusion.18 = bf16[16,8,768]{2,1,0:T(8,128)(2,1)S(1)} fusion(bf16[1,1536,768]{2,1,0:T(8,128)(2,1)S(1)} %copy-done.1, f32[128,1536]{1,0:T(8,128)S(1)} %get-tuple-element.71), kind=kOutput, calls=%fused_computation.20 | convolution fusion | flops 303857664 | bytes 3342336 | tf_op jit(solution)/shard_map/jvp()/dot_general | solution.py:57
  6.3 3.1 %collective-permute-start = (bf16[16,8,768]{2,1,0:T(8,128)(2,1)S(1)}, bf16[16,8,768]{2,1,0:T(8,128)(2,1)S(1)}, u32[]{:S(2)}, u32[]{:S(2)}) collective-permute-start(bf16[16,8,768]{2,1,0:T(8,128)(2,1)S(1)} %fusion.18), channel_id=1, source_target_pairs={{0,1},{1,0},{2,3},{3,2},{4,5},{5,4},{6,7},{7,6},{8,9},{9,8},{10,11... | collective-permute-start | bytes 589832 | tf_op jit(solution)/shard_map/ppermute | solution.py:11
  9.4 0.1 fusion.72
  9.5 0.1 fusion.73
  9.6 1.5 %collective-permute-start.1 = (bf16[8,1024]{1,0:T(8,128)(2,1)S(1)}, bf16[8,1024]{1,0:T(8,128)(2,1)S(1)}, u32[]{:S(2)}, u32[]{:S(2)}) collective-permute-start(bf16[8,1024]{1,0:T(8,128)(2,1)S(1)} %fusion.73), channel_id=1, source_target_pairs={{0,4},{4,0},{8,12},{12,8},{16,20},{20,16},{24,28},{28,24},{1,5},{5... | collective-permute-start | bytes 49160 | tf_op jit(solution)/shard_map/ppermute | solution.py:11
  11.1 2.2 %collective-permute-done.1 = bf16[8,1024]{1,0:T(8,128)(2,1)S(1)} collective-permute-done((bf16[8,1024]{1,0:T(8,128)(2,1)S(1)}, bf16[8,1024]{1,0:T(8,128)(2,1)S(1)}, u32[]{:S(2)}, u32[]{:S(2)}) %collective-permute-start.1) | collective-permute-done | bytes 16416 | tf_op jit(solution)/shard_map/ppermute | solution.py:11
  13.3 0.6 %pad_maximum_fusion.1 = bf16[16,1024]{1,0:T(8,128)(2,1)} fusion(bf16[8,1024]{1,0:T(8,128)(2,1)S(1)} %collective-permute-done.1, bf16[8,1024]{1,0:T(8,128)(2,1)S(1)} %fusion.73), kind=kLoop, calls=%fused_computation.169 | loop fusion | flops 65536 | bytes 65536 | tf_op jit(solution)/shard_map/concatenate | solution.py:168
  13.9 0.3 collective-permute-done
  14.3 0.7 %add_convert_fusion.4 = bf16[16,8,768]{2,1,0:T(8,128)(2,1)} fusion(bf16[16,8,768]{2,1,0:T(8,128)(2,1)S(1)} %collective-permute-done, bf16[16,8,768]{2,1,0:T(8,128)(2,1)S(1)} %fusion.18, f32[8,4,4,768]{3,0,2,1:T(8,128)S(1)} %copy.9), kind=kLoop, calls=%fused_computation.75 | loop fusion | flops 688128 | bytes 983040 | tf_op jit(solution)/shard_map/convert_element_type | solution.py:129
  15.0 0.6 %fusion.89 = s32[64]{0:T(128)} fusion(s32[]{:T(128)S(6)} %axis_index.28), kind=kLoop, calls=%fused_computation.257 | loop fusion | flops 960 | bytes 260 | tf_op jit(solution)/shard_map/add | solution.py:103
  15.6 1.1 %collective-permute-done.2 = bf16[16,8,768]{2,1,0:T(8,128)(2,1)S(1)} collective-permute-done((bf16[16,8,768]{2,1,0:T(8,128)(2,1)}, bf16[16,8,768]{2,1,0:T(8,128)(2,1)S(1)}, u32[]{:S(2)}, u32[]{:S(2)}) %collective-permute-start.2) | collective-permute-done | bytes 196640 | tf_op jit(solution)/shard_map/ppermute | solution.py:11
  17.6 0.1 reduce_sum.154
  17.7 0.2 multiply_reduce_fusion.2
  17.9 0.1 multiply_convert_fusion.2
  18.1 0.7 %fusion.56 = (f32[128,1536]{1,0:T(8,128)S(1)}, f32[128,1536]{1,0:T(8,128)S(1)}) fusion(bf16[1,768,1536]{2,1,0:T(8,128)(2,1)S(1)} %copy-done, bf16[16,8,768]{2,1,0:T(8,128)(2,1)S(1)} %multiply_convert_fusion.2), kind=kOutput, calls=%fused_computation.55 | convolution fusion | flops 305135616 | bytes 4128768 | tf_op jit(solution)/shard_map/jvp()/dot_general | solution.py:44
  18.8 0.9 %copy-done.2 = bf16[1,1536,768]{2,1,0:T(8,128)(2,1)S(1)} copy-done((bf16[1,1536,768]{2,1,0:T(8,128)(2,1)S(1)}, bf16[1,1536,768]{2,1,0:T(8,128)(2,1)}, u32[]{:S(2)}) %copy-start.2) | copy-done | bytes 2359320
  19.7 0.6 %fusion.4 = bf16[16,8,768]{2,1,0:T(8,128)(2,1)S(1)} fusion(bf16[1,1536,768]{2,1,0:T(8,128)(2,1)S(1)} %copy-done.2, f32[128,1536]{1,0:T(8,128)S(1)} %get-tuple-element.73), kind=kOutput, calls=%fused_computation.6 | convolution fusion | flops 303759360 | bytes 3342336 | tf_op jit(solution)/shard_map/jvp()/dot_general | solution.py:57
  20.4 1.9 %collective-permute-start.4 = (bf16[16,1024]{1,0:T(8,128)(2,1)S(1)}, bf16[16,1024]{1,0:T(8,128)(2,1)S(1)}, u32[]{:S(2)}, u32[]{:S(2)}) collective-permute-start(bf16[16,1024]{1,0:T(8,128)(2,1)S(1)} %copy-done.8), channel_id=1, source_target_pairs={{0,8},{4,12},{8,0},{12,4},{16,24},{20,28},{24,16},{28,20},{1,9},{5... | collective-permute-start | bytes 98312 | tf_op jit(solution)/shard_map/ppermute | solution.py:11
  22.3 1.5 %collective-permute-start.3 = (bf16[16,8,768]{2,1,0:T(8,128)(2,1)S(1)}, bf16[16,8,768]{2,1,0:T(8,128)(2,1)S(1)}, u32[]{:S(2)}, u32[]{:S(2)}) collective-permute-start(bf16[16,8,768]{2,1,0:T(8,128)(2,1)S(1)} %fusion.4), channel_id=1, source_target_pairs={{0,1},{1,0},{2,3},{3,2},{4,5},{5,4},{6,7},{7,6},{8,9},{9,8},{10,11... | collective-permute-start | bytes 589832 | tf_op jit(solution)/shard_map/ppermute | solution.py:11
  23.8 0.6 %collective-permute-done.4 = bf16[16,1024]{1,0:T(8,128)(2,1)S(1)} collective-permute-done((bf16[16,1024]{1,0:T(8,128)(2,1)S(1)}, bf16[16,1024]{1,0:T(8,128)(2,1)S(1)}, u32[]{:S(2)}, u32[]{:S(2)}) %collective-permute-start.4) | collective-permute-done | bytes 32800 | tf_op jit(solution)/shard_map/ppermute | solution.py:11
  24.4 2.8 %collective-permute-start.5 = (bf16[32,1024]{1,0:T(8,128)(2,1)S(1)}, bf16[32,1024]{1,0:T(8,128)(2,1)S(1)}, u32[]{:S(2)}, u32[]{:S(2)}) collective-permute-start(bf16[32,1024]{1,0:T(8,128)(2,1)S(1)} %pad_maximum_fusion), channel_id=1, source_target_pairs={{0,16},{4,20},{8,24},{12,28},{16,0},{20,4},{24,8},{28,12},{1,17},{... | collective-permute-start | bytes 196616 | tf_op jit(solution)/shard_map/ppermute | solution.py:11
  27.2 1.7 %collective-permute-done.3 = bf16[16,8,768]{2,1,0:T(8,128)(2,1)S(1)} collective-permute-done((bf16[16,8,768]{2,1,0:T(8,128)(2,1)S(1)}, bf16[16,8,768]{2,1,0:T(8,128)(2,1)S(1)}, u32[]{:S(2)}, u32[]{:S(2)}) %collective-permute-start.3) | collective-permute-done | bytes 196640 | tf_op jit(solution)/shard_map/ppermute | solution.py:11
  28.9 0.1 convert_reduce_fusion
  29.0 0.1 multiply_reduce_fusion.8
  29.1 0.2 multiply_reduce_fusion.7
  29.3 0.5 multiply_reduce_fusion.5
  29.8 0.1 broadcast_multiply_fusion
  29.9 0.3 convert_reduce_fusion.1
  30.2 0.2 fusion.85
  30.4 0.2 multiply_reduce_fusion.4
  30.7 0.6 %multiply_reduce_fusion.6 = (f32[8]{0:T(128)S(1)}, f32[8,768]{1,0:T(8,128)S(1)}) fusion(f32[8,768]{1,0:T(8,128)S(1)} %convert_reduce_fusion, f32[8]{0:T(128)S(1)} %broadcast_multiply_fusion.4, bf16[768,1024]{1,0:T(8,128)(2,1)S(1)} %copy-done.3, f32[8,1024]{1,0:T(8,128)S(1)} %get-tuple-element.75, f32[8,1024]{1,0:T(8,128)S(1)} %get-tuple-element.79, ...), kind=kOutput, calls=%fused_computation.175 | convolution fusion | flops 12652536 | bytes 1687680 | tf_op jit(solution)/shard_map/transpose(jvp())/dot_general | solution.py:74
  31.3 0.2 fusion.102
  31.5 0.1 add_multiply_fusion
  31.6 0.9 %fusion.3 = bf16[128,1536]{1,0:T(8,128)(2,1)S(1)} fusion(f32[128,1536]{1,0:T(8,128)S(1)} %get-tuple-element.72, bf16[1,1536,768]{2,1,0:T(8,128)(2,1)S(1)} %copy-done.2, f32[8,768]{1,0:T(8,128)S(1)} %add_multiply_fusion), kind=kOutput, calls=%fused_computation.5 | convolution fusion | flops 302579712 | bytes 3563520 | tf_op jit(solution)/shard_map/transpose(jvp())/dot_general | solution.py:57
  32.5 0.9 %fusion.30 = bf16[16,8,768]{2,1,0:T(8,128)(2,1)S(1)} fusion(bf16[128,1536]{1,0:T(8,128)(2,1)S(1)} %fusion.3, bf16[1,768,1536]{2,1,0:T(8,128)(2,1)S(1)} %copy-done), kind=kOutput, calls=%fused_computation.24 | convolution fusion | flops 301989888 | bytes 2949120 | tf_op jit(solution)/shard_map/transpose(jvp())/dot_general | solution.py:44
  33.4 1.6 %collective-permute-start.6 = (bf16[16,8,768]{2,1,0:T(8,128)(2,1)S(1)}, bf16[16,8,768]{2,1,0:T(8,128)(2,1)S(1)}, u32[]{:S(2)}, u32[]{:S(2)}) collective-permute-start(bf16[16,8,768]{2,1,0:T(8,128)(2,1)S(1)} %fusion.30), channel_id=1, source_target_pairs={{0,1},{1,0},{2,3},{3,2},{4,5},{5,4},{6,7},{7,6},{8,9},{9,8},{10,11... | collective-permute-start | bytes 589832 | tf_op jit(solution)/shard_map/ppermute | solution.py:11
  35.0 4.3 %collective-permute-done.6 = bf16[16,8,768]{2,1,0:T(8,128)(2,1)S(1)} collective-permute-done((bf16[16,8,768]{2,1,0:T(8,128)(2,1)S(1)}, bf16[16,8,768]{2,1,0:T(8,128)(2,1)S(1)}, u32[]{:S(2)}, u32[]{:S(2)}) %collective-permute-start.6) | collective-permute-done | bytes 196640 | tf_op jit(solution)/shard_map/ppermute | solution.py:11
  39.3 0.2 multiply_reduce_fusion.1
  39.5 0.2 fusion.70
  39.7 0.2 broadcast_add_fusion.1
  40.9 0.1 collective-permute-start.7
  41.0 1.4 %collective-permute-done.7 = bf16[16,8,768]{2,1,0:T(8,128)(2,1)S(1)} collective-permute-done((bf16[16,8,768]{2,1,0:T(8,128)(2,1)S(1)}, bf16[16,8,768]{2,1,0:T(8,128)(2,1)S(1)}, u32[]{:S(2)}, u32[]{:S(2)}) %collective-permute-start.7) | collective-permute-done | bytes 196640 | tf_op jit(solution)/shard_map/ppermute | solution.py:11
  42.5 0.9 %fusion.1 = bf16[128,1536]{1,0:T(8,128)(2,1)S(1)} fusion(f32[128,1536]{1,0:T(8,128)S(1)} %copy-done.6, bf16[1,1536,768]{2,1,0:T(8,128)(2,1)S(1)} %copy-done.2, bf16[16,8,768]{2,1,0:T(8,128)(2,1)S(1)} %collective-permute-done.7), kind=kOutput, calls=%fused_computation.2 | convolution fusion | flops 302776320 | bytes 3735552 | tf_op jit(solution)/shard_map/transpose(jvp())/dot_general | solution.py:57
  43.4 0.9 %fusion.27 = bf16[16,8,768]{2,1,0:T(8,128)(2,1)S(1)} fusion(bf16[128,1536]{1,0:T(8,128)(2,1)S(1)} %fusion.1, bf16[1,768,1536]{2,1,0:T(8,128)(2,1)S(1)} %copy-done), kind=kOutput, calls=%fused_computation.23 | convolution fusion | flops 301989888 | bytes 2949120 | tf_op jit(solution)/shard_map/transpose(jvp())/dot_general | solution.py:44
  44.2 1.6 %collective-permute-start.8 = (bf16[16,8,768]{2,1,0:T(8,128)(2,1)S(1)}, bf16[16,8,768]{2,1,0:T(8,128)(2,1)S(1)}, u32[]{:S(2)}, u32[]{:S(2)}) collective-permute-start(bf16[16,8,768]{2,1,0:T(8,128)(2,1)S(1)} %fusion.27), channel_id=1, source_target_pairs={{0,1},{1,0},{2,3},{3,2},{4,5},{5,4},{6,7},{7,6},{8,9},{9,8},{10,11... | collective-permute-start | bytes 589832 | tf_op jit(solution)/shard_map/ppermute | solution.py:11
  45.8 5.4 %collective-permute-done.8 = bf16[16,8,768]{2,1,0:T(8,128)(2,1)S(1)} collective-permute-done((bf16[16,8,768]{2,1,0:T(8,128)(2,1)S(1)}, bf16[16,8,768]{2,1,0:T(8,128)(2,1)S(1)}, u32[]{:S(2)}, u32[]{:S(2)}) %collective-permute-start.8) | collective-permute-done | bytes 196640 | tf_op jit(solution)/shard_map/ppermute | solution.py:11
  51.2 0.9 %multiply_reduce_fusion = f32[16,8]{1,0:T(8,128)S(1)} fusion(f32[16,8,768]{2,1,0:T(8,128)S(1)} %constant_dynamic-update-slice_fusion, f32[768]{0:T(1024)S(1)} %reduce.49, f32[16,8]{1,0:T(8,128)} %copy-done.7, bf16[16,8,768]{2,1,0:T(8,128)(2,1)S(1)} %collective-permute-done.8, bf16[16,8,768]{2,1,0:T(8,128)(2,1)S(1)} %fusion.27), kind=kLoop, calls=%fused_computation.64 | loop fusion | flops 884608 | bytes 790528 | tf_op jit(solution)/shard_map/transpose(jvp())/reduce_sum | solution.py:35
  52.1 0.7 %multiply_multiply_fusion.4 = f32[16,8]{1,0:T(8,128)S(1)} fusion(f32[16,8]{1,0:T(8,128)S(1)} %multiply_reduce_fusion, f32[16,8]{1,0:T(8,128)} %copy-done.18), kind=kLoop, calls=%fused_computation.189 | loop fusion | flops 768 | bytes 1536 | tf_op jit(solution)/shard_map/transpose(jvp())/div | solution.py:34
  52.8 1.0 %fusion.71 = f32[16,8]{1,0:T(8,128)S(1)} fusion(f32[16,8]{1,0:T(8,128)S(1)} %multiply_multiply_fusion.4, f32[16,8,768]{2,1,0:T(8,128)S(1)} %constant_dynamic-update-slice_fusion, f32[16,8]{1,0:T(8,128)} %copy-done.7, f32[16,8]{1,0:T(8,128)} %copy-done.9, f32[768]{0:T(1024)S(1)} %reduce.49, bf16[16,8,768]{2,1,0:T(8,128)(2,1)S(1)} %collective-permute-done.8, ...), kind=kLoop, calls=%fused_computation.94 | loop fusion | flops 1179520 | bytes 791552 | tf_op jit(solution)/shard_map/transpose(jvp())/reduce_sum | solution.py:33
  53.8 0.9 %broadcast_add_fusion = f32[16,8,768]{2,1,0:T(8,128)S(1)} fusion(f32[16,8]{1,0:T(8,128)S(1)} %negate_multiply_fusion, f32[16,8]{1,0:T(8,128)S(1)} %multiply_multiply_fusion.4, f32[16,8,768]{2,1,0:T(8,128)S(1)} %constant_dynamic-update-slice_fusion, f32[16,8]{1,0:T(8,128)} %copy-done.7, f32[16,8]{1,0:T(8,128)} %copy-done.9, f32[768]{0:T(1024)S(1)} %reduce.49, ...), kind=kLoop, calls=%fused_computation.89 | loop fusion | flops 1179648 | bytes 1184768 | tf_op jit(solution)/shard_map/transpose(jvp())/add_any | solution.py:33
  55.5 0.1 copy-done.13
  55.8 0.3 copy-done.5
  56.1 0.1 add_select_fusion
  56.2 0.9 %copy.10 = f32[1,8,4,4,768]{4,3,2,1,0:T(4,128)} copy(f32[1,8,4,4,768]{4,1,3,2,0:T(8,128)S(1)} %bitcast.94) | data formatting | bytes 786432 | tf_op jit(solution)/shard_map/broadcast_in_dim;reshape | solution.py:219
  (129 shorter events, 3.9 us)
Async XLA Ops:
  0.0 4.0 %copy-start = (bf16[1,768,1536]{2,1,0:T(8,128)(2,1)S(1)}, bf16[1,768,1536]{2,1,0:T(8,128)(2,1)}, u32[]{:S(2)}) copy-start(bf16[1,768,1536]{2,1,0:T(8,128)(2,1)} %param.11) | copy-start | bytes 7077892
  1.3 38.7 %copy-start.16 = (f32[768]{0:T(1024)}, f32[768]{0:T(1024)S(1)}, u32[]{:S(2)}) copy-start(f32[768]{0:T(1024)S(1)} %get-tuple-element.18) | copy-start | bytes 9220
  1.3 38.8 %copy-start.14 = (f32[768]{0:T(1024)}, f32[768]{0:T(1024)S(1)}, u32[]{:S(2)}) copy-start(f32[768]{0:T(1024)S(1)} %get-tuple-element.21) | copy-start | bytes 9220
  1.4 39.2 %copy-start.12 = (f32[768]{0:T(1024)}, f32[768]{0:T(1024)S(1)}, u32[]{:S(2)}) copy-start(f32[768]{0:T(1024)S(1)} %get-tuple-element.38) | copy-start | bytes 9220
  1.5 39.4 %copy-start.10 = (f32[768]{0:T(1024)}, f32[768]{0:T(1024)S(1)}, u32[]{:S(2)}) copy-start(f32[768]{0:T(1024)S(1)} %get-tuple-element.50) | copy-start | bytes 9220
  3.0 0.8 %copy-start.20 = (f32[1,768]{1,0:T(1,128)S(1)}, f32[1,768]{1,0:T(1,128)}, u32[]{:S(2)}) copy-start(f32[1,768]{1,0:T(1,128)} %param.10) | copy-start | bytes 9220
  3.6 2.0 %copy-start.7 = (f32[16,8]{1,0:T(8,128)}, f32[16,8]{1,0:T(8,128)S(1)}, u32[]{:S(2)}) copy-start(f32[16,8]{1,0:T(8,128)S(1)} %broadcast_multiply_fusion.2) | copy-start | bytes 1540
  3.8 10.5 %copy-start.18 = (f32[16,8]{1,0:T(8,128)}, f32[16,8]{1,0:T(8,128)S(1)}, u32[]{:S(2)}) copy-start(f32[16,8]{1,0:T(8,128)S(1)} %multiply_reduce_fusion.3) | copy-start | bytes 1540
  3.8 1.8 %copy-start.9 = (f32[16,8]{1,0:T(8,128)}, f32[16,8]{1,0:T(8,128)S(1)}, u32[]{:S(2)}) copy-start(f32[16,8]{1,0:T(8,128)S(1)} %fusion.83) | copy-start | bytes 1540
  4.0 1.7 %copy-start.1 = (bf16[1,1536,768]{2,1,0:T(8,128)(2,1)S(1)}, bf16[1,1536,768]{2,1,0:T(8,128)(2,1)}, u32[]{:S(2)}) copy-start(bf16[1,1536,768]{2,1,0:T(8,128)(2,1)} %param.12) | copy-start | bytes 7077892
  5.7 3.7 %copy-start.19 = (bf16[8,1024]{1,0:T(8,128)(2,1)S(1)}, bf16[8,1024]{1,0:T(8,128)(2,1)}, u32[]{:S(2)}) copy-start(bf16[8,1024]{1,0:T(8,128)(2,1)} %param.14) | copy-start | bytes 49156
  6.3 8.0 %collective-permute-start = (bf16[16,8,768]{2,1,0:T(8,128)(2,1)S(1)}, bf16[16,8,768]{2,1,0:T(8,128)(2,1)S(1)}, u32[]{:S(2)}, u32[]{:S(2)}) collective-permute-start(bf16[16,8,768]{2,1,0:T(8,128)(2,1)S(1)} %fusion.18), channel_id=1, source_target_pairs={{0,1},{1,0},{2,3},{3,2},{4,5},{5,4},{6,7},{7,6},{8,9},{9,8},{10,11... | collective-permute-start | bytes 589832 | tf_op jit(solution)/shard_map/ppermute | solution.py:11
  9.6 3.7 %collective-permute-start.1 = (bf16[8,1024]{1,0:T(8,128)(2,1)S(1)}, bf16[8,1024]{1,0:T(8,128)(2,1)S(1)}, u32[]{:S(2)}, u32[]{:S(2)}) collective-permute-start(bf16[8,1024]{1,0:T(8,128)(2,1)S(1)} %fusion.73), channel_id=1, source_target_pairs={{0,4},{4,0},{8,12},{12,8},{16,20},{20,16},{24,28},{28,24},{1,5},{5... | collective-permute-start | bytes 49160 | tf_op jit(solution)/shard_map/ppermute | solution.py:11
  15.0 1.7 %collective-permute-start.2 = (bf16[16,8,768]{2,1,0:T(8,128)(2,1)}, bf16[16,8,768]{2,1,0:T(8,128)(2,1)S(1)}, u32[]{:S(2)}, u32[]{:S(2)}) collective-permute-start(bf16[16,8,768]{2,1,0:T(8,128)(2,1)} %add_convert_fusion.4), channel_id=1, source_target_pairs={{0,2},{2,0},{1,3},{3,1},{4,6},{6,4},{5,7},{7,5},{8,10},{10,8},{9,1... | collective-permute-start | bytes 589832 | tf_op jit(solution)/shard_map/ppermute | solution.py:11
  18.1 1.7 %copy-start.2 = (bf16[1,1536,768]{2,1,0:T(8,128)(2,1)S(1)}, bf16[1,1536,768]{2,1,0:T(8,128)(2,1)}, u32[]{:S(2)}) copy-start(bf16[1,1536,768]{2,1,0:T(8,128)(2,1)} %param.12) | copy-start | bytes 7077892
  18.8 1.5 %copy-start.8 = (bf16[16,1024]{1,0:T(8,128)(2,1)S(1)}, bf16[16,1024]{1,0:T(8,128)(2,1)}, u32[]{:S(2)}) copy-start(bf16[16,1024]{1,0:T(8,128)(2,1)} %pad_maximum_fusion.1) | copy-start | bytes 98308
  19.7 9.6 %copy-start.3 = (bf16[768,1024]{1,0:T(8,128)(2,1)S(1)}, bf16[768,1024]{1,0:T(8,128)(2,1)}, u32[]{:S(2)}) copy-start(bf16[768,1024]{1,0:T(8,128)(2,1)} %param.13) | copy-start | bytes 4718596
  20.4 9.8 %copy-start.21 = (s32[8]{0:T(128)S(1)}, s32[8]{0:T(128)}, u32[]{:S(2)}) copy-start(s32[8]{0:T(128)} %param.15) | copy-start | bytes 100
  20.4 9.8 %copy-start.22 = (s32[64]{0:T(128)S(1)}, s32[64]{0:T(128)}, u32[]{:S(2)}) copy-start(s32[64]{0:T(128)} %fusion.89) | copy-start | bytes 772
  20.4 4.0 %collective-permute-start.4 = (bf16[16,1024]{1,0:T(8,128)(2,1)S(1)}, bf16[16,1024]{1,0:T(8,128)(2,1)S(1)}, u32[]{:S(2)}, u32[]{:S(2)}) collective-permute-start(bf16[16,1024]{1,0:T(8,128)(2,1)S(1)} %copy-done.8), channel_id=1, source_target_pairs={{0,8},{4,12},{8,0},{12,4},{16,24},{20,28},{24,16},{28,20},{1,9},{5... | collective-permute-start | bytes 98312 | tf_op jit(solution)/shard_map/ppermute | solution.py:11
  22.3 6.7 %collective-permute-start.3 = (bf16[16,8,768]{2,1,0:T(8,128)(2,1)S(1)}, bf16[16,8,768]{2,1,0:T(8,128)(2,1)S(1)}, u32[]{:S(2)}, u32[]{:S(2)}) collective-permute-start(bf16[16,8,768]{2,1,0:T(8,128)(2,1)S(1)} %fusion.4), channel_id=1, source_target_pairs={{0,1},{1,0},{2,3},{3,2},{4,5},{5,4},{6,7},{7,6},{8,9},{9,8},{10,11... | collective-permute-start | bytes 589832 | tf_op jit(solution)/shard_map/ppermute | solution.py:11
  24.4 5.5 %collective-permute-start.5 = (bf16[32,1024]{1,0:T(8,128)(2,1)S(1)}, bf16[32,1024]{1,0:T(8,128)(2,1)S(1)}, u32[]{:S(2)}, u32[]{:S(2)}) collective-permute-start(bf16[32,1024]{1,0:T(8,128)(2,1)S(1)} %pad_maximum_fusion), channel_id=1, source_target_pairs={{0,16},{4,20},{8,24},{12,28},{16,0},{20,4},{24,8},{28,12},{1,17},{... | collective-permute-start | bytes 196616 | tf_op jit(solution)/shard_map/ppermute | solution.py:11
  33.4 5.9 %collective-permute-start.6 = (bf16[16,8,768]{2,1,0:T(8,128)(2,1)S(1)}, bf16[16,8,768]{2,1,0:T(8,128)(2,1)S(1)}, u32[]{:S(2)}, u32[]{:S(2)}) collective-permute-start(bf16[16,8,768]{2,1,0:T(8,128)(2,1)S(1)} %fusion.30), channel_id=1, source_target_pairs={{0,1},{1,0},{2,3},{3,2},{4,5},{5,4},{6,7},{7,6},{8,9},{9,8},{10,11... | collective-permute-start | bytes 589832 | tf_op jit(solution)/shard_map/ppermute | solution.py:11
  40.4 2.1 %copy-start.6 = (f32[128,1536]{1,0:T(8,128)S(1)}, f32[128,1536]{1,0:T(8,128)}, u32[]{:S(2)}) copy-start(f32[128,1536]{1,0:T(8,128)} %get-tuple-element.70) | copy-start | bytes 2359300
  40.9 1.6 %copy-start.4 = (f32[16,8,768]{2,1,0:T(8,128)}, f32[16,8,768]{2,1,0:T(8,128)S(1)}, u32[]{:S(2)}) copy-start(f32[16,8,768]{2,1,0:T(8,128)S(1)} %constant_dynamic-update-slice_fusion.35) | copy-start | bytes 1179652
  40.9 1.5 %collective-permute-start.7 = (bf16[16,8,768]{2,1,0:T(8,128)(2,1)S(1)}, bf16[16,8,768]{2,1,0:T(8,128)(2,1)S(1)}, u32[]{:S(2)}, u32[]{:S(2)}) collective-permute-start(bf16[16,8,768]{2,1,0:T(8,128)(2,1)S(1)} %add_convert_fusion.6), channel_id=1, source_target_pairs={{0,2},{2,0},{1,3},{3,1},{4,6},{6,4},{5,7},{7,5},{8,10},{10,8},{9,1... | collective-permute-start | bytes 589832 | tf_op jit(solution)/shard_map/ppermute | solution.py:11
  44.2 7.0 %collective-permute-start.8 = (bf16[16,8,768]{2,1,0:T(8,128)(2,1)S(1)}, bf16[16,8,768]{2,1,0:T(8,128)(2,1)S(1)}, u32[]{:S(2)}, u32[]{:S(2)}) collective-permute-start(bf16[16,8,768]{2,1,0:T(8,128)(2,1)S(1)} %fusion.27), channel_id=1, source_target_pairs={{0,1},{1,0},{2,3},{3,2},{4,5},{5,4},{6,7},{7,6},{8,9},{9,8},{10,11... | collective-permute-start | bytes 589832 | tf_op jit(solution)/shard_map/ppermute | solution.py:11
  45.8 8.9 %copy-start.17 = (f32[768]{0:T(1024)S(1)}, f32[768]{0:T(1024)}, u32[]{:S(2)}) copy-start(f32[768]{0:T(1024)} %copy-done.16) | copy-start | bytes 9220
  45.8 9.1 %copy-start.15 = (f32[768]{0:T(1024)S(1)}, f32[768]{0:T(1024)}, u32[]{:S(2)}) copy-start(f32[768]{0:T(1024)} %copy-done.14) | copy-start | bytes 9220
  54.8 0.7 %copy-start.13 = (f32[768]{0:T(1024)S(1)}, f32[768]{0:T(1024)}, u32[]{:S(2)}) copy-start(f32[768]{0:T(1024)} %copy-done.12) | copy-start | bytes 9220
  55.0 0.7 %copy-start.11 = (f32[768]{0:T(1024)S(1)}, f32[768]{0:T(1024)}, u32[]{:S(2)}) copy-start(f32[768]{0:T(1024)} %copy-done.10) | copy-start | bytes 9220
  55.1 1.0 %copy-start.5 = (f32[16,8,768]{2,1,0:T(8,128)S(1)}, f32[16,8,768]{2,1,0:T(8,128)}, u32[]{:S(2)}) copy-start(f32[16,8,768]{2,1,0:T(8,128)} %copy-done.4) | copy-start | bytes 1179652

commit v10 on v9

--- a/solution.py
+++ b/solution.py
@@ -62,7 +62,8 @@
     def mlp_back(cotangent):
         (hidden_grad,) = hidden_back(cotangent)
         pre_grad = hidden_grad.astype(jnp.float32) * slope
-        (low_grad,) = expand_back(lax.optimization_barrier(pre_grad))
+        low_pre_grad = lax.optimization_barrier(pre_grad.astype(jnp.bfloat16))
+        (low_grad,) = expand_back(low_pre_grad.astype(jnp.float32))
         return (low_grad.astype(jnp.float32),)
 
     return branch, mlp_back

time: 57.6 us -> 57.6 us (level)
  no operation moved by 1% of the time
where the time goes in v10:
time: 57.6 us; the launch traced here: 57.1 us
  waiting for transfers between devices  17.1 us (30%)
  starting transfers between devices  14 us (24%)
  other arithmetic  11.6 us (20%)
  matrix products  8.93 us (16%)
  local copies, waits for them, and re-layouts  4.85 us (8%)
  between operations  0.58 us (1%)
    ppermute x9, waiting for transfers between devices, swapped(): lax.ppermute(value, axis, [(i, i ^ 1 << stride) for i in range(lax.axis_s...  17.1 us
    ppermute x9, starting transfers between devices, swapped(): lax.ppermute(value, axis, [(i, i ^ 1 << stride) for i in range(lax.axis_s...  14 us
    dot_general x4, matrix products, expand_part(): return jnp.dot(flattened, expand, preferred_element_type=jnp.float32)  4.11 us
    unnamed x61, other arithmetic  3.38 us
    dot_general x4, matrix products, mlp_part(): jnp.dot(inner, project_out, preferred_element_type=jnp.float32)  3.01 us
    unnamed x49, local copies, waits for them, and re-layouts  2.52 us
    reduce_sum x6, other arithmetic, normalize_last(): centred = values - jnp.mean(values, axis=-1, keepdims=True)  1.73 us
  transfers between devices with their start and end apart: 9, of which 8 were waited for; matrix products, arithmetic and copies ran while one was open for 4% of the time, Pallas kernels for 0%

profile of v10, /device:TPU:0, one launch (start us, length us, event | category | flops | bytes accessed | tf_op | source)
XLA Modules:
  0.0 57.1 jit_solution(8998931581289478988)
XLA Ops:
  0.0 1.1 %copy.13 = f32[1,7,7,768]{3,2,0,1:T(8,128)S(1)} copy(f32[1,7,7,768]{3,0,2,1:T(1,128)} %param.9) | data formatting | bytes 301056
  1.1 0.2 slice_reduce_fusion.5
  1.3 0.2 slice_reduce_fusion.19
  1.5 0.1 slice_reduce_fusion.47
  1.6 1.0 %copy.9 = f32[8,4,4,768]{3,0,2,1:T(8,128)S(1)} copy(bf16[8,4,4,768]{3,2,1,0:T(4,128)(2,1)} %param.8) | data formatting | bytes 589824 | tf_op jit(solution)/shard_map/convert_element_type | solution.py:124
  2.8 0.1 constant_dynamic-update-slice_fusion.10
  3.5 0.1 reduce_sum.148
  3.6 0.2 multiply_reduce_fusion.3
  3.9 0.1 multiply_convert_fusion.5
  4.0 1.6 %fusion.48 = (f32[128,1536]{1,0:T(8,128)}, f32[128,1536]{1,0:T(8,128)S(1)}) fusion(bf16[1,768,1536]{2,1,0:T(8,128)(2,1)S(1)} %copy-done, bf16[16,8,768]{2,1,0:T(8,128)(2,1)S(1)} %multiply_convert_fusion.5), kind=kOutput, calls=%fused_computation.47 | convolution fusion | flops 305135616 | bytes 4128768 | tf_op jit(solution)/shard_map/jvp()/dot_general | solution.py:44
  5.7 0.6 %fusion.26 = bf16[16,8,768]{2,1,0:T(8,128)(2,1)S(1)} fusion(bf16[1,1536,768]{2,1,0:T(8,128)(2,1)S(1)} %copy-done.1, f32[128,1536]{1,0:T(8,128)S(1)} %get-tuple-element.71), kind=kOutput, calls=%fused_computation.24 | convolution fusion | flops 303857664 | bytes 3342336 | tf_op jit(solution)/shard_map/jvp()/dot_general | solution.py:57
  6.3 3.1 %collective-permute-start = (bf16[16,8,768]{2,1,0:T(8,128)(2,1)S(1)}, bf16[16,8,768]{2,1,0:T(8,128)(2,1)S(1)}, u32[]{:S(2)}, u32[]{:S(2)}) collective-permute-start(bf16[16,8,768]{2,1,0:T(8,128)(2,1)S(1)} %fusion.26), channel_id=1, source_target_pairs={{0,1},{1,0},{2,3},{3,2},{4,5},{5,4},{6,7},{7,6},{8,9},{9,8},{10,11... | collective-permute-start | bytes 589832 | tf_op jit(solution)/shard_map/ppermute | solution.py:11
  9.4 0.1 fusion.74
  9.5 0.1 fusion.75
  9.6 1.5 %collective-permute-start.1 = (bf16[8,1024]{1,0:T(8,128)(2,1)S(1)}, bf16[8,1024]{1,0:T(8,128)(2,1)S(1)}, u32[]{:S(2)}, u32[]{:S(2)}) collective-permute-start(bf16[8,1024]{1,0:T(8,128)(2,1)S(1)} %fusion.75), channel_id=1, source_target_pairs={{0,4},{4,0},{8,12},{12,8},{16,20},{20,16},{24,28},{28,24},{1,5},{5... | collective-permute-start | bytes 49160 | tf_op jit(solution)/shard_map/ppermute | solution.py:11
  11.1 2.2 %collective-permute-done.1 = bf16[8,1024]{1,0:T(8,128)(2,1)S(1)} collective-permute-done((bf16[8,1024]{1,0:T(8,128)(2,1)S(1)}, bf16[8,1024]{1,0:T(8,128)(2,1)S(1)}, u32[]{:S(2)}, u32[]{:S(2)}) %collective-permute-start.1) | collective-permute-done | bytes 16416 | tf_op jit(solution)/shard_map/ppermute | solution.py:11
  13.3 0.6 %pad_maximum_fusion.1 = bf16[16,1024]{1,0:T(8,128)(2,1)} fusion(bf16[8,1024]{1,0:T(8,128)(2,1)S(1)} %collective-permute-done.1, bf16[8,1024]{1,0:T(8,128)(2,1)S(1)} %fusion.75), kind=kLoop, calls=%fused_computation.171 | loop fusion | flops 65536 | bytes 65536 | tf_op jit(solution)/shard_map/concatenate | solution.py:169
  13.9 0.3 collective-permute-done
  14.3 0.7 %add_convert_fusion.4 = bf16[16,8,768]{2,1,0:T(8,128)(2,1)} fusion(bf16[16,8,768]{2,1,0:T(8,128)(2,1)S(1)} %collective-permute-done, bf16[16,8,768]{2,1,0:T(8,128)(2,1)S(1)} %fusion.26, f32[8,4,4,768]{3,0,2,1:T(8,128)S(1)} %copy.9), kind=kLoop, calls=%fused_computation.77 | loop fusion | flops 688128 | bytes 983040 | tf_op jit(solution)/shard_map/convert_element_type | solution.py:130
  15.0 0.6 %fusion.91 = s32[64]{0:T(128)} fusion(s32[]{:T(128)S(6)} %axis_index.28), kind=kLoop, calls=%fused_computation.259 | loop fusion | flops 960 | bytes 260 | tf_op jit(solution)/shard_map/add | solution.py:104
  15.6 1.1 %collective-permute-done.2 = bf16[16,8,768]{2,1,0:T(8,128)(2,1)S(1)} collective-permute-done((bf16[16,8,768]{2,1,0:T(8,128)(2,1)}, bf16[16,8,768]{2,1,0:T(8,128)(2,1)S(1)}, u32[]{:S(2)}, u32[]{:S(2)}) %collective-permute-start.2) | collective-permute-done | bytes 196640 | tf_op jit(solution)/shard_map/ppermute | solution.py:11
  17.6 0.1 reduce_sum.154
  17.7 0.2 multiply_reduce_fusion.2
  17.9 0.1 multiply_convert_fusion.2
  18.1 0.7 %fusion.58 = (f32[128,1536]{1,0:T(8,128)S(1)}, f32[128,1536]{1,0:T(8,128)S(1)}) fusion(bf16[1,768,1536]{2,1,0:T(8,128)(2,1)S(1)} %copy-done, bf16[16,8,768]{2,1,0:T(8,128)(2,1)S(1)} %multiply_convert_fusion.2), kind=kOutput, calls=%fused_computation.57 | convolution fusion | flops 305135616 | bytes 4128768 | tf_op jit(solution)/shard_map/jvp()/dot_general | solution.py:44
  18.8 0.9 %copy-done.2 = bf16[1,1536,768]{2,1,0:T(8,128)(2,1)S(1)} copy-done((bf16[1,1536,768]{2,1,0:T(8,128)(2,1)S(1)}, bf16[1,1536,768]{2,1,0:T(8,128)(2,1)}, u32[]{:S(2)}) %copy-start.2) | copy-done | bytes 2359320
  19.7 0.6 %fusion.6 = bf16[16,8,768]{2,1,0:T(8,128)(2,1)S(1)} fusion(bf16[1,1536,768]{2,1,0:T(8,128)(2,1)S(1)} %copy-done.2, f32[128,1536]{1,0:T(8,128)S(1)} %get-tuple-element.73), kind=kOutput, calls=%fused_computation.8 | convolution fusion | flops 303759360 | bytes 3342336 | tf_op jit(solution)/shard_map/jvp()/dot_general | solution.py:57
  20.4 1.9 %collective-permute-start.4 = (bf16[16,1024]{1,0:T(8,128)(2,1)S(1)}, bf16[16,1024]{1,0:T(8,128)(2,1)S(1)}, u32[]{:S(2)}, u32[]{:S(2)}) collective-permute-start(bf16[16,1024]{1,0:T(8,128)(2,1)S(1)} %copy-done.8), channel_id=1, source_target_pairs={{0,8},{4,12},{8,0},{12,4},{16,24},{20,28},{24,16},{28,20},{1,9},{5... | collective-permute-start | bytes 98312 | tf_op jit(solution)/shard_map/ppermute | solution.py:11
  22.3 1.5 %collective-permute-start.3 = (bf16[16,8,768]{2,1,0:T(8,128)(2,1)S(1)}, bf16[16,8,768]{2,1,0:T(8,128)(2,1)S(1)}, u32[]{:S(2)}, u32[]{:S(2)}) collective-permute-start(bf16[16,8,768]{2,1,0:T(8,128)(2,1)S(1)} %fusion.6), channel_id=1, source_target_pairs={{0,1},{1,0},{2,3},{3,2},{4,5},{5,4},{6,7},{7,6},{8,9},{9,8},{10,11... | collective-permute-start | bytes 589832 | tf_op jit(solution)/shard_map/ppermute | solution.py:11
  23.8 0.6 %collective-permute-done.4 = bf16[16,1024]{1,0:T(8,128)(2,1)S(1)} collective-permute-done((bf16[16,1024]{1,0:T(8,128)(2,1)S(1)}, bf16[16,1024]{1,0:T(8,128)(2,1)S(1)}, u32[]{:S(2)}, u32[]{:S(2)}) %collective-permute-start.4) | collective-permute-done | bytes 32800 | tf_op jit(solution)/shard_map/ppermute | solution.py:11
  24.4 2.8 %collective-permute-start.5 = (bf16[32,1024]{1,0:T(8,128)(2,1)S(1)}, bf16[32,1024]{1,0:T(8,128)(2,1)S(1)}, u32[]{:S(2)}, u32[]{:S(2)}) collective-permute-start(bf16[32,1024]{1,0:T(8,128)(2,1)S(1)} %pad_maximum_fusion), channel_id=1, source_target_pairs={{0,16},{4,20},{8,24},{12,28},{16,0},{20,4},{24,8},{28,12},{1,17},{... | collective-permute-start | bytes 196616 | tf_op jit(solution)/shard_map/ppermute | solution.py:11
  27.2 1.7 %collective-permute-done.3 = bf16[16,8,768]{2,1,0:T(8,128)(2,1)S(1)} collective-permute-done((bf16[16,8,768]{2,1,0:T(8,128)(2,1)S(1)}, bf16[16,8,768]{2,1,0:T(8,128)(2,1)S(1)}, u32[]{:S(2)}, u32[]{:S(2)}) %collective-permute-start.3) | collective-permute-done | bytes 196640 | tf_op jit(solution)/shard_map/ppermute | solution.py:11
  28.9 0.1 convert_reduce_fusion
  29.0 0.1 multiply_reduce_fusion.8
  29.1 0.2 multiply_reduce_fusion.7
  29.3 0.5 multiply_reduce_fusion.5
  29.8 0.1 broadcast_multiply_fusion
  29.9 0.3 convert_reduce_fusion.1
  30.2 0.2 fusion.87
  30.4 0.2 multiply_reduce_fusion.4
  30.7 0.6 %multiply_reduce_fusion.6 = (f32[8]{0:T(128)S(1)}, f32[8,768]{1,0:T(8,128)S(1)}) fusion(f32[8,768]{1,0:T(8,128)S(1)} %convert_reduce_fusion, f32[8]{0:T(128)S(1)} %broadcast_multiply_fusion.4, bf16[768,1024]{1,0:T(8,128)(2,1)S(1)} %copy-done.3, f32[8,1024]{1,0:T(8,128)S(1)} %get-tuple-element.75, f32[8,1024]{1,0:T(8,128)S(1)} %get-tuple-element.79, ...), kind=kOutput, calls=%fused_computation.177 | convolution fusion | flops 12652536 | bytes 1687680 | tf_op jit(solution)/shard_map/transpose(jvp())/dot_general | solution.py:75
  31.3 0.2 fusion.104
  31.5 0.1 add_multiply_fusion
  31.6 0.9 %fusion.5 = bf16[128,1536]{1,0:T(8,128)(2,1)S(1)} fusion(f32[128,1536]{1,0:T(8,128)S(1)} %get-tuple-element.72, bf16[1,1536,768]{2,1,0:T(8,128)(2,1)S(1)} %copy-done.2, f32[8,768]{1,0:T(8,128)S(1)} %add_multiply_fusion), kind=kOutput, calls=%fused_computation.7 | convolution fusion | flops 302579712 | bytes 3563520 | tf_op jit(solution)/shard_map/transpose(jvp())/dot_general | solution.py:57
  32.5 0.9 %fusion.32 = bf16[16,8,768]{2,1,0:T(8,128)(2,1)S(1)} fusion(bf16[128,1536]{1,0:T(8,128)(2,1)S(1)} %fusion.5, bf16[1,768,1536]{2,1,0:T(8,128)(2,1)S(1)} %copy-done), kind=kOutput, calls=%fused_computation.26 | convolution fusion | flops 302088192 | bytes 2949120 | tf_op jit(solution)/shard_map/transpose(jvp())/dot_general | solution.py:44
  33.4 1.6 %collective-permute-start.6 = (bf16[16,8,768]{2,1,0:T(8,128)(2,1)S(1)}, bf16[16,8,768]{2,1,0:T(8,128)(2,1)S(1)}, u32[]{:S(2)}, u32[]{:S(2)}) collective-permute-start(bf16[16,8,768]{2,1,0:T(8,128)(2,1)S(1)} %fusion.32), channel_id=1, source_target_pairs={{0,1},{1,0},{2,3},{3,2},{4,5},{5,4},{6,7},{7,6},{8,9},{9,8},{10,11... | collective-permute-start | bytes 589832 | tf_op jit(solution)/shard_map/ppermute | solution.py:11
  35.0 4.3 %collective-permute-done.6 = bf16[16,8,768]{2,1,0:T(8,128)(2,1)S(1)} collective-permute-done((bf16[16,8,768]{2,1,0:T(8,128)(2,1)S(1)}, bf16[16,8,768]{2,1,0:T(8,128)(2,1)S(1)}, u32[]{:S(2)}, u32[]{:S(2)}) %collective-permute-start.6) | collective-permute-done | bytes 196640 | tf_op jit(solution)/shard_map/ppermute | solution.py:11
  39.3 0.2 multiply_reduce_fusion.1
  39.5 0.2 fusion.72
  39.7 0.2 broadcast_add_fusion.1
  40.9 0.1 collective-permute-start.7
  41.0 1.4 %collective-permute-done.7 = bf16[16,8,768]{2,1,0:T(8,128)(2,1)S(1)} collective-permute-done((bf16[16,8,768]{2,1,0:T(8,128)(2,1)S(1)}, bf16[16,8,768]{2,1,0:T(8,128)(2,1)S(1)}, u32[]{:S(2)}, u32[]{:S(2)}) %collective-permute-start.7) | collective-permute-done | bytes 196640 | tf_op jit(solution)/shard_map/ppermute | solution.py:11
  42.5 0.9 %fusion.2 = bf16[128,1536]{1,0:T(8,128)(2,1)S(1)} fusion(f32[128,1536]{1,0:T(8,128)S(1)} %copy-done.6, bf16[1,1536,768]{2,1,0:T(8,128)(2,1)S(1)} %copy-done.2, bf16[16,8,768]{2,1,0:T(8,128)(2,1)S(1)} %collective-permute-done.7), kind=kOutput, calls=%fused_computation.3 | convolution fusion | flops 302776320 | bytes 3735552 | tf_op jit(solution)/shard_map/transpose(jvp())/dot_general | solution.py:57
  43.4 0.9 %fusion.29 = bf16[16,8,768]{2,1,0:T(8,128)(2,1)S(1)} fusion(bf16[128,1536]{1,0:T(8,128)(2,1)S(1)} %fusion.2, bf16[1,768,1536]{2,1,0:T(8,128)(2,1)S(1)} %copy-done), kind=kOutput, calls=%fused_computation.25 | convolution fusion | flops 302088192 | bytes 2949120 | tf_op jit(solution)/shard_map/transpose(jvp())/dot_general | solution.py:44
  44.2 1.6 %collective-permute-start.8 = (bf16[16,8,768]{2,1,0:T(8,128)(2,1)S(1)}, bf16[16,8,768]{2,1,0:T(8,128)(2,1)S(1)}, u32[]{:S(2)}, u32[]{:S(2)}) collective-permute-start(bf16[16,8,768]{2,1,0:T(8,128)(2,1)S(1)} %fusion.29), channel_id=1, source_target_pairs={{0,1},{1,0},{2,3},{3,2},{4,5},{5,4},{6,7},{7,6},{8,9},{9,8},{10,11... | collective-permute-start | bytes 589832 | tf_op jit(solution)/shard_map/ppermute | solution.py:11
  45.8 5.4 %collective-permute-done.8 = bf16[16,8,768]{2,1,0:T(8,128)(2,1)S(1)} collective-permute-done((bf16[16,8,768]{2,1,0:T(8,128)(2,1)S(1)}, bf16[16,8,768]{2,1,0:T(8,128)(2,1)S(1)}, u32[]{:S(2)}, u32[]{:S(2)}) %collective-permute-start.8) | collective-permute-done | bytes 196640 | tf_op jit(solution)/shard_map/ppermute | solution.py:11
  51.2 0.9 %multiply_reduce_fusion = f32[16,8]{1,0:T(8,128)S(1)} fusion(f32[16,8,768]{2,1,0:T(8,128)S(1)} %constant_dynamic-update-slice_fusion, f32[768]{0:T(1024)S(1)} %reduce.49, f32[16,8]{1,0:T(8,128)} %copy-done.7, bf16[16,8,768]{2,1,0:T(8,128)(2,1)S(1)} %collective-permute-done.8, bf16[16,8,768]{2,1,0:T(8,128)(2,1)S(1)} %fusion.29), kind=kLoop, calls=%fused_computation.66 | loop fusion | flops 884608 | bytes 790528 | tf_op jit(solution)/shard_map/transpose(jvp())/reduce_sum | solution.py:35
  52.1 0.7 %multiply_multiply_fusion.4 = f32[16,8]{1,0:T(8,128)S(1)} fusion(f32[16,8]{1,0:T(8,128)S(1)} %multiply_reduce_fusion, f32[16,8]{1,0:T(8,128)} %copy-done.18), kind=kLoop, calls=%fused_computation.191 | loop fusion | flops 768 | bytes 1536 | tf_op jit(solution)/shard_map/transpose(jvp())/div | solution.py:34
  52.8 1.0 %fusion.73 = f32[16,8]{1,0:T(8,128)S(1)} fusion(f32[16,8]{1,0:T(8,128)S(1)} %multiply_multiply_fusion.4, f32[16,8,768]{2,1,0:T(8,128)S(1)} %constant_dynamic-update-slice_fusion, f32[16,8]{1,0:T(8,128)} %copy-done.7, f32[16,8]{1,0:T(8,128)} %copy-done.9, f32[768]{0:T(1024)S(1)} %reduce.49, bf16[16,8,768]{2,1,0:T(8,128)(2,1)S(1)} %collective-permute-done.8, ...), kind=kLoop, calls=%fused_computation.96 | loop fusion | flops 1179520 | bytes 791552 | tf_op jit(solution)/shard_map/transpose(jvp())/reduce_sum | solution.py:33
  53.8 0.9 %broadcast_add_fusion = f32[16,8,768]{2,1,0:T(8,128)S(1)} fusion(f32[16,8]{1,0:T(8,128)S(1)} %negate_multiply_fusion, f32[16,8]{1,0:T(8,128)S(1)} %multiply_multiply_fusion.4, f32[16,8,768]{2,1,0:T(8,128)S(1)} %constant_dynamic-update-slice_fusion, f32[16,8]{1,0:T(8,128)} %copy-done.7, f32[16,8]{1,0:T(8,128)} %copy-done.9, f32[768]{0:T(1024)S(1)} %reduce.49, ...), kind=kLoop, calls=%fused_computation.91 | loop fusion | flops 1179648 | bytes 1184768 | tf_op jit(solution)/shard_map/transpose(jvp())/add_any | solution.py:33
  55.5 0.1 copy-done.13
  55.8 0.3 copy-done.5
  56.1 0.1 add_select_fusion
  56.2 0.9 %copy.10 = f32[1,8,4,4,768]{4,3,2,1,0:T(4,128)} copy(f32[1,8,4,4,768]{4,1,3,2,0:T(8,128)S(1)} %bitcast.94) | data formatting | bytes 786432 | tf_op jit(solution)/shard_map/broadcast_in_dim;reshape | solution.py:220
  (129 shorter events, 3.9 us)
Async XLA Ops:
  0.0 4.0 %copy-start = (bf16[1,768,1536]{2,1,0:T(8,128)(2,1)S(1)}, bf16[1,768,1536]{2,1,0:T(8,128)(2,1)}, u32[]{:S(2)}) copy-start(bf16[1,768,1536]{2,1,0:T(8,128)(2,1)} %param.11) | copy-start | bytes 7077892
  1.3 38.7 %copy-start.16 = (f32[768]{0:T(1024)}, f32[768]{0:T(1024)S(1)}, u32[]{:S(2)}) copy-start(f32[768]{0:T(1024)S(1)} %get-tuple-element.18) | copy-start | bytes 9220
  1.3 38.8 %copy-start.14 = (f32[768]{0:T(1024)}, f32[768]{0:T(1024)S(1)}, u32[]{:S(2)}) copy-start(f32[768]{0:T(1024)S(1)} %get-tuple-element.21) | copy-start | bytes 9220
  1.4 39.2 %copy-start.12 = (f32[768]{0:T(1024)}, f32[768]{0:T(1024)S(1)}, u32[]{:S(2)}) copy-start(f32[768]{0:T(1024)S(1)} %get-tuple-element.38) | copy-start | bytes 9220
  1.5 39.4 %copy-start.10 = (f32[768]{0:T(1024)}, f32[768]{0:T(1024)S(1)}, u32[]{:S(2)}) copy-start(f32[768]{0:T(1024)S(1)} %get-tuple-element.50) | copy-start | bytes 9220
  3.0 0.8 %copy-start.20 = (f32[1,768]{1,0:T(1,128)S(1)}, f32[1,768]{1,0:T(1,128)}, u32[]{:S(2)}) copy-start(f32[1,768]{1,0:T(1,128)} %param.10) | copy-start | bytes 9220
  3.6 2.0 %copy-start.7 = (f32[16,8]{1,0:T(8,128)}, f32[16,8]{1,0:T(8,128)S(1)}, u32[]{:S(2)}) copy-start(f32[16,8]{1,0:T(8,128)S(1)} %broadcast_multiply_fusion.2) | copy-start | bytes 1540
  3.8 10.5 %copy-start.18 = (f32[16,8]{1,0:T(8,128)}, f32[16,8]{1,0:T(8,128)S(1)}, u32[]{:S(2)}) copy-start(f32[16,8]{1,0:T(8,128)S(1)} %multiply_reduce_fusion.3) | copy-start | bytes 1540
  3.8 1.8 %copy-start.9 = (f32[16,8]{1,0:T(8,128)}, f32[16,8]{1,0:T(8,128)S(1)}, u32[]{:S(2)}) copy-start(f32[16,8]{1,0:T(8,128)S(1)} %fusion.85) | copy-start | bytes 1540
  4.0 1.7 %copy-start.1 = (bf16[1,1536,768]{2,1,0:T(8,128)(2,1)S(1)}, bf16[1,1536,768]{2,1,0:T(8,128)(2,1)}, u32[]{:S(2)}) copy-start(bf16[1,1536,768]{2,1,0:T(8,128)(2,1)} %param.12) | copy-start | bytes 7077892
  5.7 3.7 %copy-start.19 = (bf16[8,1024]{1,0:T(8,128)(2,1)S(1)}, bf16[8,1024]{1,0:T(8,128)(2,1)}, u32[]{:S(2)}) copy-start(bf16[8,1024]{1,0:T(8,128)(2,1)} %param.14) | copy-start | bytes 49156
  6.3 8.0 %collective-permute-start = (bf16[16,8,768]{2,1,0:T(8,128)(2,1)S(1)}, bf16[16,8,768]{2,1,0:T(8,128)(2,1)S(1)}, u32[]{:S(2)}, u32[]{:S(2)}) collective-permute-start(bf16[16,8,768]{2,1,0:T(8,128)(2,1)S(1)} %fusion.26), channel_id=1, source_target_pairs={{0,1},{1,0},{2,3},{3,2},{4,5},{5,4},{6,7},{7,6},{8,9},{9,8},{10,11... | collective-permute-start | bytes 589832 | tf_op jit(solution)/shard_map/ppermute | solution.py:11
  9.6 3.7 %collective-permute-start.1 = (bf16[8,1024]{1,0:T(8,128)(2,1)S(1)}, bf16[8,1024]{1,0:T(8,128)(2,1)S(1)}, u32[]{:S(2)}, u32[]{:S(2)}) collective-permute-start(bf16[8,1024]{1,0:T(8,128)(2,1)S(1)} %fusion.75), channel_id=1, source_target_pairs={{0,4},{4,0},{8,12},{12,8},{16,20},{20,16},{24,28},{28,24},{1,5},{5... | collective-permute-start | bytes 49160 | tf_op jit(solution)/shard_map/ppermute | solution.py:11
  15.0 1.7 %collective-permute-start.2 = (bf16[16,8,768]{2,1,0:T(8,128)(2,1)}, bf16[16,8,768]{2,1,0:T(8,128)(2,1)S(1)}, u32[]{:S(2)}, u32[]{:S(2)}) collective-permute-start(bf16[16,8,768]{2,1,0:T(8,128)(2,1)} %add_convert_fusion.4), channel_id=1, source_target_pairs={{0,2},{2,0},{1,3},{3,1},{4,6},{6,4},{5,7},{7,5},{8,10},{10,8},{9,1... | collective-permute-start | bytes 589832 | tf_op jit(solution)/shard_map/ppermute | solution.py:11
  18.1 1.7 %copy-start.2 = (bf16[1,1536,768]{2,1,0:T(8,128)(2,1)S(1)}, bf16[1,1536,768]{2,1,0:T(8,128)(2,1)}, u32[]{:S(2)}) copy-start(bf16[1,1536,768]{2,1,0:T(8,128)(2,1)} %param.12) | copy-start | bytes 7077892
  18.8 1.5 %copy-start.8 = (bf16[16,1024]{1,0:T(8,128)(2,1)S(1)}, bf16[16,1024]{1,0:T(8,128)(2,1)}, u32[]{:S(2)}) copy-start(bf16[16,1024]{1,0:T(8,128)(2,1)} %pad_maximum_fusion.1) | copy-start | bytes 98308
  19.7 9.6 %copy-start.3 = (bf16[768,1024]{1,0:T(8,128)(2,1)S(1)}, bf16[768,1024]{1,0:T(8,128)(2,1)}, u32[]{:S(2)}) copy-start(bf16[768,1024]{1,0:T(8,128)(2,1)} %param.13) | copy-start | bytes 4718596
  20.4 9.8 %copy-start.21 = (s32[8]{0:T(128)S(1)}, s32[8]{0:T(128)}, u32[]{:S(2)}) copy-start(s32[8]{0:T(128)} %param.15) | copy-start | bytes 100
  20.4 9.8 %copy-start.22 = (s32[64]{0:T(128)S(1)}, s32[64]{0:T(128)}, u32[]{:S(2)}) copy-start(s32[64]{0:T(128)} %fusion.91) | copy-start | bytes 772
  20.4 4.0 %collective-permute-start.4 = (bf16[16,1024]{1,0:T(8,128)(2,1)S(1)}, bf16[16,1024]{1,0:T(8,128)(2,1)S(1)}, u32[]{:S(2)}, u32[]{:S(2)}) collective-permute-start(bf16[16,1024]{1,0:T(8,128)(2,1)S(1)} %copy-done.8), channel_id=1, source_target_pairs={{0,8},{4,12},{8,0},{12,4},{16,24},{20,28},{24,16},{28,20},{1,9},{5... | collective-permute-start | bytes 98312 | tf_op jit(solution)/shard_map/ppermute | solution.py:11
  22.3 6.7 %collective-permute-start.3 = (bf16[16,8,768]{2,1,0:T(8,128)(2,1)S(1)}, bf16[16,8,768]{2,1,0:T(8,128)(2,1)S(1)}, u32[]{:S(2)}, u32[]{:S(2)}) collective-permute-start(bf16[16,8,768]{2,1,0:T(8,128)(2,1)S(1)} %fusion.6), channel_id=1, source_target_pairs={{0,1},{1,0},{2,3},{3,2},{4,5},{5,4},{6,7},{7,6},{8,9},{9,8},{10,11... | collective-permute-start | bytes 589832 | tf_op jit(solution)/shard_map/ppermute | solution.py:11
  24.4 5.5 %collective-permute-start.5 = (bf16[32,1024]{1,0:T(8,128)(2,1)S(1)}, bf16[32,1024]{1,0:T(8,128)(2,1)S(1)}, u32[]{:S(2)}, u32[]{:S(2)}) collective-permute-start(bf16[32,1024]{1,0:T(8,128)(2,1)S(1)} %pad_maximum_fusion), channel_id=1, source_target_pairs={{0,16},{4,20},{8,24},{12,28},{16,0},{20,4},{24,8},{28,12},{1,17},{... | collective-permute-start | bytes 196616 | tf_op jit(solution)/shard_map/ppermute | solution.py:11
  33.4 5.9 %collective-permute-start.6 = (bf16[16,8,768]{2,1,0:T(8,128)(2,1)S(1)}, bf16[16,8,768]{2,1,0:T(8,128)(2,1)S(1)}, u32[]{:S(2)}, u32[]{:S(2)}) collective-permute-start(bf16[16,8,768]{2,1,0:T(8,128)(2,1)S(1)} %fusion.32), channel_id=1, source_target_pairs={{0,1},{1,0},{2,3},{3,2},{4,5},{5,4},{6,7},{7,6},{8,9},{9,8},{10,11... | collective-permute-start | bytes 589832 | tf_op jit(solution)/shard_map/ppermute | solution.py:11
  40.4 2.1 %copy-start.6 = (f32[128,1536]{1,0:T(8,128)S(1)}, f32[128,1536]{1,0:T(8,128)}, u32[]{:S(2)}) copy-start(f32[128,1536]{1,0:T(8,128)} %get-tuple-element.70) | copy-start | bytes 2359300
  40.9 1.6 %copy-start.4 = (f32[16,8,768]{2,1,0:T(8,128)}, f32[16,8,768]{2,1,0:T(8,128)S(1)}, u32[]{:S(2)}) copy-start(f32[16,8,768]{2,1,0:T(8,128)S(1)} %constant_dynamic-update-slice_fusion.35) | copy-start | bytes 1179652
  40.9 1.5 %collective-permute-start.7 = (bf16[16,8,768]{2,1,0:T(8,128)(2,1)S(1)}, bf16[16,8,768]{2,1,0:T(8,128)(2,1)S(1)}, u32[]{:S(2)}, u32[]{:S(2)}) collective-permute-start(bf16[16,8,768]{2,1,0:T(8,128)(2,1)S(1)} %add_convert_fusion.6), channel_id=1, source_target_pairs={{0,2},{2,0},{1,3},{3,1},{4,6},{6,4},{5,7},{7,5},{8,10},{10,8},{9,1... | collective-permute-start | bytes 589832 | tf_op jit(solution)/shard_map/ppermute | solution.py:11
  44.2 7.0 %collective-permute-start.8 = (bf16[16,8,768]{2,1,0:T(8,128)(2,1)S(1)}, bf16[16,8,768]{2,1,0:T(8,128)(2,1)S(1)}, u32[]{:S(2)}, u32[]{:S(2)}) collective-permute-start(bf16[16,8,768]{2,1,0:T(8,128)(2,1)S(1)} %fusion.29), channel_id=1, source_target_pairs={{0,1},{1,0},{2,3},{3,2},{4,5},{5,4},{6,7},{7,6},{8,9},{9,8},{10,11... | collective-permute-start | bytes 589832 | tf_op jit(solution)/shard_map/ppermute | solution.py:11
  45.8 8.9 %copy-start.17 = (f32[768]{0:T(1024)S(1)}, f32[768]{0:T(1024)}, u32[]{:S(2)}) copy-start(f32[768]{0:T(1024)} %copy-done.16) | copy-start | bytes 9220
  45.8 9.1 %copy-start.15 = (f32[768]{0:T(1024)S(1)}, f32[768]{0:T(1024)}, u32[]{:S(2)}) copy-start(f32[768]{0:T(1024)} %copy-done.14) | copy-start | bytes 9220
  54.8 0.7 %copy-start.13 = (f32[768]{0:T(1024)S(1)}, f32[768]{0:T(1024)}, u32[]{:S(2)}) copy-start(f32[768]{0:T(1024)} %copy-done.12) | copy-start | bytes 9220
  55.0 0.7 %copy-start.11 = (f32[768]{0:T(1024)S(1)}, f32[768]{0:T(1024)}, u32[]{:S(2)}) copy-start(f32[768]{0:T(1024)} %copy-done.10) | copy-start | bytes 9220
  55.1 1.0 %copy-start.5 = (f32[16,8,768]{2,1,0:T(8,128)S(1)}, f32[16,8,768]{2,1,0:T(8,128)}, u32[]{:S(2)}) copy-start(f32[16,8,768]{2,1,0:T(8,128)} %copy-done.4) | copy-start | bytes 1179652
